TPU v7x, 768 devices: a whole 4x8x12 slice. The times are simulated.
768 devices in a mesh: row: 24 (over z, y_hi), col: 32 (over x, y_lo, core).
Axes of the slice: x: 4, y: 8 (y_hi: 2, y_lo: 4; y = y_hi * 4 + y_lo), z: 12, core: 2. Of those that a mesh axis runs over, the one named last changes fastest.
Arguments:
- iterate: bfloat16 [7680, 7680], P('row', 'col'), may hold values from -2 to 2
- pattern: int32 [120, 120], replicated, may hold values 0 or 1
Outputs:
- squared: bfloat16 [7680, 7680], P('row', 'col')
- traces: float32 [2], replicated
All inputs are finite; a program needn't handle non-finite values.
Results may differ from a plain program's by a relative error of at most 0.001.
Values may be sent and summed in bfloat16 or wider, within the bound.
No kernel may reach another device: no remote copies, remote signals or barrier semaphores. Data moves between devices by JAX's collectives and lax.ppermute only.
A program may use at most 64 MiB of HBM per device.

v0:
```python
import jax
import jax.numpy as jnp
from jax import lax
from jax.sharding import Mesh
from jax.sharding import PartitionSpec as P

BS = 64
ROW = ("row_0", "row_1")
COL = ("col_0", "col_1", "col_2")
ROW_COL = ("row_0", "row_1", "col_0", "col_1", "col_2")


def gather_axes(value, axes, dim):
    if not axes:
        return value
    nearer = lax.all_gather(value, axes[-1], axis=dim, tiled=True)
    return gather_axes(nearer, axes[:-1], dim)


def one_axis_at_a_time(value, axes):
    for axis in axes:
        value = lax.psum(value, axis)
    return value


def tile_keep(block_mask, global_rows, global_cols):
    row_blocks = global_rows // BS
    col_blocks = global_cols // BS
    window = jnp.take(jnp.take(block_mask, row_blocks, axis=0), col_blocks, axis=1)
    return window > 0


def on_device(iterate, pattern):
    tile_rows, tile_cols = iterate.shape
    nblocks = pattern.shape[0]
    order_total = nblocks * BS
    row_index = lax.axis_index(ROW)
    col_index = lax.axis_index(COL)
    identity = jnp.eye(nblocks, dtype=jnp.int32)
    block_mask = jnp.maximum(pattern, identity)
    global_rows = row_index * tile_rows + jnp.arange(tile_rows, dtype=jnp.int32)
    global_cols = col_index * tile_cols + jnp.arange(tile_cols, dtype=jnp.int32)
    keep_mask = tile_keep(block_mask, global_rows, global_cols)
    masked = jnp.where(keep_mask, iterate, jnp.zeros((), iterate.dtype))
    right_panel = gather_axes(masked, ROW, 0)
    running = jnp.dot(
        lax.all_gather(masked, COL, axis=1, tiled=True),
        right_panel,
        preferred_element_type=jnp.float32,
    )
    squared = jnp.where(keep_mask, running, jnp.zeros((), jnp.float32)).astype(jnp.bfloat16)
    on_diagonal = global_rows[:, None] == global_cols[None, :]
    trace_first = jnp.sum(
        jnp.where(on_diagonal, masked, jnp.zeros((), masked.dtype)), dtype=jnp.float32
    )
    trace_second = jnp.sum(jnp.where(on_diagonal, running, jnp.zeros((), jnp.float32)))
    summed_first, summed_second = (
        one_axis_at_a_time(trace_first, ROW_COL),
        one_axis_at_a_time(trace_second, ROW_COL),
    )
    traces = jnp.stack([summed_first, summed_second]) / order_total
    return (squared, traces)


def solution(mesh):
    torus = Mesh(
        mesh.devices.reshape(12, 2, 4, 4, 2), ("row_0", "row_1", "col_0", "col_1", "col_2")
    )
    placed = (P(ROW, COL), P())
    return jax.shard_map(
        on_device, mesh=torus, in_specs=placed, out_specs=(P(ROW, COL), P()), check_vma=False
    )
```

profile of v0, /device:TPU:1, one launch (start us, length us, event | category | flops | bytes accessed | tf_op | source)
XLA Modules:
  0.0 231.0 jit_solution(4829239028242747734)
XLA Ops:
  7.2 0.0 copy-start.1
  7.2 0.0 all-gather.6.cloned.1.call-start
  7.3 0.8 convert_maximum_fusion
  8.2 1.1 gather_fusion
  9.3 0.1 broadcast_select_fusion.1
  9.4 0.1 copy.9
  9.5 1.0 gather_fusion.1
  10.5 0.1 copy.10
  10.7 0.0 copy-done.1
  10.7 0.8 broadcast_select_fusion
  11.4 0.0 all-gather.6.cloned.1.call-update
  11.4 0.0 all-gather.4.cloned.1.call-start
  11.5 11.7 %all_gather.10 = bf16[640,240]{1,0:T(8,128)(2,1)} all-gather(bf16[320,240]{1,0:T(8,128)(2,1)} %get-tuple-element.14), channel_id=1, replica_groups=mesh['row_0'=12,'row_1'=2,'col_0'=4,'col_1'=4,'col_2'=2] {'row_1'}, dimensions={0}, use_global_device_ids=true | all-gather | bytes 460800 | tf_op jit(solution)/shard_map/all_gather | solution.py:16
  23.2 0.0 all-gather.4.cloned.1.call-update
  23.3 66.6 %all-gather.6.cloned.1.call-done = bf16[32,240,320]{1,2,0:T(8,128)(2,1)} async-done(((bf16[1,240,320]{1,2,0:T(8,128)(2,1)}), bf16[32,240,320]{1,2,0:T(8,128)(2,1)}) %all-gather.6.cloned.1.call-update) | async-done | bytes 4915216 | tf_op jit(solution)/shard_map/all_gather | solution.py:47
  89.9 7.8 %copy.11 = bf16[32,240,320]{1,0,2:T(8,128)(2,1)} copy(bf16[32,240,320]{1,2,0:T(8,128)(2,1)} %all-gather.6.cloned.1.call-done) | data formatting | bytes 9830400 | tf_op jit(solution)/shard_map/all_gather | solution.py:47
  97.7 11.4 %reshape.159 = bf16[7680,320]{0,1:T(8,128)(2,1)} reshape(bf16[32,240,320]{1,0,2:T(8,128)(2,1)} %copy.11) | data formatting | bytes 9830400
  109.0 43.3 %all-gather.4.cloned.1.call-done = bf16[7680,240]{1,0:T(8,128)(2,1)} async-done(((bf16[640,240]{1,0:T(8,128)(2,1)}), bf16[7680,240]{1,0:T(8,128)(2,1)}) %all-gather.4.cloned.1.call-update) | async-done | bytes 3686416 | tf_op jit(solution)/shard_map/all_gather | solution.py:16
  152.4 0.0 copy-start
  152.4 5.7 %select_convert_fusion = (bf16[320,240]{1,0:T(8,128)(2,1)}, f32[320,240]{1,0:T(8,128)S(1)}) fusion(pred[320,240]{1,0:T(32,128)(4,1)S(1)} %get-tuple-element.15, bf16[7680,320]{0,1:T(8,128)(2,1)} %reshape.159, bf16[7680,240]{1,0:T(8,128)(2,1)} %all-gather.4.cloned.1.call-done), kind=kOutput, calls=%fused_computation.7 | convolution fusion | flops 1179724800 | bytes 9139200 | tf_op jit(solution)/shard_map/dot_general | solution.py:46
  158.1 0.0 copy-done
  158.1 0.8 convert_reduce_fusion
  158.9 17.2 %all-reduce = (f32[]{:T(128)}, f32[]{:T(128)}) all-reduce(f32[]{:T(128)} %get-tuple-element.3, f32[]{:T(128)} %get-tuple-element.2), channel_id=1, replica_groups=mesh['row_0'=12,'row_1'=2,'col_0'=4,'col_1'=4,'col_2'=2] {'row_0'}, use_global_device_ids=true, to_apply=%region_7.8 | all-reduce | flops 2 | bytes 16 | tf_op jit(solution)/shard_map/psum | solution.py:22
  176.1 8.3 %all-reduce.4 = (f32[]{:T(128)}, f32[]{:T(128)}) all-reduce(f32[]{:T(128)} %get-tuple-element.4, f32[]{:T(128)} %get-tuple-element.5), channel_id=1, replica_groups=mesh['row_0'=12,'row_1'=2,'col_0'=4,'col_1'=4,'col_2'=2] {'row_1'}, use_global_device_ids=true, to_apply=%region_8.9 | all-reduce | flops 2 | bytes 16 | tf_op jit(solution)/shard_map/psum | solution.py:22
  184.4 9.0 %all-reduce.2 = (f32[]{:T(128)}, f32[]{:T(128)}) all-reduce(f32[]{:T(128)} %get-tuple-element.12, f32[]{:T(128)} %get-tuple-element.13), channel_id=1, replica_groups=mesh['row_0'=12,'row_1'=2,'col_0'=4,'col_1'=4,'col_2'=2] {'col_0'}, use_global_device_ids=true, to_apply=%region_9.10 | all-reduce | flops 2 | bytes 16 | tf_op jit(solution)/shard_map/psum | solution.py:22
  193.5 10.4 %all-reduce.1 = (f32[]{:T(128)}, f32[]{:T(128)}) all-reduce(f32[]{:T(128)} %get-tuple-element.8, f32[]{:T(128)} %get-tuple-element.9), channel_id=1, replica_groups=mesh['row_0'=12,'row_1'=2,'col_0'=4,'col_1'=4,'col_2'=2] {'col_1'}, use_global_device_ids=true, to_apply=%region_10.11 | all-reduce | flops 2 | bytes 16 | tf_op jit(solution)/shard_map/psum | solution.py:22
  203.8 18.6 %all-reduce.3 = (f32[1]{0:T(128)}, f32[1]{0:T(128)}) all-reduce(f32[1]{0:T(128)} %bitcast.5, f32[1]{0:T(128)} %bitcast.4), channel_id=1, replica_groups=mesh['row_0'=12,'row_1'=2,'col_0'=4,'col_1'=4,'col_2'=2] {'col_2'}, use_global_device_ids=true, to_apply=%region_11.12 | all-reduce | flops 2 | bytes 16 | tf_op jit(solution)/shard_map/psum | solution.py:22
  222.4 1.8 maximum_multiply_fusion
  (8 shorter events, 0.1 us)
Async XLA Ops:
  7.2 3.5 %copy-start.1 = (bf16[320,240]{1,0:T(8,128)(2,1)S(1)}, bf16[320,240]{1,0:T(8,128)(2,1)}, u32[]{:S(2)}) copy-start(bf16[320,240]{1,0:T(8,128)(2,1)} %param.2) | copy-start | bytes 460804
  7.2 82.7 %all-gather.6.cloned.1.call-start = ((), (), s32[]{:S(2)}) async-start(), calls=%async_computation.1 | async-start | bytes 5406720 | tf_op jit(solution)/shard_map/all_gather | solution.py:47
  11.4 140.9 %all-gather.4.cloned.1.call-start = ((), (), s32[]{:S(2)}) async-start(), calls=%async_computation | async-start | bytes 4259840 | tf_op jit(solution)/shard_map/all_gather | solution.py:16
  152.4 5.7 %copy-start = (bf16[320,240]{1,0:T(8,128)(2,1)S(1)}, bf16[320,240]{1,0:T(8,128)(2,1)}, u32[]{:S(2)}) copy-start(bf16[320,240]{1,0:T(8,128)(2,1)} %get-tuple-element.14) | copy-start | bytes 460804
Sparse Core Ops, SparseCore 0:
  11.6 78.2 all-gather.5
  92.2 60.0 all-gather.3
where the time goes:
time: 232 us; the launch traced here: 231 us
  waiting for transfers between devices  110 us (47%)
  blocking collectives  75.3 us (32%)
  local copies, waits for them, and re-layouts  21.5 us (9%)
  between operations  14.2 us (6%)
  matrix products  5.73 us (2%)
  other arithmetic  4.34 us (2%)
    all_gather x1, waiting for transfers between devices, on_device(): lax.all_gather(masked, COL, axis=1, tiled=True)  66.6 us
    psum x5, blocking collectives, one_axis_at_a_time(): value = lax.psum(value, axis)  63.5 us
    all_gather x1, waiting for transfers between devices, gather_axes(): nearer = lax.all_gather(value, axes[-1], axis=dim, tiled=True)  43.3 us
    all_gather x1, blocking collectives, gather_axes(): nearer = lax.all_gather(value, axes[-1], axis=dim, tiled=True)  11.7 us
    unnamed x5, local copies, waits for them, and re-layouts  11.4 us
    all_gather x1, local copies, waits for them, and re-layouts, on_device(): lax.all_gather(masked, COL, axis=1, tiled=True)  7.8 us
    dot_general x1, matrix products, on_device(): jnp.dot(lax.all_gather(masked, COL, axis=1, tiled=True), right_panel, pre...  5.73 us
  transfers between devices with their start and end apart: 2, of which 2 were waited for; matrix products, arithmetic and copies ran while one was open for 8% of the time, Pallas kernels for 0%

commit v1 on v0

v1 whole, which is shorter than its diff:
```python
import functools

import jax
import jax.numpy as jnp
from jax import lax
from jax.experimental import pallas as pl
from jax.experimental.pallas import tpu as pltpu
from jax.sharding import Mesh
from jax.sharding import PartitionSpec as P

BS = 64
ROW = ("row_0", "row_1")
COL = ("col_0", "col_1", "col_2")
ROW_COL = ("row_0", "row_1", "col_0", "col_1", "col_2")


def tile_keep(block_mask, global_rows, global_cols):
    row_blocks = global_rows // BS
    col_blocks = global_cols // BS
    window = jnp.take(jnp.take(block_mask, row_blocks, axis=0), col_blocks, axis=1)
    return window > 0


def panel_kernel(left_ref, right_ref, out_ref):
    pieces, _, depth = left_ref.shape

    def body(piece, total):
        rows = pl.ds(pl.multiple_of(piece * depth, depth), depth)
        return total + jnp.dot(
            left_ref[piece], right_ref[rows, :], preferred_element_type=jnp.float32
        )

    out_ref[...] = lax.fori_loop(
        0, pieces, body, jnp.zeros(out_ref.shape, jnp.float32)
    )


def panel_product(left, right):
    pieces, tile_rows, depth = left.shape
    tile_cols = right.shape[1]
    return pl.pallas_call(
        panel_kernel,
        out_shape=jax.ShapeDtypeStruct((tile_rows, tile_cols), jnp.float32),
        in_specs=[pl.BlockSpec(memory_space=pltpu.VMEM)] * 2,
        out_specs=pl.BlockSpec(memory_space=pltpu.VMEM),
        cost_estimate=pl.CostEstimate(
            flops=2 * pieces * tile_rows * depth * tile_cols,
            bytes_accessed=2 * (left.size + right.size) + 4 * tile_rows * tile_cols,
            transcendentals=0,
        ),
    )(left, right)


def on_device(iterate, pattern):
    tile_rows, tile_cols = iterate.shape
    nblocks = pattern.shape[0]
    order_total = nblocks * BS
    row_index = lax.axis_index(ROW)
    col_index = lax.axis_index(COL)
    identity = jnp.eye(nblocks, dtype=jnp.int32)
    block_mask = jnp.maximum(pattern, identity)
    global_rows = row_index * tile_rows + jnp.arange(tile_rows, dtype=jnp.int32)
    global_cols = col_index * tile_cols + jnp.arange(tile_cols, dtype=jnp.int32)
    keep_mask = tile_keep(block_mask, global_rows, global_cols)
    masked = jnp.where(keep_mask, iterate, jnp.zeros((), iterate.dtype))
    on_diagonal = global_rows[:, None] == global_cols[None, :]
    trace_first = jnp.sum(
        jnp.where(on_diagonal, masked, jnp.zeros((), masked.dtype)), dtype=jnp.float32
    )
    left_panel = lax.all_gather(masked, COL, axis=0, tiled=False)
    right_panel = lax.all_gather(masked, ROW, axis=0, tiled=True)
    running = panel_product(left_panel, right_panel)
    squared = jnp.where(keep_mask, running, jnp.zeros((), jnp.float32)).astype(jnp.bfloat16)
    trace_second = jnp.sum(jnp.where(on_diagonal, running, jnp.zeros((), jnp.float32)))
    summed = lax.psum(jnp.stack([trace_first, trace_second]), ROW_COL)
    traces = summed / order_total
    return (squared, traces)


def solution(mesh):
    torus = Mesh(
        mesh.devices.reshape(12, 2, 4, 4, 2), ("row_0", "row_1", "col_0", "col_1", "col_2")
    )
    placed = (P(ROW, COL), P())
    return jax.shard_map(
        on_device, mesh=torus, in_specs=placed, out_specs=(P(ROW, COL), P()), check_vma=False
    )
```

time: 232 us -> 383 us (1.65)
  waiting for transfers between devices: 110 us -> 237 us
  blocking collectives: 75.3 us -> 111 us
  local copies, waits for them, and re-layouts: 21.5 us -> 2.32 us
  Pallas kernels: 0 us -> 11.5 us
  matrix products: 5.73 us -> 0 us
    all_gather x2, waiting for transfers between devices: 110 us -> 237 us  [the longest x1 159 us: on_device(): right_panel = lax.all_gather(masked, ROW, axis=0, tiled=True)]
    psum x5 -> x1, blocking collectives: 63.5 us -> 111 us  [on_device(): summed = lax.psum(jnp.stack([trace_first, trace_second]), ROW_COL)]
    all_gather x1 -> x0, blocking collectives: 11.7 us -> none  [gather_axes(): nearer = lax.all_gather(value, axes[-1], axis=dim, tiled=True)]
    pallas_call x0 -> x1, Pallas kernels: none -> 11.5 us  [panel_product(): pl.pallas_call(panel_kernel, out_shape=jax.ShapeDtypeStruct((tile_rows, t...]
    unnamed x5 -> x4, local copies, waits for them, and re-layouts: 11.4 us -> 0.01 us
    all_gather x1 -> x0, local copies, waits for them, and re-layouts: 7.8 us -> none  [on_device(): lax.all_gather(masked, COL, axis=1, tiled=True)]
    dot_general x1 -> x0, matrix products: 5.73 us -> none  [on_device(): jnp.dot(lax.all_gather(masked, COL, axis=1, tiled=True), right_panel, pre...]
  transfers between devices with their start and end apart: 2 -> 2, of which waited for: 2 -> 2; matrix products, arithmetic and copies ran while one was open for 8% -> 0% of each run, Pallas kernels for 0% -> 0%
where the time goes in v1:
time: 383 us
  waiting for transfers between devices  237 us (62%)
  blocking collectives  111 us (29%)
  between operations  14.2 us (4%)
  Pallas kernels  11.5 us (3%)
  other arithmetic  7.11 us (2%)
    all_gather x1, waiting for transfers between devices, on_device(): right_panel = lax.all_gather(masked, ROW, axis=0, tiled=True)  159 us
    psum x1, blocking collectives, on_device(): summed = lax.psum(jnp.stack([trace_first, trace_second]), ROW_COL)  111 us
    all_gather x1, waiting for transfers between devices, on_device(): left_panel = lax.all_gather(masked, COL, axis=0, tiled=False)  77.5 us
    pallas_call x1, Pallas kernels, panel_product(): pl.pallas_call(panel_kernel, out_shape=jax.ShapeDtypeStruct((tile_rows, t...  11.5 us
  transfers between devices with their start and end apart: 2, of which 2 were waited for; matrix products, arithmetic and copies ran while one was open for 0% of the time, Pallas kernels for 0%

profile of v1, /device:TPU:1, one launch (start us, length us, event | category | flops | bytes accessed | tf_op | source)
XLA Modules:
  0.0 383.0 jit_solution(3849744508465353829)
XLA Ops:
  7.2 0.0 copy-start.1
  7.2 0.0 all-gather.4.cloned.1.call-start
  7.3 0.8 convert_maximum_fusion
  8.2 1.1 gather_fusion
  9.3 0.1 broadcast_select_fusion.1
  9.4 0.1 copy.6
  9.5 1.0 gather_fusion.1
  10.5 0.1 copy.7
  10.7 0.0 copy-done.1
  10.7 0.8 broadcast_select_fusion
  11.4 0.0 copy-start
  11.4 0.0 all-gather.4.cloned.1.call-update
  11.4 0.0 all-gather.6.cloned.1.call-start
  11.5 0.7 all-gather.6.cloned.1.call-update
  12.2 159.0 %all-gather.4.cloned.1.call-done.right_ref = bf16[7680,240]{1,0:T(8,128)(2,1)} async-done(((bf16[320,240]{1,0:T(8,128)(2,1)}), bf16[7680,240]{1,0:T(8,128)(2,1)}) %all-gather.4.cloned.1.call-update) | async-done | bytes 3686416 | tf_op jit(solution)/shard_map/all_gather | solution.py:71
  171.2 77.5 %all-gather.6.cloned.1.call-done = bf16[10240,240]{1,0:T(8,128)(2,1)} async-done(((bf16[320,240]{1,0:T(8,128)(2,1)}), bf16[10240,240]{1,0:T(8,128)(2,1)}) %all-gather.6.cloned.1.call-update) | async-done | bytes 4915216 | tf_op jit(solution)/shard_map/all_gather | solution.py:70
  248.7 11.5 %shard_map.41 = f32[320,240]{1,0:T(8,128)} custom-call(bf16[32,320,240]{2,1,0:T(8,128)(2,1)} %bitcast.7, bf16[7680,240]{1,0:T(8,128)(2,1)} %all-gather.4.cloned.1.call-done.right_ref), custom_call_target="tpu_custom_call" | custom-call | flops 1179648000 | bytes 8908800 | tf_op jit(solution)/shard_map/pallas_call | solution.py:41
  260.2 0.0 copy-done
  260.2 1.7 convert_reduce_fusion
  261.9 1.4 pad_maximum_fusion
  263.3 1.7 select_convert_fusion
  265.0 110.7 %psum.7 = f32[2]{0:T(128)S(1)} all-reduce(f32[2]{0:T(128)S(1)} %pad_maximum_fusion), channel_id=1, replica_groups=mesh['row_0'=12,'row_1'=2,'col_0'=4,'col_1'=4,'col_2'=2] {'row_0','row_1..., use_global_device_ids=true, to_apply=%region_2.3 | all-reduce | flops 2 | bytes 16 | tf_op jit(solution)/shard_map/psum | solution.py:75
  375.7 0.5 broadcast_multiply_fusion
  (8 shorter events, 0.1 us)
Async XLA Ops:
  7.2 3.5 copy-start.1
  7.2 164.0 %all-gather.4.cloned.1.call-start = ((), (), s32[]{:S(2)}) async-start(), calls=%async_computation | async-start | bytes 4096000 | tf_op jit(solution)/shard_map/all_gather | solution.py:71
  11.4 248.8 %copy-start = (bf16[320,240]{1,0:T(8,128)(2,1)S(1)}, bf16[320,240]{1,0:T(8,128)(2,1)}, u32[]{:S(2)}) copy-start(bf16[320,240]{1,0:T(8,128)(2,1)} %get-tuple-element.4) | copy-start | bytes 460804
  11.4 237.3 %all-gather.6.cloned.1.call-start = ((), (), s32[]{:S(2)}) async-start(), calls=%async_computation.1 | async-start | bytes 5406720 | tf_op jit(solution)/shard_map/all_gather | solution.py:70
Sparse Core Ops, SparseCore 0:
  12.2 158.9 all-gather.3
  174.2 74.4 all-gather.5

commit v2 on v1

--- a/solution.py
+++ b/solution.py
@@ -23,16 +23,13 @@
 
 def panel_kernel(left_ref, right_ref, out_ref):
     pieces, _, depth = left_ref.shape
-
-    def body(piece, total):
-        rows = pl.ds(pl.multiple_of(piece * depth, depth), depth)
-        return total + jnp.dot(
-            left_ref[piece], right_ref[rows, :], preferred_element_type=jnp.float32
+    out_ref[...] = jnp.dot(left_ref[0], right_ref[0:depth, :], preferred_element_type=jnp.float32)
+    for piece in range(1, pieces):
+        out_ref[...] += jnp.dot(
+            left_ref[piece],
+            right_ref[piece * depth:(piece + 1) * depth, :],
+            preferred_element_type=jnp.float32,
         )
-
-    out_ref[...] = lax.fori_loop(
-        0, pieces, body, jnp.zeros(out_ref.shape, jnp.float32)
-    )
 
 
 def panel_product(left, right):
@@ -49,6 +46,31 @@
             transcendentals=0,
         ),
     )(left, right)
+
+
+def column_slab(masked):
+    depth = lax.psum(1, "row_0")
+    half = lax.axis_index("row_1")
+    other = lax.ppermute(masked, "row_1", [(0, 1), (1, 0)])
+    pair = jnp.where(
+        half == 0,
+        jnp.concatenate([masked, other]),
+        jnp.concatenate([other, masked]),
+    )
+    here = lax.axis_index("row_0")
+    slab = jnp.zeros((depth,) + pair.shape, pair.dtype)
+    slab = lax.dynamic_update_index_in_dim(slab, pair, here, 0)
+    forward = [(i, (i + 1) % depth) for i in range(depth)]
+    backward = [(i, (i - 1) % depth) for i in range(depth)]
+    ahead = pair
+    behind = pair
+    for step in range(1, depth // 2 + 1):
+        ahead = lax.ppermute(ahead, "row_0", forward)
+        slab = lax.dynamic_update_index_in_dim(slab, ahead, (here - step) % depth, 0)
+        if step < depth - depth // 2:
+            behind = lax.ppermute(behind, "row_0", backward)
+            slab = lax.dynamic_update_index_in_dim(slab, behind, (here + step) % depth, 0)
+    return slab.reshape(depth * pair.shape[0], pair.shape[1])
 
 
 def on_device(iterate, pattern):
@@ -68,11 +90,13 @@
         jnp.where(on_diagonal, masked, jnp.zeros((), masked.dtype)), dtype=jnp.float32
     )
     left_panel = lax.all_gather(masked, COL, axis=0, tiled=False)
-    right_panel = lax.all_gather(masked, ROW, axis=0, tiled=True)
+    right_panel = column_slab(masked)
     running = panel_product(left_panel, right_panel)
     squared = jnp.where(keep_mask, running, jnp.zeros((), jnp.float32)).astype(jnp.bfloat16)
     trace_second = jnp.sum(jnp.where(on_diagonal, running, jnp.zeros((), jnp.float32)))
-    summed = lax.psum(jnp.stack([trace_first, trace_second]), ROW_COL)
+    summed = jnp.stack([trace_first, trace_second])
+    for axis in ROW_COL:
+        summed = lax.psum(summed, axis)
     traces = summed / order_total
     return (squared, traces)
 

time: 383 us -> 178 us (0.46)
  the two profiles are of different devices: /device:TPU:1 before, /device:TPU:40 now
where the time goes in v2:
time: 178 us; the launch traced here: 177 us
  blocking collectives  56.4 us (32%)
  starting transfers between devices  49.7 us (28%)
  waiting for transfers between devices  27.8 us (16%)
  between operations  14.5 us (8%)
  local copies, waits for them, and re-layouts  13 us (7%)
  other arithmetic  9.03 us (5%)
  Pallas kernels  6.45 us (4%)
    psum x5, blocking collectives, on_device(): summed = lax.psum(summed, axis)  56.4 us
    ppermute x5, starting transfers between devices, column_slab(): behind = lax.ppermute(behind, 'row_0', backward)  32.8 us
    ppermute x6, waiting for transfers between devices, column_slab(): ahead = lax.ppermute(ahead, 'row_0', forward)  16 us
    ppermute x6, starting transfers between devices, column_slab(): ahead = lax.ppermute(ahead, 'row_0', forward)  13.8 us
    ppermute x1, waiting for transfers between devices, column_slab(): other = lax.ppermute(masked, 'row_1', [(0, 1), (1, 0)])  11.7 us
    pallas_call x1, Pallas kernels, panel_product(): pl.pallas_call(panel_kernel, out_shape=jax.ShapeDtypeStruct((tile_rows, t...  6.45 us
    dynamic_update_slice x6, local copies, waits for them, and re-layouts, column_slab(): lax.dynamic_update_index_in_dim(slab, ahead, (here - step) % depth, 0)  4.62 us
    dynamic_update_slice x5, local copies, waits for them, and re-layouts, column_slab(): lax.dynamic_update_index_in_dim(slab, behind, (here + step) % depth, 0)  3.74 us
  transfers between devices with their start and end apart: 13, of which 7 were waited for; matrix products, arithmetic and copies ran while one was open for 7% of the time, Pallas kernels for 0%

profile of v2, /device:TPU:40, one launch (start us, length us, event | category | flops | bytes accessed | tf_op | source)
XLA Modules:
  0.0 176.8 jit_solution(5764671260527354964)
XLA Ops:
  7.3 0.8 convert_maximum_fusion
  8.2 1.1 gather_fusion
  9.5 1.0 gather_fusion.1
  10.5 0.1 copy.7
  10.7 0.8 broadcast_select_fusion
  11.4 3.0 %collective-permute-start = (bf16[320,240]{1,0:T(8,128)(2,1)}, bf16[320,240]{1,0:T(8,128)(2,1)S(1)}, u32[]{:S(2)}, u32[]{:S(2)}) collective-permute-start(bf16[320,240]{1,0:T(8,128)(2,1)} %get-tuple-element.4), channel_id=1, source_target_pairs={{0,32},{32,0},{1,33},{33,1},{2,34},{34,2},{3,35},{35,3},{4,36},{36... | collective-permute-start | bytes 460808 | tf_op jit(solution)/shard_map/ppermute | solution.py:54
  14.7 11.7 %collective-permute-done = bf16[320,240]{1,0:T(8,128)(2,1)S(1)} collective-permute-done((bf16[320,240]{1,0:T(8,128)(2,1)}, bf16[320,240]{1,0:T(8,128)(2,1)S(1)}, u32[]{:S(2)}, u32[]{:S(2)}) %collective-permute-start) | collective-permute-done | bytes 153632 | tf_op jit(solution)/shard_map/ppermute | solution.py:54
  26.4 1.1 maximum_select_fusion.1
  27.5 4.3 %collective-permute-start.1 = (bf16[640,240]{1,0:T(8,128)(2,1)S(1)}, bf16[640,240]{1,0:T(8,128)(2,1)S(1)}, u32[]{:S(2)}, u32[]{:S(2)}) collective-permute-start(bf16[640,240]{1,0:T(8,128)(2,1)S(1)} %maximum_select_fusion.1), channel_id=1, source_target_pairs={{0,64},{64,128},{128,192},{192,256},{256,320},{320,384},{384,448},... | collective-permute-start | bytes 921608 | tf_op jit(solution)/shard_map/ppermute | solution.py:68
  31.8 12.3 %collective-permute-start.2 = (bf16[640,240]{1,0:T(8,128)(2,1)S(1)}, bf16[640,240]{1,0:T(8,128)(2,1)S(1)}, u32[]{:S(2)}, u32[]{:S(2)}) collective-permute-start(bf16[640,240]{1,0:T(8,128)(2,1)S(1)} %maximum_select_fusion.1), channel_id=1, source_target_pairs={{0,704},{64,0},{128,64},{192,128},{256,192},{320,256},{384,320},{4... | collective-permute-start | bytes 921608 | tf_op jit(solution)/shard_map/ppermute | solution.py:71
  44.1 2.3 %broadcast_in_dim.75 = bf16[12,640,240]{2,1,0:T(8,128)(2,1)} broadcast(bf16[]{:T(256)} %constant.152.clone.1), dimensions={} | broadcast | bytes 3686402 | tf_op jit(solution)/shard_map/broadcast_in_dim | solution.py:61
  46.4 0.8 fusion.1
  47.2 1.9 %collective-permute-done.1 = bf16[640,240]{1,0:T(8,128)(2,1)S(1)} collective-permute-done((bf16[640,240]{1,0:T(8,128)(2,1)S(1)}, bf16[640,240]{1,0:T(8,128)(2,1)S(1)}, u32[]{:S(2)}, u32[]{:S(2)}) %collective-permute-start.1) | collective-permute-done | bytes 307232 | tf_op jit(solution)/shard_map/ppermute | solution.py:68
  49.1 1.9 %collective-permute-start.3 = (bf16[640,240]{1,0:T(8,128)(2,1)S(1)}, bf16[640,240]{1,0:T(8,128)(2,1)S(1)}, u32[]{:S(2)}, u32[]{:S(2)}) collective-permute-start(bf16[640,240]{1,0:T(8,128)(2,1)S(1)} %collective-permute-done.1), channel_id=1, source_target_pairs={{0,64},{64,128},{128,192},{192,256},{256,320},{320,384},{384,448},... | collective-permute-start | bytes 921608 | tf_op jit(solution)/shard_map/ppermute | solution.py:68
  51.0 5.1 %collective-permute-start.4 = (bf16[640,240]{1,0:T(8,128)(2,1)S(1)}, bf16[640,240]{1,0:T(8,128)(2,1)S(1)}, u32[]{:S(2)}, u32[]{:S(2)}) collective-permute-start(bf16[640,240]{1,0:T(8,128)(2,1)S(1)} %collective-permute-done.2), channel_id=1, source_target_pairs={{0,704},{64,0},{128,64},{192,128},{256,192},{320,256},{384,320},{4... | collective-permute-start | bytes 921608 | tf_op jit(solution)/shard_map/ppermute | solution.py:71
  56.2 0.8 bitcast_dynamic-update-slice_fusion.10
  57.0 0.7 bitcast_dynamic-update-slice_fusion.9
  57.7 2.6 %collective-permute-done.3 = bf16[640,240]{1,0:T(8,128)(2,1)S(1)} collective-permute-done((bf16[640,240]{1,0:T(8,128)(2,1)S(1)}, bf16[640,240]{1,0:T(8,128)(2,1)S(1)}, u32[]{:S(2)}, u32[]{:S(2)}) %collective-permute-start.3) | collective-permute-done | bytes 307232 | tf_op jit(solution)/shard_map/ppermute | solution.py:68
  60.3 1.9 %collective-permute-start.5 = (bf16[640,240]{1,0:T(8,128)(2,1)S(1)}, bf16[640,240]{1,0:T(8,128)(2,1)S(1)}, u32[]{:S(2)}, u32[]{:S(2)}) collective-permute-start(bf16[640,240]{1,0:T(8,128)(2,1)S(1)} %collective-permute-done.3), channel_id=1, source_target_pairs={{0,64},{64,128},{128,192},{192,256},{256,320},{320,384},{384,448},... | collective-permute-start | bytes 921608 | tf_op jit(solution)/shard_map/ppermute | solution.py:68
  62.2 5.1 %collective-permute-start.6 = (bf16[640,240]{1,0:T(8,128)(2,1)S(1)}, bf16[640,240]{1,0:T(8,128)(2,1)S(1)}, u32[]{:S(2)}, u32[]{:S(2)}) collective-permute-start(bf16[640,240]{1,0:T(8,128)(2,1)S(1)} %collective-permute-done.4), channel_id=1, source_target_pairs={{0,704},{64,0},{128,64},{192,128},{256,192},{320,256},{384,320},{4... | collective-permute-start | bytes 921608 | tf_op jit(solution)/shard_map/ppermute | solution.py:71
  67.4 0.8 bitcast_dynamic-update-slice_fusion.8
  68.2 0.8 bitcast_dynamic-update-slice_fusion.7
  68.9 1.6 collective-permute-done.5
  70.6 1.9 %collective-permute-start.7 = (bf16[640,240]{1,0:T(8,128)(2,1)S(1)}, bf16[640,240]{1,0:T(8,128)(2,1)S(1)}, u32[]{:S(2)}, u32[]{:S(2)}) collective-permute-start(bf16[640,240]{1,0:T(8,128)(2,1)S(1)} %collective-permute-done.5), channel_id=1, source_target_pairs={{0,64},{64,128},{128,192},{192,256},{256,320},{320,384},{384,448},... | collective-permute-start | bytes 921608 | tf_op jit(solution)/shard_map/ppermute | solution.py:68
  72.5 5.1 %collective-permute-start.8 = (bf16[640,240]{1,0:T(8,128)(2,1)S(1)}, bf16[640,240]{1,0:T(8,128)(2,1)S(1)}, u32[]{:S(2)}, u32[]{:S(2)}) collective-permute-start(bf16[640,240]{1,0:T(8,128)(2,1)S(1)} %collective-permute-done.6), channel_id=1, source_target_pairs={{0,704},{64,0},{128,64},{192,128},{256,192},{320,256},{384,320},{4... | collective-permute-start | bytes 921608 | tf_op jit(solution)/shard_map/ppermute | solution.py:71
  77.6 0.8 bitcast_dynamic-update-slice_fusion.6
  78.4 0.7 bitcast_dynamic-update-slice_fusion.5
  79.2 1.6 collective-permute-done.7
  80.7 1.9 %collective-permute-start.9 = (bf16[640,240]{1,0:T(8,128)(2,1)S(1)}, bf16[640,240]{1,0:T(8,128)(2,1)S(1)}, u32[]{:S(2)}, u32[]{:S(2)}) collective-permute-start(bf16[640,240]{1,0:T(8,128)(2,1)S(1)} %collective-permute-done.7), channel_id=1, source_target_pairs={{0,64},{64,128},{128,192},{192,256},{256,320},{320,384},{384,448},... | collective-permute-start | bytes 921608 | tf_op jit(solution)/shard_map/ppermute | solution.py:68
  82.6 5.1 %collective-permute-start.10 = (bf16[640,240]{1,0:T(8,128)(2,1)S(1)}, bf16[640,240]{1,0:T(8,128)(2,1)S(1)}, u32[]{:S(2)}, u32[]{:S(2)}) collective-permute-start(bf16[640,240]{1,0:T(8,128)(2,1)S(1)} %collective-permute-done.8), channel_id=1, source_target_pairs={{0,704},{64,0},{128,64},{192,128},{256,192},{320,256},{384,320},{4... | collective-permute-start | bytes 921608 | tf_op jit(solution)/shard_map/ppermute | solution.py:71
  87.8 0.8 bitcast_dynamic-update-slice_fusion.4
  88.5 0.8 bitcast_dynamic-update-slice_fusion.3
  89.3 1.6 collective-permute-done.9
  90.9 1.9 %collective-permute-start.11 = (bf16[640,240]{1,0:T(8,128)(2,1)S(1)}, bf16[640,240]{1,0:T(8,128)(2,1)S(1)}, u32[]{:S(2)}, u32[]{:S(2)}) collective-permute-start(bf16[640,240]{1,0:T(8,128)(2,1)S(1)} %collective-permute-done.9), channel_id=1, source_target_pairs={{0,64},{64,128},{128,192},{192,256},{256,320},{320,384},{384,448},... | collective-permute-start | bytes 921608 | tf_op jit(solution)/shard_map/ppermute | solution.py:68
  92.8 0.7 bitcast_dynamic-update-slice_fusion.2
  93.6 0.7 bitcast_dynamic-update-slice_fusion.1
  94.3 6.8 %collective-permute-done.11 = bf16[640,240]{1,0:T(8,128)(2,1)S(1)} collective-permute-done((bf16[640,240]{1,0:T(8,128)(2,1)S(1)}, bf16[640,240]{1,0:T(8,128)(2,1)S(1)}, u32[]{:S(2)}, u32[]{:S(2)}) %collective-permute-start.11) | collective-permute-done | bytes 307232 | tf_op jit(solution)/shard_map/ppermute | solution.py:68
  101.1 0.8 bitcast_dynamic-update-slice_fusion
  101.8 6.4 %shard_map.41 = f32[320,240]{1,0:T(8,128)} custom-call(bf16[32,320,240]{2,1,0:T(8,128)(2,1)} %bitcast.32, bf16[7680,240]{1,0:T(8,128)(2,1)} %bitcast.16.right_ref), custom_call_target="tpu_custom_call" | custom-call | flops 1179648000 | bytes 8908800 | tf_op jit(solution)/shard_map/pallas_call | solution.py:38
  108.3 1.7 convert_reduce_fusion
  110.0 1.4 pad_maximum_fusion
  111.4 20.6 %psum.35 = f32[2]{0:T(128)S(1)} all-reduce(f32[2]{0:T(128)S(1)} %pad_maximum_fusion), channel_id=1, replica_groups=mesh['row_0'=12,'row_1'=2,'col_0'=4,'col_1'=4,'col_2'=2] {'row_0'}, use_global_device_ids=true, to_apply=%region_2.3 | all-reduce | flops 2 | bytes 16 | tf_op jit(solution)/shard_map/psum | solution.py:99
  131.9 8.8 %psum.36 = f32[2]{0:T(128)S(1)} all-reduce(f32[2]{0:T(128)S(1)} %psum.35), channel_id=1, replica_groups=mesh['row_0'=12,'row_1'=2,'col_0'=4,'col_1'=4,'col_2'=2] {'row_1'}, use_global_device_ids=true, to_apply=%region_3.4 | all-reduce | flops 2 | bytes 16 | tf_op jit(solution)/shard_map/psum | solution.py:99
  140.8 10.6 %psum.37 = f32[2]{0:T(128)S(1)} all-reduce(f32[2]{0:T(128)S(1)} %psum.36), channel_id=1, replica_groups=mesh['row_0'=12,'row_1'=2,'col_0'=4,'col_1'=4,'col_2'=2] {'col_0'}, use_global_device_ids=true, to_apply=%region_4.5 | all-reduce | flops 2 | bytes 16 | tf_op jit(solution)/shard_map/psum | solution.py:99
  151.4 13.9 %psum.38 = f32[2]{0:T(128)S(1)} all-reduce(f32[2]{0:T(128)S(1)} %psum.37), channel_id=1, replica_groups=mesh['row_0'=12,'row_1'=2,'col_0'=4,'col_1'=4,'col_2'=2] {'col_1'}, use_global_device_ids=true, to_apply=%region_5.6 | all-reduce | flops 2 | bytes 16 | tf_op jit(solution)/shard_map/psum | solution.py:99
  165.3 2.5 %psum.39 = f32[2]{0:T(128)S(1)} all-reduce(f32[2]{0:T(128)S(1)} %psum.38), channel_id=1, replica_groups=mesh['row_0'=12,'row_1'=2,'col_0'=4,'col_1'=4,'col_2'=2] {'col_2'}, use_global_device_ids=true, to_apply=%region_6.7 | all-reduce | flops 2 | bytes 16 | tf_op jit(solution)/shard_map/psum | solution.py:99
  167.8 0.5 broadcast_multiply_fusion
  168.3 1.7 select_convert_fusion
  (22 shorter events, 0.4 us)
Async XLA Ops:
  7.2 3.5 %copy-start.1 = (bf16[320,240]{1,0:T(8,128)(2,1)S(1)}, bf16[320,240]{1,0:T(8,128)(2,1)}, u32[]{:S(2)}) copy-start(bf16[320,240]{1,0:T(8,128)(2,1)} %param.2) | copy-start | bytes 460804
  7.2 94.6 %all-gather.3.cloned.1.call-start = ((), (), s32[]{:S(2)}) async-start(), calls=%async_computation | async-start | bytes 5406720 | tf_op jit(solution)/shard_map/all_gather | solution.py:92
  11.4 35.0 %copy-start = (bf16[320,240]{1,0:T(8,128)(2,1)S(1)}, bf16[320,240]{1,0:T(8,128)(2,1)}, u32[]{:S(2)}) copy-start(bf16[320,240]{1,0:T(8,128)(2,1)} %get-tuple-element.4) | copy-start | bytes 460804
  11.4 15.0 %collective-permute-start = (bf16[320,240]{1,0:T(8,128)(2,1)}, bf16[320,240]{1,0:T(8,128)(2,1)S(1)}, u32[]{:S(2)}, u32[]{:S(2)}) collective-permute-start(bf16[320,240]{1,0:T(8,128)(2,1)} %get-tuple-element.4), channel_id=1, source_target_pairs={{0,32},{32,0},{1,33},{33,1},{2,34},{34,2},{3,35},{35,3},{4,36},{36... | collective-permute-start | bytes 460808 | tf_op jit(solution)/shard_map/ppermute | solution.py:54
  27.5 21.6 %collective-permute-start.1 = (bf16[640,240]{1,0:T(8,128)(2,1)S(1)}, bf16[640,240]{1,0:T(8,128)(2,1)S(1)}, u32[]{:S(2)}, u32[]{:S(2)}) collective-permute-start(bf16[640,240]{1,0:T(8,128)(2,1)S(1)} %maximum_select_fusion.1), channel_id=1, source_target_pairs={{0,64},{64,128},{128,192},{192,256},{256,320},{320,384},{384,448},... | collective-permute-start | bytes 921608 | tf_op jit(solution)/shard_map/ppermute | solution.py:68
  31.8 19.2 %collective-permute-start.2 = (bf16[640,240]{1,0:T(8,128)(2,1)S(1)}, bf16[640,240]{1,0:T(8,128)(2,1)S(1)}, u32[]{:S(2)}, u32[]{:S(2)}) collective-permute-start(bf16[640,240]{1,0:T(8,128)(2,1)S(1)} %maximum_select_fusion.1), channel_id=1, source_target_pairs={{0,704},{64,0},{128,64},{192,128},{256,192},{320,256},{384,320},{4... | collective-permute-start | bytes 921608 | tf_op jit(solution)/shard_map/ppermute | solution.py:71
  49.1 11.2 %collective-permute-start.3 = (bf16[640,240]{1,0:T(8,128)(2,1)S(1)}, bf16[640,240]{1,0:T(8,128)(2,1)S(1)}, u32[]{:S(2)}, u32[]{:S(2)}) collective-permute-start(bf16[640,240]{1,0:T(8,128)(2,1)S(1)} %collective-permute-done.1), channel_id=1, source_target_pairs={{0,64},{64,128},{128,192},{192,256},{256,320},{320,384},{384,448},... | collective-permute-start | bytes 921608 | tf_op jit(solution)/shard_map/ppermute | solution.py:68
  51.0 11.2 %collective-permute-start.4 = (bf16[640,240]{1,0:T(8,128)(2,1)S(1)}, bf16[640,240]{1,0:T(8,128)(2,1)S(1)}, u32[]{:S(2)}, u32[]{:S(2)}) collective-permute-start(bf16[640,240]{1,0:T(8,128)(2,1)S(1)} %collective-permute-done.2), channel_id=1, source_target_pairs={{0,704},{64,0},{128,64},{192,128},{256,192},{320,256},{384,320},{4... | collective-permute-start | bytes 921608 | tf_op jit(solution)/shard_map/ppermute | solution.py:71
  60.3 10.3 %collective-permute-start.5 = (bf16[640,240]{1,0:T(8,128)(2,1)S(1)}, bf16[640,240]{1,0:T(8,128)(2,1)S(1)}, u32[]{:S(2)}, u32[]{:S(2)}) collective-permute-start(bf16[640,240]{1,0:T(8,128)(2,1)S(1)} %collective-permute-done.3), channel_id=1, source_target_pairs={{0,64},{64,128},{128,192},{192,256},{256,320},{320,384},{384,448},... | collective-permute-start | bytes 921608 | tf_op jit(solution)/shard_map/ppermute | solution.py:68
  62.2 10.2 %collective-permute-start.6 = (bf16[640,240]{1,0:T(8,128)(2,1)S(1)}, bf16[640,240]{1,0:T(8,128)(2,1)S(1)}, u32[]{:S(2)}, u32[]{:S(2)}) collective-permute-start(bf16[640,240]{1,0:T(8,128)(2,1)S(1)} %collective-permute-done.4), channel_id=1, source_target_pairs={{0,704},{64,0},{128,64},{192,128},{256,192},{320,256},{384,320},{4... | collective-permute-start | bytes 921608 | tf_op jit(solution)/shard_map/ppermute | solution.py:71
  70.6 10.2 %collective-permute-start.7 = (bf16[640,240]{1,0:T(8,128)(2,1)S(1)}, bf16[640,240]{1,0:T(8,128)(2,1)S(1)}, u32[]{:S(2)}, u32[]{:S(2)}) collective-permute-start(bf16[640,240]{1,0:T(8,128)(2,1)S(1)} %collective-permute-done.5), channel_id=1, source_target_pairs={{0,64},{64,128},{128,192},{192,256},{256,320},{320,384},{384,448},... | collective-permute-start | bytes 921608 | tf_op jit(solution)/shard_map/ppermute | solution.py:68
  72.5 10.2 %collective-permute-start.8 = (bf16[640,240]{1,0:T(8,128)(2,1)S(1)}, bf16[640,240]{1,0:T(8,128)(2,1)S(1)}, u32[]{:S(2)}, u32[]{:S(2)}) collective-permute-start(bf16[640,240]{1,0:T(8,128)(2,1)S(1)} %collective-permute-done.6), channel_id=1, source_target_pairs={{0,704},{64,0},{128,64},{192,128},{256,192},{320,256},{384,320},{4... | collective-permute-start | bytes 921608 | tf_op jit(solution)/shard_map/ppermute | solution.py:71
  80.7 10.2 %collective-permute-start.9 = (bf16[640,240]{1,0:T(8,128)(2,1)S(1)}, bf16[640,240]{1,0:T(8,128)(2,1)S(1)}, u32[]{:S(2)}, u32[]{:S(2)}) collective-permute-start(bf16[640,240]{1,0:T(8,128)(2,1)S(1)} %collective-permute-done.7), channel_id=1, source_target_pairs={{0,64},{64,128},{128,192},{192,256},{256,320},{320,384},{384,448},... | collective-permute-start | bytes 921608 | tf_op jit(solution)/shard_map/ppermute | solution.py:68
  82.6 10.9 %collective-permute-start.10 = (bf16[640,240]{1,0:T(8,128)(2,1)S(1)}, bf16[640,240]{1,0:T(8,128)(2,1)S(1)}, u32[]{:S(2)}, u32[]{:S(2)}) collective-permute-start(bf16[640,240]{1,0:T(8,128)(2,1)S(1)} %collective-permute-done.8), channel_id=1, source_target_pairs={{0,704},{64,0},{128,64},{192,128},{256,192},{320,256},{384,320},{4... | collective-permute-start | bytes 921608 | tf_op jit(solution)/shard_map/ppermute | solution.py:71
  90.9 10.2 %collective-permute-start.11 = (bf16[640,240]{1,0:T(8,128)(2,1)S(1)}, bf16[640,240]{1,0:T(8,128)(2,1)S(1)}, u32[]{:S(2)}, u32[]{:S(2)}) collective-permute-start(bf16[640,240]{1,0:T(8,128)(2,1)S(1)} %collective-permute-done.9), channel_id=1, source_target_pairs={{0,64},{64,128},{128,192},{192,256},{256,320},{320,384},{384,448},... | collective-permute-start | bytes 921608 | tf_op jit(solution)/shard_map/ppermute | solution.py:68
Sparse Core Ops, SparseCore 0:
  11.6 75.2 all-gather.2

commit v3 on v2

v3 whole, which is shorter than its diff:
```python
import jax
import jax.numpy as jnp
from jax import lax
from jax.experimental import pallas as pl
from jax.experimental.pallas import tpu as pltpu
from jax.sharding import Mesh
from jax.sharding import PartitionSpec as P

BS = 64
ROW = ("row_0", "row_1")
COL = ("col_0", "col_1", "col_2")
ROW_COL = ("row_0", "row_1", "col_0", "col_1", "col_2")


def tile_keep(pattern, row_index, col_index, tile_rows, tile_cols):
    row_blocks = tile_rows // BS
    span = (tile_cols + BS - 1) // BS + 1
    first_col = col_index * tile_cols
    first_block = first_col // BS
    padded = jnp.pad(pattern, ((0, 0), (0, span)))
    window = lax.dynamic_slice(padded, (row_index * row_blocks, first_block), (row_blocks, span))
    block_rows = row_index * row_blocks + jnp.arange(row_blocks, dtype=jnp.int32)[:, None]
    block_cols = first_block + jnp.arange(span, dtype=jnp.int32)[None, :]
    window = jnp.maximum(window, (block_rows == block_cols).astype(window.dtype))
    per_row = jnp.repeat(window, BS, axis=0)
    local_block = (first_col + jnp.arange(tile_cols, dtype=jnp.int32)) // BS - first_block
    keep = jnp.zeros((tile_rows, tile_cols), jnp.bool_)
    for block in range(span):
        keep = keep | ((local_block[None, :] == block) & (per_row[:, block:block + 1] > 0))
    return keep


def panel_kernel(shift_ref, left_ref, right_ref, keep_ref, square_ref, trace_ref, total_ref):
    pieces, _, depth = left_ref.shape
    total_ref[...] = jnp.dot(
        left_ref[0], right_ref[0:depth, :], preferred_element_type=jnp.float32
    )
    for piece in range(1, pieces):
        total_ref[...] += jnp.dot(
            left_ref[piece],
            right_ref[piece * depth:(piece + 1) * depth, :],
            preferred_element_type=jnp.float32,
        )
    total = total_ref[...]
    square_ref[...] = jnp.where(keep_ref[...] != 0, total, 0.0).astype(square_ref.dtype)
    rows = lax.broadcasted_iota(jnp.int32, total.shape, 0)
    cols = lax.broadcasted_iota(jnp.int32, total.shape, 1)
    diagonal = jnp.sum(jnp.where(cols - rows == shift_ref[0], total, 0.0))
    trace_ref[...] = jnp.full(trace_ref.shape, diagonal, jnp.float32)


def panel_product(shift, left, right, keep):
    pieces, tile_rows, depth = left.shape
    tile_cols = right.shape[1]
    vmem = pl.BlockSpec(memory_space=pltpu.VMEM)
    return pl.pallas_call(
        panel_kernel,
        out_shape=(
            jax.ShapeDtypeStruct((tile_rows, tile_cols), jnp.bfloat16),
            jax.ShapeDtypeStruct((8, 128), jnp.float32),
        ),
        in_specs=[pl.BlockSpec(memory_space=pltpu.SMEM), vmem, vmem, vmem],
        out_specs=(vmem, vmem),
        scratch_shapes=[pltpu.VMEM((tile_rows, tile_cols), jnp.float32)],
        cost_estimate=pl.CostEstimate(
            flops=2 * pieces * tile_rows * depth * tile_cols,
            bytes_accessed=2 * (left.size + right.size) + 6 * tile_rows * tile_cols,
            transcendentals=0,
        ),
    )(shift, left, right, keep)


def column_slab(masked):
    depth = lax.psum(1, "row_0")
    half = lax.axis_index("row_1")
    other = lax.ppermute(masked, "row_1", [(0, 1), (1, 0)])
    pair = jnp.where(
        half == 0,
        jnp.concatenate([masked, other]),
        jnp.concatenate([other, masked]),
    )
    here = lax.axis_index("row_0")
    slab = jnp.zeros((depth,) + pair.shape, pair.dtype)
    slab = lax.dynamic_update_index_in_dim(slab, pair, here, 0)
    forward = [(i, (i + 1) % depth) for i in range(depth)]
    backward = [(i, (i - 1) % depth) for i in range(depth)]
    ahead = pair
    behind = pair
    for step in range(1, depth // 2 + 1):
        ahead = lax.ppermute(ahead, "row_0", forward)
        slab = lax.dynamic_update_index_in_dim(slab, ahead, (here - step) % depth, 0)
        if step < depth - depth // 2:
            behind = lax.ppermute(behind, "row_0", backward)
            slab = lax.dynamic_update_index_in_dim(slab, behind, (here + step) % depth, 0)
    return slab.reshape(depth * pair.shape[0], pair.shape[1])


def on_device(iterate, pattern):
    tile_rows, tile_cols = iterate.shape
    nblocks = pattern.shape[0]
    order_total = nblocks * BS
    row_index = lax.axis_index(ROW)
    col_index = lax.axis_index(COL)
    keep_mask = tile_keep(pattern, row_index, col_index, tile_rows, tile_cols)
    masked = jnp.where(keep_mask, iterate, jnp.zeros((), iterate.dtype))
    left_panel = lax.all_gather(masked, COL, axis=0, tiled=False)
    right_panel = column_slab(masked)
    shift = row_index * tile_rows - col_index * tile_cols
    global_rows = jnp.arange(tile_rows, dtype=jnp.int32)[:, None]
    global_cols = jnp.arange(tile_cols, dtype=jnp.int32)[None, :]
    on_diagonal = global_cols - global_rows == shift
    trace_first = jnp.sum(
        jnp.where(on_diagonal, masked, jnp.zeros((), masked.dtype)), dtype=jnp.float32
    )
    squared, diagonal = panel_product(
        shift.reshape(1), left_panel, right_panel, keep_mask.astype(jnp.int32)
    )
    summed = jnp.stack([trace_first, diagonal[0, 0]])
    for axis in ROW_COL:
        summed = lax.psum(summed, axis)
    traces = summed / order_total
    return (squared, traces)


def solution(mesh):
    torus = Mesh(
        mesh.devices.reshape(12, 2, 4, 4, 2), ("row_0", "row_1", "col_0", "col_1", "col_2")
    )
    placed = (P(ROW, COL), P())
    return jax.shard_map(
        on_device, mesh=torus, in_specs=placed, out_specs=(P(ROW, COL), P()), check_vma=False
    )
```

time: 178 us -> 176 us (0.989)
    gather x3 -> x0, local copies, waits for them, and re-layouts: 2.19 us -> none  [the longest x2 1.11 us: tile_keep(): jnp.take(jnp.take(block_mask, row_blocks, axis=0), col_blocks, axis=1)]
  transfers between devices with their start and end apart: 13 -> 13, of which waited for: 7 -> 7; matrix products, arithmetic and copies ran while one was open for 7% -> 8% of each run, Pallas kernels for 0% -> 0%
where the time goes in v3:
time: 176 us; the launch traced here: 175 us
  blocking collectives  56.9 us (32%)
  starting transfers between devices  49.7 us (28%)
  waiting for transfers between devices  27.2 us (15%)
  between operations  14.5 us (8%)
  local copies, waits for them, and re-layouts  12.1 us (7%)
  other arithmetic  8.16 us (5%)
  Pallas kernels  6.43 us (4%)
    psum x5, blocking collectives, on_device(): summed = lax.psum(summed, axis)  56.9 us
    ppermute x5, starting transfers between devices, column_slab(): behind = lax.ppermute(behind, 'row_0', backward)  32.8 us
    ppermute x6, waiting for transfers between devices, column_slab(): ahead = lax.ppermute(ahead, 'row_0', forward)  15.4 us
    ppermute x6, starting transfers between devices, column_slab(): ahead = lax.ppermute(ahead, 'row_0', forward)  13.8 us
    ppermute x1, waiting for transfers between devices, column_slab(): other = lax.ppermute(masked, 'row_1', [(0, 1), (1, 0)])  11.7 us
    pallas_call x1, Pallas kernels, panel_product(): pl.pallas_call(panel_kernel, out_shape=(jax.ShapeDtypeStruct((tile_rows,...  6.43 us
    dynamic_update_slice x6, local copies, waits for them, and re-layouts, column_slab(): lax.dynamic_update_index_in_dim(slab, ahead, (here - step) % depth, 0)  4.62 us
    dynamic_update_slice x5, local copies, waits for them, and re-layouts, column_slab(): lax.dynamic_update_index_in_dim(slab, behind, (here + step) % depth, 0)  3.74 us
  transfers between devices with their start and end apart: 13, of which 7 were waited for; matrix products, arithmetic and copies ran while one was open for 8% of the time, Pallas kernels for 0%

profile of v3, /device:TPU:40, one launch (start us, length us, event | category | flops | bytes accessed | tf_op | source)
XLA Modules:
  0.0 174.9 jit_solution(11127322356536887208)
XLA Ops:
  7.3 0.8 fusion.2
  8.1 0.1 copy.4
  8.2 0.1 broadcast_in_dim.55
  8.3 0.1 reshape.117
  8.4 2.5 %convert_reduce_fusion = (f32[]{:T(128)}, bf16[320,240]{1,0:T(8,128)(2,1)}) fusion(s32[]{:T(128)} %sub.66, bf16[320,240]{1,0:T(8,128)(2,1)} %param.2, pred[320]{0:T(512)(128)(4,1)S(1)} %get-tuple-element.7, pred[240]{0:T(512)(128)(4,1)S(1)} %get-tuple-element.13, pred[320]{0:T(512)(128)(4,1)S(1)} %get-tuple-element.8, ...), kind=kLoop, calls=%fused_computation.14 | loop fusion | flops 1151999 | bytes 310008 | tf_op jit(solution)/shard_map/reduce_sum | solution.py:112
  10.9 3.0 %collective-permute-start = (bf16[320,240]{1,0:T(8,128)(2,1)}, bf16[320,240]{1,0:T(8,128)(2,1)S(1)}, u32[]{:S(2)}, u32[]{:S(2)}) collective-permute-start(bf16[320,240]{1,0:T(8,128)(2,1)} %get-tuple-element.12), channel_id=1, source_target_pairs={{0,32},{32,0},{1,33},{33,1},{2,34},{34,2},{3,35},{35,3},{4,36},{36... | collective-permute-start | bytes 460808 | tf_op jit(solution)/shard_map/ppermute | solution.py:76
  14.2 11.7 %collective-permute-done = bf16[320,240]{1,0:T(8,128)(2,1)S(1)} collective-permute-done((bf16[320,240]{1,0:T(8,128)(2,1)}, bf16[320,240]{1,0:T(8,128)(2,1)S(1)}, u32[]{:S(2)}, u32[]{:S(2)}) %collective-permute-start) | collective-permute-done | bytes 153632 | tf_op jit(solution)/shard_map/ppermute | solution.py:76
  25.9 1.1 maximum_select_fusion.1
  27.0 4.3 %collective-permute-start.1 = (bf16[640,240]{1,0:T(8,128)(2,1)S(1)}, bf16[640,240]{1,0:T(8,128)(2,1)S(1)}, u32[]{:S(2)}, u32[]{:S(2)}) collective-permute-start(bf16[640,240]{1,0:T(8,128)(2,1)S(1)} %maximum_select_fusion.1), channel_id=1, source_target_pairs={{0,64},{64,128},{128,192},{192,256},{256,320},{320,384},{384,448},... | collective-permute-start | bytes 921608 | tf_op jit(solution)/shard_map/ppermute | solution.py:90
  31.3 12.3 %collective-permute-start.2 = (bf16[640,240]{1,0:T(8,128)(2,1)S(1)}, bf16[640,240]{1,0:T(8,128)(2,1)S(1)}, u32[]{:S(2)}, u32[]{:S(2)}) collective-permute-start(bf16[640,240]{1,0:T(8,128)(2,1)S(1)} %maximum_select_fusion.1), channel_id=1, source_target_pairs={{0,704},{64,0},{128,64},{192,128},{256,192},{320,256},{384,320},{4... | collective-permute-start | bytes 921608 | tf_op jit(solution)/shard_map/ppermute | solution.py:93
  43.5 1.0 fusion.4.keep_ref
  44.6 2.3 %broadcast_in_dim.57 = bf16[12,640,240]{2,1,0:T(8,128)(2,1)} broadcast(bf16[]{:T(256)} %constant.137.clone.1), dimensions={} | broadcast | bytes 3686402 | tf_op jit(solution)/shard_map/broadcast_in_dim | solution.py:83
  46.9 0.8 fusion
  47.7 1.0 collective-permute-done.1
  48.7 1.9 %collective-permute-start.3 = (bf16[640,240]{1,0:T(8,128)(2,1)S(1)}, bf16[640,240]{1,0:T(8,128)(2,1)S(1)}, u32[]{:S(2)}, u32[]{:S(2)}) collective-permute-start(bf16[640,240]{1,0:T(8,128)(2,1)S(1)} %collective-permute-done.1), channel_id=1, source_target_pairs={{0,64},{64,128},{128,192},{192,256},{256,320},{320,384},{384,448},... | collective-permute-start | bytes 921608 | tf_op jit(solution)/shard_map/ppermute | solution.py:90
  50.6 5.1 %collective-permute-start.4 = (bf16[640,240]{1,0:T(8,128)(2,1)S(1)}, bf16[640,240]{1,0:T(8,128)(2,1)S(1)}, u32[]{:S(2)}, u32[]{:S(2)}) collective-permute-start(bf16[640,240]{1,0:T(8,128)(2,1)S(1)} %collective-permute-done.2), channel_id=1, source_target_pairs={{0,704},{64,0},{128,64},{192,128},{256,192},{320,256},{384,320},{4... | collective-permute-start | bytes 921608 | tf_op jit(solution)/shard_map/ppermute | solution.py:93
  55.8 0.8 bitcast_dynamic-update-slice_fusion.10
  56.6 0.7 bitcast_dynamic-update-slice_fusion.9
  57.3 2.7 %collective-permute-done.3 = bf16[640,240]{1,0:T(8,128)(2,1)S(1)} collective-permute-done((bf16[640,240]{1,0:T(8,128)(2,1)S(1)}, bf16[640,240]{1,0:T(8,128)(2,1)S(1)}, u32[]{:S(2)}, u32[]{:S(2)}) %collective-permute-start.3) | collective-permute-done | bytes 307232 | tf_op jit(solution)/shard_map/ppermute | solution.py:90
  60.0 1.9 %collective-permute-start.5 = (bf16[640,240]{1,0:T(8,128)(2,1)S(1)}, bf16[640,240]{1,0:T(8,128)(2,1)S(1)}, u32[]{:S(2)}, u32[]{:S(2)}) collective-permute-start(bf16[640,240]{1,0:T(8,128)(2,1)S(1)} %collective-permute-done.3), channel_id=1, source_target_pairs={{0,64},{64,128},{128,192},{192,256},{256,320},{320,384},{384,448},... | collective-permute-start | bytes 921608 | tf_op jit(solution)/shard_map/ppermute | solution.py:90
  62.0 5.1 %collective-permute-start.6 = (bf16[640,240]{1,0:T(8,128)(2,1)S(1)}, bf16[640,240]{1,0:T(8,128)(2,1)S(1)}, u32[]{:S(2)}, u32[]{:S(2)}) collective-permute-start(bf16[640,240]{1,0:T(8,128)(2,1)S(1)} %collective-permute-done.4), channel_id=1, source_target_pairs={{0,704},{64,0},{128,64},{192,128},{256,192},{320,256},{384,320},{4... | collective-permute-start | bytes 921608 | tf_op jit(solution)/shard_map/ppermute | solution.py:93
  67.1 0.8 bitcast_dynamic-update-slice_fusion.8
  67.9 0.8 bitcast_dynamic-update-slice_fusion.7
  68.6 1.8 %collective-permute-done.5 = bf16[640,240]{1,0:T(8,128)(2,1)S(1)} collective-permute-done((bf16[640,240]{1,0:T(8,128)(2,1)S(1)}, bf16[640,240]{1,0:T(8,128)(2,1)S(1)}, u32[]{:S(2)}, u32[]{:S(2)}) %collective-permute-start.5) | collective-permute-done | bytes 307232 | tf_op jit(solution)/shard_map/ppermute | solution.py:90
  70.4 1.9 %collective-permute-start.7 = (bf16[640,240]{1,0:T(8,128)(2,1)S(1)}, bf16[640,240]{1,0:T(8,128)(2,1)S(1)}, u32[]{:S(2)}, u32[]{:S(2)}) collective-permute-start(bf16[640,240]{1,0:T(8,128)(2,1)S(1)} %collective-permute-done.5), channel_id=1, source_target_pairs={{0,64},{64,128},{128,192},{192,256},{256,320},{320,384},{384,448},... | collective-permute-start | bytes 921608 | tf_op jit(solution)/shard_map/ppermute | solution.py:90
  72.4 5.1 %collective-permute-start.8 = (bf16[640,240]{1,0:T(8,128)(2,1)S(1)}, bf16[640,240]{1,0:T(8,128)(2,1)S(1)}, u32[]{:S(2)}, u32[]{:S(2)}) collective-permute-start(bf16[640,240]{1,0:T(8,128)(2,1)S(1)} %collective-permute-done.6), channel_id=1, source_target_pairs={{0,704},{64,0},{128,64},{192,128},{256,192},{320,256},{384,320},{4... | collective-permute-start | bytes 921608 | tf_op jit(solution)/shard_map/ppermute | solution.py:93
  77.5 0.8 bitcast_dynamic-update-slice_fusion.6
  78.3 0.7 bitcast_dynamic-update-slice_fusion.5
  79.0 1.6 collective-permute-done.7
  80.6 1.9 %collective-permute-start.9 = (bf16[640,240]{1,0:T(8,128)(2,1)S(1)}, bf16[640,240]{1,0:T(8,128)(2,1)S(1)}, u32[]{:S(2)}, u32[]{:S(2)}) collective-permute-start(bf16[640,240]{1,0:T(8,128)(2,1)S(1)} %collective-permute-done.7), channel_id=1, source_target_pairs={{0,64},{64,128},{128,192},{192,256},{256,320},{320,384},{384,448},... | collective-permute-start | bytes 921608 | tf_op jit(solution)/shard_map/ppermute | solution.py:90
  82.5 5.1 %collective-permute-start.10 = (bf16[640,240]{1,0:T(8,128)(2,1)S(1)}, bf16[640,240]{1,0:T(8,128)(2,1)S(1)}, u32[]{:S(2)}, u32[]{:S(2)}) collective-permute-start(bf16[640,240]{1,0:T(8,128)(2,1)S(1)} %collective-permute-done.8), channel_id=1, source_target_pairs={{0,704},{64,0},{128,64},{192,128},{256,192},{320,256},{384,320},{4... | collective-permute-start | bytes 921608 | tf_op jit(solution)/shard_map/ppermute | solution.py:93
  87.7 0.8 bitcast_dynamic-update-slice_fusion.4
  88.4 0.8 bitcast_dynamic-update-slice_fusion.3
  89.2 1.6 collective-permute-done.9
  90.8 1.9 %collective-permute-start.11 = (bf16[640,240]{1,0:T(8,128)(2,1)S(1)}, bf16[640,240]{1,0:T(8,128)(2,1)S(1)}, u32[]{:S(2)}, u32[]{:S(2)}) collective-permute-start(bf16[640,240]{1,0:T(8,128)(2,1)S(1)} %collective-permute-done.9), channel_id=1, source_target_pairs={{0,64},{64,128},{128,192},{192,256},{256,320},{320,384},{384,448},... | collective-permute-start | bytes 921608 | tf_op jit(solution)/shard_map/ppermute | solution.py:90
  92.7 0.7 bitcast_dynamic-update-slice_fusion.2
  93.4 0.7 bitcast_dynamic-update-slice_fusion.1
  94.2 6.8 %collective-permute-done.11 = bf16[640,240]{1,0:T(8,128)(2,1)S(1)} collective-permute-done((bf16[640,240]{1,0:T(8,128)(2,1)S(1)}, bf16[640,240]{1,0:T(8,128)(2,1)S(1)}, u32[]{:S(2)}, u32[]{:S(2)}) %collective-permute-start.11) | collective-permute-done | bytes 307232 | tf_op jit(solution)/shard_map/ppermute | solution.py:90
  100.9 0.8 bitcast_dynamic-update-slice_fusion
  101.7 6.4 %shard_map.41 = (bf16[320,240]{1,0:T(8,128)(2,1)}, f32[8,128]{1,0:T(8,128)}) custom-call(s32[1]{0:T(128)} %bitcast.shift_ref, bf16[32,320,240]{2,1,0:T(8,128)(2,1)} %bitcast.31, bf16[7680,240]{1,0:T(8,128)(2,1)} %bitcast.15.right_ref, s32[320,240]{1,0:T(8,128)} %fusion.4.keep_ref), custom_call_target="tpu_custom_call" | custom-call | flops 1179648000 | bytes 9062400 | tf_op jit(solution)/shard_map/pallas_call | solution.py:56
  108.1 1.2 slice.23
  109.3 1.3 pad_maximum_fusion
  110.7 20.6 %psum.35 = f32[2]{0:T(128)S(1)} all-reduce(f32[2]{0:T(128)S(1)} %pad_maximum_fusion), channel_id=1, replica_groups=mesh['row_0'=12,'row_1'=2,'col_0'=4,'col_1'=4,'col_2'=2] {'row_0'}, use_global_device_ids=true, to_apply=%region_1.2 | all-reduce | flops 2 | bytes 16 | tf_op jit(solution)/shard_map/psum | solution.py:120
  131.2 8.8 %psum.36 = f32[2]{0:T(128)S(1)} all-reduce(f32[2]{0:T(128)S(1)} %psum.35), channel_id=1, replica_groups=mesh['row_0'=12,'row_1'=2,'col_0'=4,'col_1'=4,'col_2'=2] {'row_1'}, use_global_device_ids=true, to_apply=%region_2.3 | all-reduce | flops 2 | bytes 16 | tf_op jit(solution)/shard_map/psum | solution.py:120
  140.1 10.4 %psum.37 = f32[2]{0:T(128)S(1)} all-reduce(f32[2]{0:T(128)S(1)} %psum.36), channel_id=1, replica_groups=mesh['row_0'=12,'row_1'=2,'col_0'=4,'col_1'=4,'col_2'=2] {'col_0'}, use_global_device_ids=true, to_apply=%region_3.4 | all-reduce | flops 2 | bytes 16 | tf_op jit(solution)/shard_map/psum | solution.py:120
  150.5 14.6 %psum.38 = f32[2]{0:T(128)S(1)} all-reduce(f32[2]{0:T(128)S(1)} %psum.37), channel_id=1, replica_groups=mesh['row_0'=12,'row_1'=2,'col_0'=4,'col_1'=4,'col_2'=2] {'col_1'}, use_global_device_ids=true, to_apply=%region_4.5 | all-reduce | flops 2 | bytes 16 | tf_op jit(solution)/shard_map/psum | solution.py:120
  165.1 2.5 %psum.39 = f32[2]{0:T(128)S(1)} all-reduce(f32[2]{0:T(128)S(1)} %psum.38), channel_id=1, replica_groups=mesh['row_0'=12,'row_1'=2,'col_0'=4,'col_1'=4,'col_2'=2] {'col_2'}, use_global_device_ids=true, to_apply=%region_5.6 | all-reduce | flops 2 | bytes 16 | tf_op jit(solution)/shard_map/psum | solution.py:120
  167.6 0.5 broadcast_multiply_fusion
  (15 shorter events, 0.2 us)
Async XLA Ops:
  7.2 94.5 %all-gather.3.cloned.1.call-start = ((), (), s32[]{:S(2)}) async-start(), calls=%async_computation | async-start | bytes 5406720 | tf_op jit(solution)/shard_map/all_gather | solution.py:106
  10.9 36.0 %copy-start = (bf16[320,240]{1,0:T(8,128)(2,1)S(1)}, bf16[320,240]{1,0:T(8,128)(2,1)}, u32[]{:S(2)}) copy-start(bf16[320,240]{1,0:T(8,128)(2,1)} %get-tuple-element.12) | copy-start | bytes 460804
  10.9 15.0 %collective-permute-start = (bf16[320,240]{1,0:T(8,128)(2,1)}, bf16[320,240]{1,0:T(8,128)(2,1)S(1)}, u32[]{:S(2)}, u32[]{:S(2)}) collective-permute-start(bf16[320,240]{1,0:T(8,128)(2,1)} %get-tuple-element.12), channel_id=1, source_target_pairs={{0,32},{32,0},{1,33},{33,1},{2,34},{34,2},{3,35},{35,3},{4,36},{36... | collective-permute-start | bytes 460808 | tf_op jit(solution)/shard_map/ppermute | solution.py:76
  27.0 21.7 %collective-permute-start.1 = (bf16[640,240]{1,0:T(8,128)(2,1)S(1)}, bf16[640,240]{1,0:T(8,128)(2,1)S(1)}, u32[]{:S(2)}, u32[]{:S(2)}) collective-permute-start(bf16[640,240]{1,0:T(8,128)(2,1)S(1)} %maximum_select_fusion.1), channel_id=1, source_target_pairs={{0,64},{64,128},{128,192},{192,256},{256,320},{320,384},{384,448},... | collective-permute-start | bytes 921608 | tf_op jit(solution)/shard_map/ppermute | solution.py:90
  31.3 19.4 %collective-permute-start.2 = (bf16[640,240]{1,0:T(8,128)(2,1)S(1)}, bf16[640,240]{1,0:T(8,128)(2,1)S(1)}, u32[]{:S(2)}, u32[]{:S(2)}) collective-permute-start(bf16[640,240]{1,0:T(8,128)(2,1)S(1)} %maximum_select_fusion.1), channel_id=1, source_target_pairs={{0,704},{64,0},{128,64},{192,128},{256,192},{320,256},{384,320},{4... | collective-permute-start | bytes 921608 | tf_op jit(solution)/shard_map/ppermute | solution.py:93
  48.7 11.3 %collective-permute-start.3 = (bf16[640,240]{1,0:T(8,128)(2,1)S(1)}, bf16[640,240]{1,0:T(8,128)(2,1)S(1)}, u32[]{:S(2)}, u32[]{:S(2)}) collective-permute-start(bf16[640,240]{1,0:T(8,128)(2,1)S(1)} %collective-permute-done.1), channel_id=1, source_target_pairs={{0,64},{64,128},{128,192},{192,256},{256,320},{320,384},{384,448},... | collective-permute-start | bytes 921608 | tf_op jit(solution)/shard_map/ppermute | solution.py:90
  50.6 11.3 %collective-permute-start.4 = (bf16[640,240]{1,0:T(8,128)(2,1)S(1)}, bf16[640,240]{1,0:T(8,128)(2,1)S(1)}, u32[]{:S(2)}, u32[]{:S(2)}) collective-permute-start(bf16[640,240]{1,0:T(8,128)(2,1)S(1)} %collective-permute-done.2), channel_id=1, source_target_pairs={{0,704},{64,0},{128,64},{192,128},{256,192},{320,256},{384,320},{4... | collective-permute-start | bytes 921608 | tf_op jit(solution)/shard_map/ppermute | solution.py:93
  60.0 10.4 %collective-permute-start.5 = (bf16[640,240]{1,0:T(8,128)(2,1)S(1)}, bf16[640,240]{1,0:T(8,128)(2,1)S(1)}, u32[]{:S(2)}, u32[]{:S(2)}) collective-permute-start(bf16[640,240]{1,0:T(8,128)(2,1)S(1)} %collective-permute-done.3), channel_id=1, source_target_pairs={{0,64},{64,128},{128,192},{192,256},{256,320},{320,384},{384,448},... | collective-permute-start | bytes 921608 | tf_op jit(solution)/shard_map/ppermute | solution.py:90
  62.0 10.4 %collective-permute-start.6 = (bf16[640,240]{1,0:T(8,128)(2,1)S(1)}, bf16[640,240]{1,0:T(8,128)(2,1)S(1)}, u32[]{:S(2)}, u32[]{:S(2)}) collective-permute-start(bf16[640,240]{1,0:T(8,128)(2,1)S(1)} %collective-permute-done.4), channel_id=1, source_target_pairs={{0,704},{64,0},{128,64},{192,128},{256,192},{320,256},{384,320},{4... | collective-permute-start | bytes 921608 | tf_op jit(solution)/shard_map/ppermute | solution.py:93
  70.4 10.2 %collective-permute-start.7 = (bf16[640,240]{1,0:T(8,128)(2,1)S(1)}, bf16[640,240]{1,0:T(8,128)(2,1)S(1)}, u32[]{:S(2)}, u32[]{:S(2)}) collective-permute-start(bf16[640,240]{1,0:T(8,128)(2,1)S(1)} %collective-permute-done.5), channel_id=1, source_target_pairs={{0,64},{64,128},{128,192},{192,256},{256,320},{320,384},{384,448},... | collective-permute-start | bytes 921608 | tf_op jit(solution)/shard_map/ppermute | solution.py:90
  72.4 10.2 %collective-permute-start.8 = (bf16[640,240]{1,0:T(8,128)(2,1)S(1)}, bf16[640,240]{1,0:T(8,128)(2,1)S(1)}, u32[]{:S(2)}, u32[]{:S(2)}) collective-permute-start(bf16[640,240]{1,0:T(8,128)(2,1)S(1)} %collective-permute-done.6), channel_id=1, source_target_pairs={{0,704},{64,0},{128,64},{192,128},{256,192},{320,256},{384,320},{4... | collective-permute-start | bytes 921608 | tf_op jit(solution)/shard_map/ppermute | solution.py:93
  80.6 10.2 %collective-permute-start.9 = (bf16[640,240]{1,0:T(8,128)(2,1)S(1)}, bf16[640,240]{1,0:T(8,128)(2,1)S(1)}, u32[]{:S(2)}, u32[]{:S(2)}) collective-permute-start(bf16[640,240]{1,0:T(8,128)(2,1)S(1)} %collective-permute-done.7), channel_id=1, source_target_pairs={{0,64},{64,128},{128,192},{192,256},{256,320},{320,384},{384,448},... | collective-permute-start | bytes 921608 | tf_op jit(solution)/shard_map/ppermute | solution.py:90
  82.5 10.9 %collective-permute-start.10 = (bf16[640,240]{1,0:T(8,128)(2,1)S(1)}, bf16[640,240]{1,0:T(8,128)(2,1)S(1)}, u32[]{:S(2)}, u32[]{:S(2)}) collective-permute-start(bf16[640,240]{1,0:T(8,128)(2,1)S(1)} %collective-permute-done.8), channel_id=1, source_target_pairs={{0,704},{64,0},{128,64},{192,128},{256,192},{320,256},{384,320},{4... | collective-permute-start | bytes 921608 | tf_op jit(solution)/shard_map/ppermute | solution.py:93
  90.8 10.2 %collective-permute-start.11 = (bf16[640,240]{1,0:T(8,128)(2,1)S(1)}, bf16[640,240]{1,0:T(8,128)(2,1)S(1)}, u32[]{:S(2)}, u32[]{:S(2)}) collective-permute-start(bf16[640,240]{1,0:T(8,128)(2,1)S(1)} %collective-permute-done.9), channel_id=1, source_target_pairs={{0,64},{64,128},{128,192},{192,256},{256,320},{320,384},{384,448},... | collective-permute-start | bytes 921608 | tf_op jit(solution)/shard_map/ppermute | solution.py:90
Sparse Core Ops, SparseCore 0:
  11.0 75.2 all-gather.2

commit v4 on v3

--- a/solution.py
+++ b/solution.py
@@ -30,7 +30,9 @@
     return keep
 
 
-def panel_kernel(shift_ref, left_ref, right_ref, keep_ref, square_ref, trace_ref, total_ref):
+def panel_kernel(
+    place_ref, left_ref, right_ref, keep_ref, square_ref, trace_ref, total_ref
+):
     pieces, _, depth = left_ref.shape
     total_ref[...] = jnp.dot(
         left_ref[0], right_ref[0:depth, :], preferred_element_type=jnp.float32
@@ -45,29 +47,33 @@
     square_ref[...] = jnp.where(keep_ref[...] != 0, total, 0.0).astype(square_ref.dtype)
     rows = lax.broadcasted_iota(jnp.int32, total.shape, 0)
     cols = lax.broadcasted_iota(jnp.int32, total.shape, 1)
-    diagonal = jnp.sum(jnp.where(cols - rows == shift_ref[0], total, 0.0))
-    trace_ref[...] = jnp.full(trace_ref.shape, diagonal, jnp.float32)
+    on_diagonal = cols - rows == place_ref[0]
+    own = left_ref[place_ref[1]].astype(jnp.float32)
+    scale = 1.0 / place_ref[2].astype(jnp.float32)
+    trace_ref[0] = jnp.sum(jnp.where(on_diagonal, own, 0.0)) * scale
+    trace_ref[1] = jnp.sum(jnp.where(on_diagonal, total, 0.0)) * scale
 
 
-def panel_product(shift, left, right, keep):
+def panel_product(place, left, right, keep):
     pieces, tile_rows, depth = left.shape
     tile_cols = right.shape[1]
     vmem = pl.BlockSpec(memory_space=pltpu.VMEM)
+    smem = pl.BlockSpec(memory_space=pltpu.SMEM)
     return pl.pallas_call(
         panel_kernel,
         out_shape=(
             jax.ShapeDtypeStruct((tile_rows, tile_cols), jnp.bfloat16),
-            jax.ShapeDtypeStruct((8, 128), jnp.float32),
+            jax.ShapeDtypeStruct((2,), jnp.float32),
         ),
-        in_specs=[pl.BlockSpec(memory_space=pltpu.SMEM), vmem, vmem, vmem],
-        out_specs=(vmem, vmem),
+        in_specs=[smem, vmem, vmem, vmem],
+        out_specs=(vmem, smem),
         scratch_shapes=[pltpu.VMEM((tile_rows, tile_cols), jnp.float32)],
         cost_estimate=pl.CostEstimate(
             flops=2 * pieces * tile_rows * depth * tile_cols,
             bytes_accessed=2 * (left.size + right.size) + 6 * tile_rows * tile_cols,
             transcendentals=0,
         ),
-    )(shift, left, right, keep)
+    )(place, left, right, keep)
 
 
 def column_slab(masked):
@@ -106,19 +112,12 @@
     left_panel = lax.all_gather(masked, COL, axis=0, tiled=False)
     right_panel = column_slab(masked)
     shift = row_index * tile_rows - col_index * tile_cols
-    global_rows = jnp.arange(tile_rows, dtype=jnp.int32)[:, None]
-    global_cols = jnp.arange(tile_cols, dtype=jnp.int32)[None, :]
-    on_diagonal = global_cols - global_rows == shift
-    trace_first = jnp.sum(
-        jnp.where(on_diagonal, masked, jnp.zeros((), masked.dtype)), dtype=jnp.float32
+    place = jnp.stack([shift, col_index, jnp.int32(order_total)]).astype(jnp.int32)
+    squared, traces = panel_product(
+        place, left_panel, right_panel, keep_mask.astype(jnp.int32)
     )
-    squared, diagonal = panel_product(
-        shift.reshape(1), left_panel, right_panel, keep_mask.astype(jnp.int32)
-    )
-    summed = jnp.stack([trace_first, diagonal[0, 0]])
-    for axis in ROW_COL:
-        summed = lax.psum(summed, axis)
-    traces = summed / order_total
+    for axis in reversed(ROW_COL):
+        traces = lax.psum(traces, axis)
     return (squared, traces)
 
 

time: 176 us -> 172 us (0.977)
    reduce_sum x1 -> x0, other arithmetic: 2.48 us -> none  [on_device(): jnp.sum(jnp.where(on_diagonal, masked, jnp.zeros((), masked.dtype)), dtyp...]
    select_n x0 -> x1, other arithmetic: none -> 1.87 us  [on_device(): masked = jnp.where(keep_mask, iterate, jnp.zeros((), iterate.dtype))]
    ppermute x1, waiting for transfers between devices: 11.7 us -> 9.83 us  [column_slab(): other = lax.ppermute(masked, 'row_1', [(0, 1), (1, 0)])]
  transfers between devices with their start and end apart: 13 -> 13, of which waited for: 7 -> 7; matrix products, arithmetic and copies ran while one was open for 8% -> 9% of each run, Pallas kernels for 0% -> 0%
where the time goes in v4:
time: 172 us
  blocking collectives  57.5 us (33%)
  starting transfers between devices  49.5 us (29%)
  waiting for transfers between devices  25.5 us (15%)
  between operations  14.5 us (8%)
  local copies, waits for them, and re-layouts  10.9 us (6%)
  other arithmetic  7.54 us (4%)
  Pallas kernels  6.42 us (4%)
    psum x5, blocking collectives, on_device(): traces = lax.psum(traces, axis)  57.5 us
    ppermute x5, starting transfers between devices, column_slab(): behind = lax.ppermute(behind, 'row_0', backward)  32.8 us
    ppermute x6, waiting for transfers between devices, column_slab(): ahead = lax.ppermute(ahead, 'row_0', forward)  15.6 us
    ppermute x6, starting transfers between devices, column_slab(): ahead = lax.ppermute(ahead, 'row_0', forward)  13.8 us
    ppermute x1, waiting for transfers between devices, column_slab(): other = lax.ppermute(masked, 'row_1', [(0, 1), (1, 0)])  9.83 us
    pallas_call x1, Pallas kernels, panel_product(): pl.pallas_call(panel_kernel, out_shape=(jax.ShapeDtypeStruct((tile_rows,...  6.42 us
    dynamic_update_slice x6, local copies, waits for them, and re-layouts, column_slab(): lax.dynamic_update_index_in_dim(slab, ahead, (here - step) % depth, 0)  4.62 us
    dynamic_update_slice x5, local copies, waits for them, and re-layouts, column_slab(): lax.dynamic_update_index_in_dim(slab, behind, (here + step) % depth, 0)  3.74 us
  transfers between devices with their start and end apart: 13, of which 7 were waited for; matrix products, arithmetic and copies ran while one was open for 9% of the time, Pallas kernels for 0%

profile of v4, /device:TPU:40, one launch (start us, length us, event | category | flops | bytes accessed | tf_op | source)
XLA Modules:
  0.0 171.8 jit_solution(1213041212188514284)
XLA Ops:
  7.2 0.0 all-gather.3.cloned.1.call-start
  7.3 0.8 fusion.1
  8.1 0.1 copy.4
  8.2 0.1 broadcast_in_dim.52
  8.3 0.1 reshape.113
  8.4 1.9 %broadcast_select_fusion = bf16[320,240]{1,0:T(8,128)(2,1)} fusion(bf16[320,240]{1,0:T(8,128)(2,1)} %param.2, pred[320]{0:T(512)(128)(4,1)S(1)} %get-tuple-element.7, pred[240]{0:T(512)(128)(4,1)S(1)} %get-tuple-element.11, pred[320]{0:T(512)(128)(4,1)S(1)} %get-tuple-element.8, pred[240]{0:T(512)(128)(4,1)S(1)} %get-tuple-element.12, ...), kind=kLoop, calls=%fused_computation.15 | loop fusion | flops 768000 | bytes 310000 | tf_op jit(solution)/shard_map/jit(_where)/select_n | solution.py:111
  10.3 2.9 %collective-permute-start = (bf16[320,240]{1,0:T(8,128)(2,1)}, bf16[320,240]{1,0:T(8,128)(2,1)S(1)}, u32[]{:S(2)}, u32[]{:S(2)}) collective-permute-start(bf16[320,240]{1,0:T(8,128)(2,1)} %broadcast_select_fusion), channel_id=1, source_target_pairs={{0,32},{32,0},{1,33},{33,1},{2,34},{34,2},{3,35},{35,3},{4,36},{36... | collective-permute-start | bytes 460808 | tf_op jit(solution)/shard_map/ppermute | solution.py:82
  13.2 1.2 fusion.4
  14.7 0.6 pad_add_fusion.place_ref
  15.3 9.8 %collective-permute-done = bf16[320,240]{1,0:T(8,128)(2,1)S(1)} collective-permute-done((bf16[320,240]{1,0:T(8,128)(2,1)}, bf16[320,240]{1,0:T(8,128)(2,1)S(1)}, u32[]{:S(2)}, u32[]{:S(2)}) %collective-permute-start) | collective-permute-done | bytes 153632 | tf_op jit(solution)/shard_map/ppermute | solution.py:82
  25.1 1.1 maximum_select_fusion.1
  26.2 4.3 %collective-permute-start.1 = (bf16[640,240]{1,0:T(8,128)(2,1)S(1)}, bf16[640,240]{1,0:T(8,128)(2,1)S(1)}, u32[]{:S(2)}, u32[]{:S(2)}) collective-permute-start(bf16[640,240]{1,0:T(8,128)(2,1)S(1)} %maximum_select_fusion.1), channel_id=1, source_target_pairs={{0,64},{64,128},{128,192},{192,256},{256,320},{320,384},{384,448},... | collective-permute-start | bytes 921608 | tf_op jit(solution)/shard_map/ppermute | solution.py:96
  30.5 12.2 %collective-permute-start.2 = (bf16[640,240]{1,0:T(8,128)(2,1)S(1)}, bf16[640,240]{1,0:T(8,128)(2,1)S(1)}, u32[]{:S(2)}, u32[]{:S(2)}) collective-permute-start(bf16[640,240]{1,0:T(8,128)(2,1)S(1)} %maximum_select_fusion.1), channel_id=1, source_target_pairs={{0,704},{64,0},{128,64},{192,128},{256,192},{320,256},{384,320},{4... | collective-permute-start | bytes 921608 | tf_op jit(solution)/shard_map/ppermute | solution.py:99
  42.7 1.0 fusion.3.keep_ref
  43.8 2.3 %broadcast_in_dim.54 = bf16[12,640,240]{2,1,0:T(8,128)(2,1)} broadcast(bf16[]{:T(256)} %constant.136.clone.1), dimensions={} | broadcast | bytes 3686402 | tf_op jit(solution)/shard_map/broadcast_in_dim | solution.py:89
  46.1 0.8 fusion
  46.9 1.1 collective-permute-done.1
  48.0 1.9 %collective-permute-start.3 = (bf16[640,240]{1,0:T(8,128)(2,1)S(1)}, bf16[640,240]{1,0:T(8,128)(2,1)S(1)}, u32[]{:S(2)}, u32[]{:S(2)}) collective-permute-start(bf16[640,240]{1,0:T(8,128)(2,1)S(1)} %collective-permute-done.1), channel_id=1, source_target_pairs={{0,64},{64,128},{128,192},{192,256},{256,320},{320,384},{384,448},... | collective-permute-start | bytes 921608 | tf_op jit(solution)/shard_map/ppermute | solution.py:96
  49.9 5.1 %collective-permute-start.4 = (bf16[640,240]{1,0:T(8,128)(2,1)S(1)}, bf16[640,240]{1,0:T(8,128)(2,1)S(1)}, u32[]{:S(2)}, u32[]{:S(2)}) collective-permute-start(bf16[640,240]{1,0:T(8,128)(2,1)S(1)} %collective-permute-done.2), channel_id=1, source_target_pairs={{0,704},{64,0},{128,64},{192,128},{256,192},{320,256},{384,320},{4... | collective-permute-start | bytes 921608 | tf_op jit(solution)/shard_map/ppermute | solution.py:99
  55.0 0.8 bitcast_dynamic-update-slice_fusion.10
  55.8 0.7 bitcast_dynamic-update-slice_fusion.9
  56.6 2.8 %collective-permute-done.3 = bf16[640,240]{1,0:T(8,128)(2,1)S(1)} collective-permute-done((bf16[640,240]{1,0:T(8,128)(2,1)S(1)}, bf16[640,240]{1,0:T(8,128)(2,1)S(1)}, u32[]{:S(2)}, u32[]{:S(2)}) %collective-permute-start.3) | collective-permute-done | bytes 307232 | tf_op jit(solution)/shard_map/ppermute | solution.py:96
  59.3 1.9 %collective-permute-start.5 = (bf16[640,240]{1,0:T(8,128)(2,1)S(1)}, bf16[640,240]{1,0:T(8,128)(2,1)S(1)}, u32[]{:S(2)}, u32[]{:S(2)}) collective-permute-start(bf16[640,240]{1,0:T(8,128)(2,1)S(1)} %collective-permute-done.3), channel_id=1, source_target_pairs={{0,64},{64,128},{128,192},{192,256},{256,320},{320,384},{384,448},... | collective-permute-start | bytes 921608 | tf_op jit(solution)/shard_map/ppermute | solution.py:96
  61.3 5.1 %collective-permute-start.6 = (bf16[640,240]{1,0:T(8,128)(2,1)S(1)}, bf16[640,240]{1,0:T(8,128)(2,1)S(1)}, u32[]{:S(2)}, u32[]{:S(2)}) collective-permute-start(bf16[640,240]{1,0:T(8,128)(2,1)S(1)} %collective-permute-done.4), channel_id=1, source_target_pairs={{0,704},{64,0},{128,64},{192,128},{256,192},{320,256},{384,320},{4... | collective-permute-start | bytes 921608 | tf_op jit(solution)/shard_map/ppermute | solution.py:99
  66.4 0.8 bitcast_dynamic-update-slice_fusion.8
  67.2 0.8 bitcast_dynamic-update-slice_fusion.7
  67.9 1.8 %collective-permute-done.5 = bf16[640,240]{1,0:T(8,128)(2,1)S(1)} collective-permute-done((bf16[640,240]{1,0:T(8,128)(2,1)S(1)}, bf16[640,240]{1,0:T(8,128)(2,1)S(1)}, u32[]{:S(2)}, u32[]{:S(2)}) %collective-permute-start.5) | collective-permute-done | bytes 307232 | tf_op jit(solution)/shard_map/ppermute | solution.py:96
  69.8 1.9 %collective-permute-start.7 = (bf16[640,240]{1,0:T(8,128)(2,1)S(1)}, bf16[640,240]{1,0:T(8,128)(2,1)S(1)}, u32[]{:S(2)}, u32[]{:S(2)}) collective-permute-start(bf16[640,240]{1,0:T(8,128)(2,1)S(1)} %collective-permute-done.5), channel_id=1, source_target_pairs={{0,64},{64,128},{128,192},{192,256},{256,320},{320,384},{384,448},... | collective-permute-start | bytes 921608 | tf_op jit(solution)/shard_map/ppermute | solution.py:96
  71.7 5.1 %collective-permute-start.8 = (bf16[640,240]{1,0:T(8,128)(2,1)S(1)}, bf16[640,240]{1,0:T(8,128)(2,1)S(1)}, u32[]{:S(2)}, u32[]{:S(2)}) collective-permute-start(bf16[640,240]{1,0:T(8,128)(2,1)S(1)} %collective-permute-done.6), channel_id=1, source_target_pairs={{0,704},{64,0},{128,64},{192,128},{256,192},{320,256},{384,320},{4... | collective-permute-start | bytes 921608 | tf_op jit(solution)/shard_map/ppermute | solution.py:99
  76.9 0.8 bitcast_dynamic-update-slice_fusion.6
  77.6 0.7 bitcast_dynamic-update-slice_fusion.5
  78.4 1.6 collective-permute-done.7
  80.0 1.9 %collective-permute-start.9 = (bf16[640,240]{1,0:T(8,128)(2,1)S(1)}, bf16[640,240]{1,0:T(8,128)(2,1)S(1)}, u32[]{:S(2)}, u32[]{:S(2)}) collective-permute-start(bf16[640,240]{1,0:T(8,128)(2,1)S(1)} %collective-permute-done.7), channel_id=1, source_target_pairs={{0,64},{64,128},{128,192},{192,256},{256,320},{320,384},{384,448},... | collective-permute-start | bytes 921608 | tf_op jit(solution)/shard_map/ppermute | solution.py:96
  81.9 5.1 %collective-permute-start.10 = (bf16[640,240]{1,0:T(8,128)(2,1)S(1)}, bf16[640,240]{1,0:T(8,128)(2,1)S(1)}, u32[]{:S(2)}, u32[]{:S(2)}) collective-permute-start(bf16[640,240]{1,0:T(8,128)(2,1)S(1)} %collective-permute-done.8), channel_id=1, source_target_pairs={{0,704},{64,0},{128,64},{192,128},{256,192},{320,256},{384,320},{4... | collective-permute-start | bytes 921608 | tf_op jit(solution)/shard_map/ppermute | solution.py:99
  87.0 0.8 bitcast_dynamic-update-slice_fusion.4
  87.8 0.8 bitcast_dynamic-update-slice_fusion.3
  88.5 1.6 collective-permute-done.9
  90.1 1.9 %collective-permute-start.11 = (bf16[640,240]{1,0:T(8,128)(2,1)S(1)}, bf16[640,240]{1,0:T(8,128)(2,1)S(1)}, u32[]{:S(2)}, u32[]{:S(2)}) collective-permute-start(bf16[640,240]{1,0:T(8,128)(2,1)S(1)} %collective-permute-done.9), channel_id=1, source_target_pairs={{0,64},{64,128},{128,192},{192,256},{256,320},{320,384},{384,448},... | collective-permute-start | bytes 921608 | tf_op jit(solution)/shard_map/ppermute | solution.py:96
  92.0 0.7 bitcast_dynamic-update-slice_fusion.2
  92.8 0.7 bitcast_dynamic-update-slice_fusion.1
  93.5 6.8 %collective-permute-done.11 = bf16[640,240]{1,0:T(8,128)(2,1)S(1)} collective-permute-done((bf16[640,240]{1,0:T(8,128)(2,1)S(1)}, bf16[640,240]{1,0:T(8,128)(2,1)S(1)}, u32[]{:S(2)}, u32[]{:S(2)}) %collective-permute-start.11) | collective-permute-done | bytes 307232 | tf_op jit(solution)/shard_map/ppermute | solution.py:96
  100.3 0.8 bitcast_dynamic-update-slice_fusion
  101.0 6.4 %shard_map.41 = (bf16[320,240]{1,0:T(8,128)(2,1)}, f32[2]{0:T(128)}) custom-call(s32[3]{0:T(128)} %pad_add_fusion.place_ref, bf16[32,320,240]{2,1,0:T(8,128)(2,1)} %bitcast.31, bf16[7680,240]{1,0:T(8,128)(2,1)} %bitcast.16.right_ref, s32[320,240]{1,0:T(8,128)} %fusion.3.keep_ref), custom_call_target="tpu_custom_call" | custom-call | flops 1179648000 | bytes 9062400 | tf_op jit(solution)/shard_map/pallas_call | solution.py:62
  107.5 2.6 %psum.35 = f32[2]{0:T(128)S(1)} all-reduce(f32[2]{0:T(128)} %get-tuple-element.5), channel_id=1, replica_groups=mesh['row_0'=12,'row_1'=2,'col_0'=4,'col_1'=4,'col_2'=2] {'col_2'}, use_global_device_ids=true, to_apply=%region_0.1 | all-reduce | flops 2 | bytes 16 | tf_op jit(solution)/shard_map/psum | solution.py:120
  110.1 14.4 %psum.36 = f32[2]{0:T(128)S(1)} all-reduce(f32[2]{0:T(128)S(1)} %psum.35), channel_id=1, replica_groups=mesh['row_0'=12,'row_1'=2,'col_0'=4,'col_1'=4,'col_2'=2] {'col_1'}, use_global_device_ids=true, to_apply=%region_1.2 | all-reduce | flops 2 | bytes 16 | tf_op jit(solution)/shard_map/psum | solution.py:120
  124.5 10.5 %psum.37 = f32[2]{0:T(128)S(1)} all-reduce(f32[2]{0:T(128)S(1)} %psum.36), channel_id=1, replica_groups=mesh['row_0'=12,'row_1'=2,'col_0'=4,'col_1'=4,'col_2'=2] {'col_0'}, use_global_device_ids=true, to_apply=%region_2.3 | all-reduce | flops 2 | bytes 16 | tf_op jit(solution)/shard_map/psum | solution.py:120
  135.0 8.8 %psum.38 = f32[2]{0:T(128)S(1)} all-reduce(f32[2]{0:T(128)S(1)} %psum.37), channel_id=1, replica_groups=mesh['row_0'=12,'row_1'=2,'col_0'=4,'col_1'=4,'col_2'=2] {'row_1'}, use_global_device_ids=true, to_apply=%region_3.4 | all-reduce | flops 2 | bytes 16 | tf_op jit(solution)/shard_map/psum | solution.py:120
  143.9 21.1 %psum.39 = f32[2]{0:T(128)} all-reduce(f32[2]{0:T(128)S(1)} %psum.38), channel_id=1, replica_groups=mesh['row_0'=12,'row_1'=2,'col_0'=4,'col_1'=4,'col_2'=2] {'row_0'}, use_global_device_ids=true, to_apply=%region_4.5 | all-reduce | flops 2 | bytes 16 | tf_op jit(solution)/shard_map/psum | solution.py:120
  (12 shorter events, 0.1 us)
Async XLA Ops:
  7.2 93.9 %all-gather.3.cloned.1.call-start = ((), (), s32[]{:S(2)}) async-start(), calls=%async_computation | async-start | bytes 5406720 | tf_op jit(solution)/shard_map/all_gather | solution.py:112
  10.3 14.8 %collective-permute-start = (bf16[320,240]{1,0:T(8,128)(2,1)}, bf16[320,240]{1,0:T(8,128)(2,1)S(1)}, u32[]{:S(2)}, u32[]{:S(2)}) collective-permute-start(bf16[320,240]{1,0:T(8,128)(2,1)} %broadcast_select_fusion), channel_id=1, source_target_pairs={{0,32},{32,0},{1,33},{33,1},{2,34},{34,2},{3,35},{35,3},{4,36},{36... | collective-permute-start | bytes 460808 | tf_op jit(solution)/shard_map/ppermute | solution.py:82
  26.2 21.7 %collective-permute-start.1 = (bf16[640,240]{1,0:T(8,128)(2,1)S(1)}, bf16[640,240]{1,0:T(8,128)(2,1)S(1)}, u32[]{:S(2)}, u32[]{:S(2)}) collective-permute-start(bf16[640,240]{1,0:T(8,128)(2,1)S(1)} %maximum_select_fusion.1), channel_id=1, source_target_pairs={{0,64},{64,128},{128,192},{192,256},{256,320},{320,384},{384,448},... | collective-permute-start | bytes 921608 | tf_op jit(solution)/shard_map/ppermute | solution.py:96
  30.5 19.4 %collective-permute-start.2 = (bf16[640,240]{1,0:T(8,128)(2,1)S(1)}, bf16[640,240]{1,0:T(8,128)(2,1)S(1)}, u32[]{:S(2)}, u32[]{:S(2)}) collective-permute-start(bf16[640,240]{1,0:T(8,128)(2,1)S(1)} %maximum_select_fusion.1), channel_id=1, source_target_pairs={{0,704},{64,0},{128,64},{192,128},{256,192},{320,256},{384,320},{4... | collective-permute-start | bytes 921608 | tf_op jit(solution)/shard_map/ppermute | solution.py:99
  48.0 11.4 %collective-permute-start.3 = (bf16[640,240]{1,0:T(8,128)(2,1)S(1)}, bf16[640,240]{1,0:T(8,128)(2,1)S(1)}, u32[]{:S(2)}, u32[]{:S(2)}) collective-permute-start(bf16[640,240]{1,0:T(8,128)(2,1)S(1)} %collective-permute-done.1), channel_id=1, source_target_pairs={{0,64},{64,128},{128,192},{192,256},{256,320},{320,384},{384,448},... | collective-permute-start | bytes 921608 | tf_op jit(solution)/shard_map/ppermute | solution.py:96
  49.9 11.4 %collective-permute-start.4 = (bf16[640,240]{1,0:T(8,128)(2,1)S(1)}, bf16[640,240]{1,0:T(8,128)(2,1)S(1)}, u32[]{:S(2)}, u32[]{:S(2)}) collective-permute-start(bf16[640,240]{1,0:T(8,128)(2,1)S(1)} %collective-permute-done.2), channel_id=1, source_target_pairs={{0,704},{64,0},{128,64},{192,128},{256,192},{320,256},{384,320},{4... | collective-permute-start | bytes 921608 | tf_op jit(solution)/shard_map/ppermute | solution.py:99
  59.3 10.4 %collective-permute-start.5 = (bf16[640,240]{1,0:T(8,128)(2,1)S(1)}, bf16[640,240]{1,0:T(8,128)(2,1)S(1)}, u32[]{:S(2)}, u32[]{:S(2)}) collective-permute-start(bf16[640,240]{1,0:T(8,128)(2,1)S(1)} %collective-permute-done.3), channel_id=1, source_target_pairs={{0,64},{64,128},{128,192},{192,256},{256,320},{320,384},{384,448},... | collective-permute-start | bytes 921608 | tf_op jit(solution)/shard_map/ppermute | solution.py:96
  61.3 10.4 %collective-permute-start.6 = (bf16[640,240]{1,0:T(8,128)(2,1)S(1)}, bf16[640,240]{1,0:T(8,128)(2,1)S(1)}, u32[]{:S(2)}, u32[]{:S(2)}) collective-permute-start(bf16[640,240]{1,0:T(8,128)(2,1)S(1)} %collective-permute-done.4), channel_id=1, source_target_pairs={{0,704},{64,0},{128,64},{192,128},{256,192},{320,256},{384,320},{4... | collective-permute-start | bytes 921608 | tf_op jit(solution)/shard_map/ppermute | solution.py:99
  69.8 10.2 %collective-permute-start.7 = (bf16[640,240]{1,0:T(8,128)(2,1)S(1)}, bf16[640,240]{1,0:T(8,128)(2,1)S(1)}, u32[]{:S(2)}, u32[]{:S(2)}) collective-permute-start(bf16[640,240]{1,0:T(8,128)(2,1)S(1)} %collective-permute-done.5), channel_id=1, source_target_pairs={{0,64},{64,128},{128,192},{192,256},{256,320},{320,384},{384,448},... | collective-permute-start | bytes 921608 | tf_op jit(solution)/shard_map/ppermute | solution.py:96
  71.7 10.2 %collective-permute-start.8 = (bf16[640,240]{1,0:T(8,128)(2,1)S(1)}, bf16[640,240]{1,0:T(8,128)(2,1)S(1)}, u32[]{:S(2)}, u32[]{:S(2)}) collective-permute-start(bf16[640,240]{1,0:T(8,128)(2,1)S(1)} %collective-permute-done.6), channel_id=1, source_target_pairs={{0,704},{64,0},{128,64},{192,128},{256,192},{320,256},{384,320},{4... | collective-permute-start | bytes 921608 | tf_op jit(solution)/shard_map/ppermute | solution.py:99
  80.0 10.2 %collective-permute-start.9 = (bf16[640,240]{1,0:T(8,128)(2,1)S(1)}, bf16[640,240]{1,0:T(8,128)(2,1)S(1)}, u32[]{:S(2)}, u32[]{:S(2)}) collective-permute-start(bf16[640,240]{1,0:T(8,128)(2,1)S(1)} %collective-permute-done.7), channel_id=1, source_target_pairs={{0,64},{64,128},{128,192},{192,256},{256,320},{320,384},{384,448},... | collective-permute-start | bytes 921608 | tf_op jit(solution)/shard_map/ppermute | solution.py:96
  81.9 10.9 %collective-permute-start.10 = (bf16[640,240]{1,0:T(8,128)(2,1)S(1)}, bf16[640,240]{1,0:T(8,128)(2,1)S(1)}, u32[]{:S(2)}, u32[]{:S(2)}) collective-permute-start(bf16[640,240]{1,0:T(8,128)(2,1)S(1)} %collective-permute-done.8), channel_id=1, source_target_pairs={{0,704},{64,0},{128,64},{192,128},{256,192},{320,256},{384,320},{4... | collective-permute-start | bytes 921608 | tf_op jit(solution)/shard_map/ppermute | solution.py:99
  90.1 10.2 %collective-permute-start.11 = (bf16[640,240]{1,0:T(8,128)(2,1)S(1)}, bf16[640,240]{1,0:T(8,128)(2,1)S(1)}, u32[]{:S(2)}, u32[]{:S(2)}) collective-permute-start(bf16[640,240]{1,0:T(8,128)(2,1)S(1)} %collective-permute-done.9), channel_id=1, source_target_pairs={{0,64},{64,128},{128,192},{192,256},{256,320},{320,384},{384,448},... | collective-permute-start | bytes 921608 | tf_op jit(solution)/shard_map/ppermute | solution.py:96
Sparse Core Ops, SparseCore 0:
  11.0 75.1 all-gather.2

commit v5 on v3

--- a/solution.py
+++ b/solution.py
@@ -1,3 +1,5 @@
+import math
+
 import jax
 import jax.numpy as jnp
 from jax import lax
@@ -30,7 +32,7 @@
     return keep
 
 
-def panel_kernel(shift_ref, left_ref, right_ref, keep_ref, square_ref, trace_ref, total_ref):
+def panel_kernel(left_ref, right_ref, keep_ref, square_ref, total_ref):
     pieces, _, depth = left_ref.shape
     total_ref[...] = jnp.dot(
         left_ref[0], right_ref[0:depth, :], preferred_element_type=jnp.float32
@@ -41,36 +43,137 @@
             right_ref[piece * depth:(piece + 1) * depth, :],
             preferred_element_type=jnp.float32,
         )
-    total = total_ref[...]
-    square_ref[...] = jnp.where(keep_ref[...] != 0, total, 0.0).astype(square_ref.dtype)
-    rows = lax.broadcasted_iota(jnp.int32, total.shape, 0)
-    cols = lax.broadcasted_iota(jnp.int32, total.shape, 1)
-    diagonal = jnp.sum(jnp.where(cols - rows == shift_ref[0], total, 0.0))
-    trace_ref[...] = jnp.full(trace_ref.shape, diagonal, jnp.float32)
-
-
-def panel_product(shift, left, right, keep):
+    square_ref[...] = jnp.where(keep_ref[...] != 0, total_ref[...], 0.0).astype(square_ref.dtype)
+
+
+def panel_product(left, right, keep):
     pieces, tile_rows, depth = left.shape
     tile_cols = right.shape[1]
     vmem = pl.BlockSpec(memory_space=pltpu.VMEM)
     return pl.pallas_call(
         panel_kernel,
-        out_shape=(
-            jax.ShapeDtypeStruct((tile_rows, tile_cols), jnp.bfloat16),
-            jax.ShapeDtypeStruct((8, 128), jnp.float32),
-        ),
-        in_specs=[pl.BlockSpec(memory_space=pltpu.SMEM), vmem, vmem, vmem],
-        out_specs=(vmem, vmem),
+        out_shape=jax.ShapeDtypeStruct((tile_rows, tile_cols), jnp.bfloat16),
+        in_specs=[vmem, vmem, vmem],
+        out_specs=vmem,
         scratch_shapes=[pltpu.VMEM((tile_rows, tile_cols), jnp.float32)],
         cost_estimate=pl.CostEstimate(
             flops=2 * pieces * tile_rows * depth * tile_cols,
             bytes_accessed=2 * (left.size + right.size) + 6 * tile_rows * tile_cols,
             transcendentals=0,
         ),
-    )(shift, left, right, keep)
-
-
-def column_slab(masked):
+    )(left, right, keep)
+
+
+def local_rounds(row_group, col_group, rows_per, cols_per):
+    senders = [(a, b) for a in range(row_group) for b in range(col_group)]
+    edges = {}
+    for a, b in senders:
+        edges[(a, b)] = [
+            (u, v, ((cols_per * b + v) // rows_per, (rows_per * a + u) // cols_per))
+            for u in range(rows_per)
+            for v in range(cols_per)
+        ]
+    rounds = []
+    for _ in range(rows_per * cols_per):
+        owner = {}
+
+        def augment(sender, seen):
+            for index, (_, _, receiver) in enumerate(edges[sender]):
+                if receiver in seen:
+                    continue
+                seen.add(receiver)
+                if receiver not in owner or augment(owner[receiver][0], seen):
+                    owner[receiver] = (sender, index)
+                    return True
+            return False
+
+        for sender in senders:
+            if not augment(sender, set()):
+                raise ValueError("no matching")
+        chosen = {}
+        for receiver, (sender, index) in owner.items():
+            chosen[sender] = edges[sender][index]
+        for sender, edge in chosen.items():
+            edges[sender].remove(edge)
+        rounds.append(chosen)
+    return rounds
+
+
+def transposed_pairs(tile, rows, cols, fine):
+    tile_rows, tile_cols = tile.shape
+    rows_per, cols_per = tile_rows // fine, tile_cols // fine
+    super_size = math.lcm(tile_rows, tile_cols)
+    row_group, col_group = super_size // tile_rows, super_size // tile_cols
+    row_index = lax.axis_index(ROW)
+    col_index = lax.axis_index(COL)
+    local = (row_index % row_group) * col_group + col_index % col_group
+    same_super = row_index // row_group == col_index // col_group
+    total = jnp.zeros((), jnp.float32)
+    for chosen in local_rounds(row_group, col_group, rows_per, cols_per):
+        send_u, send_v, recv_u, recv_v, to_self = [], [], [], [], []
+        by_receiver = {}
+        for (a, b), (u, v, (a2, b2)) in sorted(chosen.items()):
+            by_receiver[(a2, b2)] = (cols_per * b + v - rows_per * a2, rows_per * a + u - cols_per * b2)
+        for a in range(row_group):
+            for b in range(col_group):
+                u, v, (a2, b2) = chosen[(a, b)]
+                send_u.append(u)
+                send_v.append(v)
+                recv_u.append(by_receiver[(a, b)][0])
+                recv_v.append(by_receiver[(a, b)][1])
+                to_self.append((a2, b2) == (a, b))
+        pairs = []
+        for r in range(rows):
+            for c in range(cols):
+                big_i, a = divmod(r, row_group)
+                big_j, b = divmod(c, col_group)
+                u, v, (a2, b2) = chosen[(a, b)]
+                dest = (big_j * row_group + a2) * cols + big_i * col_group + b2
+                if dest != r * cols + c:
+                    pairs.append((r * cols + c, dest))
+        pick = lambda table: jnp.asarray(table, jnp.int32)[local]
+        block = lax.dynamic_slice(
+            tile, (pick(send_u) * fine, pick(send_v) * fine), (fine, fine)
+        )
+        got = lax.ppermute(block, ROW_COL, pairs)
+        got = jnp.where(same_super & jnp.asarray(to_self)[local], block, got)
+        mine = lax.dynamic_slice(
+            tile, (pick(recv_u) * fine, pick(recv_v) * fine), (fine, fine)
+        )
+        total = total + jnp.sum(mine.astype(jnp.float32) * got.astype(jnp.float32).T)
+    return total
+
+
+def exchange(value, axis, size, stride, group):
+    position = (lax.axis_index(axis) // stride) % group
+    received = [value]
+    for shift in range(1, group):
+        pairs = []
+        for i in range(size):
+            here = (i // stride) % group
+            pairs.append((i, i + stride * ((here + shift) % group - here)))
+        received.append(lax.ppermute(value, axis, pairs))
+    total = None
+    for origin in range(group):
+        pick = received[0]
+        for here in range(group):
+            pick = jnp.where(position == here, received[(here - origin) % group], pick)
+        total = pick if total is None else total + pick
+    return total
+
+
+def reduction_stages():
+    stages = []
+    for axis, size in (("col_2", 2), ("col_1", 4), ("col_0", 4), ("row_1", 2), ("row_0", 12)):
+        stride = 1
+        for group in (4, 3, 2):
+            while size % (stride * group) == 0 and stride * group <= size:
+                stages.append((axis, size, stride, group))
+                stride *= group
+    return stages
+
+
+def column_slab(masked, partial, stages):
     depth = lax.psum(1, "row_0")
     half = lax.axis_index("row_1")
     other = lax.ppermute(masked, "row_1", [(0, 1), (1, 0)])
@@ -88,11 +191,17 @@
     behind = pair
     for step in range(1, depth // 2 + 1):
         ahead = lax.ppermute(ahead, "row_0", forward)
+        if step < depth - depth // 2:
+            behind = lax.ppermute(behind, "row_0", backward)
+        if stages:
+            partial = exchange(partial, *stages.pop(0))
+        ahead, behind, partial = lax.optimization_barrier((ahead, behind, partial))
         slab = lax.dynamic_update_index_in_dim(slab, ahead, (here - step) % depth, 0)
         if step < depth - depth // 2:
-            behind = lax.ppermute(behind, "row_0", backward)
             slab = lax.dynamic_update_index_in_dim(slab, behind, (here + step) % depth, 0)
-    return slab.reshape(depth * pair.shape[0], pair.shape[1])
+    for stage in stages:
+        partial = exchange(partial, *stage)
+    return slab.reshape(depth * pair.shape[0], pair.shape[1]), partial
 
 
 def on_device(iterate, pattern):
@@ -104,20 +213,18 @@
     keep_mask = tile_keep(pattern, row_index, col_index, tile_rows, tile_cols)
     masked = jnp.where(keep_mask, iterate, jnp.zeros((), iterate.dtype))
     left_panel = lax.all_gather(masked, COL, axis=0, tiled=False)
-    right_panel = column_slab(masked)
     shift = row_index * tile_rows - col_index * tile_cols
-    global_rows = jnp.arange(tile_rows, dtype=jnp.int32)[:, None]
-    global_cols = jnp.arange(tile_cols, dtype=jnp.int32)[None, :]
-    on_diagonal = global_cols - global_rows == shift
+    rows_local = jnp.arange(tile_rows, dtype=jnp.int32)[:, None]
+    cols_local = jnp.arange(tile_cols, dtype=jnp.int32)[None, :]
+    on_diagonal = cols_local - rows_local == shift
     trace_first = jnp.sum(
         jnp.where(on_diagonal, masked, jnp.zeros((), masked.dtype)), dtype=jnp.float32
     )
-    squared, diagonal = panel_product(
-        shift.reshape(1), left_panel, right_panel, keep_mask.astype(jnp.int32)
-    )
-    summed = jnp.stack([trace_first, diagonal[0, 0]])
-    for axis in ROW_COL:
-        summed = lax.psum(summed, axis)
+    rows, cols = lax.psum(1, ROW), lax.psum(1, COL)
+    trace_second = transposed_pairs(masked, rows, cols, math.gcd(tile_rows, tile_cols))
+    partial = jnp.stack([trace_first, trace_second])
+    right_panel, summed = column_slab(masked, partial, reduction_stages())
+    squared = panel_product(left_panel, right_panel, keep_mask.astype(jnp.int32))
     traces = summed / order_total
     return (squared, traces)
 

time: 176 us -> 402 us (2.28)
  the two profiles are of different devices: /device:TPU:40 before, /device:TPU:10 now
where the time goes in v5:
time: 402 us; the launch traced here: 400 us
  starting transfers between devices  207 us (51%)
  local copies, waits for them, and re-layouts  78.4 us (20%)
  between operations  54.4 us (14%)
  waiting for transfers between devices  39.2 us (10%)
  other arithmetic  14.9 us (4%)
  Pallas kernels  6.38 us (2%)
    ppermute x12, starting transfers between devices, transposed_pairs(): got = lax.ppermute(block, ROW_COL, pairs)  79.6 us
    ppermute x13, starting transfers between devices, exchange(): received.append(lax.ppermute(value, axis, pairs))  63.4 us
    dynamic_slice x46, local copies, waits for them, and re-layouts, transposed_pairs(): pick = lambda table: jnp.asarray(table, jnp.int32)[local]  58.9 us
    ppermute x5, starting transfers between devices, column_slab(): behind = lax.ppermute(behind, 'row_0', backward)  46.1 us
    ppermute x6, waiting for transfers between devices, column_slab(): ahead = lax.ppermute(ahead, 'row_0', forward)  15.4 us
    ppermute x6, starting transfers between devices, column_slab(): ahead = lax.ppermute(ahead, 'row_0', forward)  15.4 us
    ppermute x12, waiting for transfers between devices, transposed_pairs(): got = lax.ppermute(block, ROW_COL, pairs)  13.5 us
    ppermute x5, waiting for transfers between devices, column_slab(): behind = lax.ppermute(behind, 'row_0', backward)  9.06 us
  transfers between devices with their start and end apart: 38, of which 14 were waited for; matrix products, arithmetic and copies ran while one was open for 22% of the time, Pallas kernels for 0%

profile of v5, /device:TPU:10, one launch (start us, length us, event | category | flops | bytes accessed | tf_op | source)
XLA Modules:
  0.0 399.8 jit_solution(3916733821673895738)
XLA Ops:
  8.4 2.5 convert_reduce_fusion
  39.1 11.6 %collective-permute-start.14 = (bf16[80,80]{0,1:T(8,128)(2,1)S(1)}, bf16[80,80]{0,1:T(8,128)(2,1)S(1)}, u32[]{:S(2)}, u32[]{:S(2)}) collective-permute-start(bf16[80,80]{0,1:T(8,128)(2,1)S(1)} %copy.104), channel_id=1, source_target_pairs={{1,32},{2,33},{3,64},{4,96},{5,128},{6,129},{7,160},{8,192},{9,224... | collective-permute-start | bytes 38408 | tf_op jit(solution)/shard_map/ppermute | solution.py:138
  86.6 2.4 collective-permute-start.11
  89.1 8.1 %collective-permute-start.7 = (bf16[80,80]{0,1:T(8,128)(2,1)S(1)}, bf16[80,80]{0,1:T(8,128)(2,1)S(1)}, u32[]{:S(2)}, u32[]{:S(2)}) collective-permute-start(bf16[80,80]{0,1:T(8,128)(2,1)S(1)} %copy.97), channel_id=1, source_target_pairs={{1,32},{2,64},{3,65},{4,96},{5,128},{6,160},{7,161},{8,192},{9,224... | collective-permute-start | bytes 38408 | tf_op jit(solution)/shard_map/ppermute | solution.py:138
  97.3 5.0 %collective-permute-start.10 = (bf16[80,80]{0,1:T(8,128)(2,1)S(1)}, bf16[80,80]{0,1:T(8,128)(2,1)S(1)}, u32[]{:S(2)}, u32[]{:S(2)}) collective-permute-start(bf16[80,80]{0,1:T(8,128)(2,1)S(1)} %copy.100), channel_id=1, source_target_pairs={{1,33},{2,32},{3,64},{4,96},{5,129},{6,128},{7,160},{8,192},{9,225... | collective-permute-start | bytes 38408 | tf_op jit(solution)/shard_map/ppermute | solution.py:138
  102.4 8.6 %collective-permute-start.6 = (bf16[80,80]{0,1:T(8,128)(2,1)S(1)}, bf16[80,80]{0,1:T(8,128)(2,1)S(1)}, u32[]{:S(2)}, u32[]{:S(2)}) collective-permute-start(bf16[80,80]{0,1:T(8,128)(2,1)S(1)} %copy.96), channel_id=1, source_target_pairs={{1,32},{2,64},{3,65},{4,96},{5,128},{6,160},{7,161},{8,192},{9,224... | collective-permute-start | bytes 38408 | tf_op jit(solution)/shard_map/ppermute | solution.py:138
  147.5 4.1 %collective-permute-start.12 = (bf16[80,80]{0,1:T(8,128)(2,1)S(1)}, bf16[80,80]{0,1:T(8,128)(2,1)S(1)}, u32[]{:S(2)}, u32[]{:S(2)}) collective-permute-start(bf16[80,80]{0,1:T(8,128)(2,1)S(1)} %copy.102), channel_id=1, source_target_pairs={{1,32},{2,33},{3,64},{4,96},{5,128},{6,129},{7,160},{8,192},{9,224... | collective-permute-start | bytes 38408 | tf_op jit(solution)/shard_map/ppermute | solution.py:138
  151.7 6.1 %collective-permute-start.13 = (bf16[80,80]{0,1:T(8,128)(2,1)S(1)}, bf16[80,80]{0,1:T(8,128)(2,1)S(1)}, u32[]{:S(2)}, u32[]{:S(2)}) collective-permute-start(bf16[80,80]{0,1:T(8,128)(2,1)S(1)} %copy.103), channel_id=1, source_target_pairs={{1,32},{2,65},{3,64},{4,96},{5,128},{6,161},{7,160},{8,192},{9,224... | collective-permute-start | bytes 38408 | tf_op jit(solution)/shard_map/ppermute | solution.py:138
  157.8 7.2 %collective-permute-start.3 = (bf16[80,80]{0,1:T(8,128)(2,1)S(1)}, bf16[80,80]{0,1:T(8,128)(2,1)S(1)}, u32[]{:S(2)}, u32[]{:S(2)}) collective-permute-start(bf16[80,80]{0,1:T(8,128)(2,1)S(1)} %copy.93), channel_id=1, source_target_pairs={{0,1},{1,0},{2,32},{3,64},{4,97},{5,96},{6,128},{7,160},{8,193},{9... | collective-permute-start | bytes 38408 | tf_op jit(solution)/shard_map/ppermute | solution.py:138
  166.7 5.9 %collective-permute-done.3 = bf16[80,80]{0,1:T(8,128)(2,1)S(1)} collective-permute-done((bf16[80,80]{0,1:T(8,128)(2,1)S(1)}, bf16[80,80]{0,1:T(8,128)(2,1)S(1)}, u32[]{:S(2)}, u32[]{:S(2)}) %collective-permute-start.3) | collective-permute-done | bytes 12832 | tf_op jit(solution)/shard_map/ppermute | solution.py:138
  172.6 1.9 collective-permute-start
  174.6 11.9 %collective-permute-start.9 = (bf16[80,80]{1,0:T(8,128)(2,1)S(1)}, bf16[80,80]{1,0:T(8,128)(2,1)S(1)}, u32[]{:S(2)}, u32[]{:S(2)}) collective-permute-start(bf16[80,80]{1,0:T(8,128)(2,1)S(1)} %get-tuple-element.64), channel_id=1, source_target_pairs={{1,32},{2,64},{3,65},{4,96},{5,128},{6,160},{7,161},{8,192},{9,224... | collective-permute-start | bytes 38408 | tf_op jit(solution)/shard_map/ppermute | solution.py:138
  186.6 1.9 collective-permute-start.8
  188.5 10.5 %collective-permute-start.5 = (bf16[80,80]{1,0:T(8,128)(2,1)S(1)}, bf16[80,80]{1,0:T(8,128)(2,1)S(1)}, u32[]{:S(2)}, u32[]{:S(2)}) collective-permute-start(bf16[80,80]{1,0:T(8,128)(2,1)S(1)} %get-tuple-element.62), channel_id=1, source_target_pairs={{0,1},{1,0},{2,32},{3,64},{4,97},{5,96},{6,128},{7,160},{8,193},{9... | collective-permute-start | bytes 38408 | tf_op jit(solution)/shard_map/ppermute | solution.py:138
  199.1 1.9 collective-permute-start.4
  201.0 1.6 fusion.2
  203.9 7.6 %collective-permute-done.4 = bf16[80,80]{1,0:T(8,128)(2,1)S(1)} collective-permute-done((bf16[80,80]{1,0:T(8,128)(2,1)S(1)}, bf16[80,80]{1,0:T(8,128)(2,1)S(1)}, u32[]{:S(2)}, u32[]{:S(2)}) %collective-permute-start.4) | collective-permute-done | bytes 12832 | tf_op jit(solution)/shard_map/ppermute | solution.py:138
  221.8 4.7 %collective-permute-start.15 = (f32[2]{0:T(128)S(1)}, f32[2]{0:T(128)S(1)}, u32[]{:S(2)}, u32[]{:S(2)}) collective-permute-start(f32[2]{0:T(128)S(1)} %pad_maximum_fusion), channel_id=1, source_target_pairs={{0,1},{1,0},{2,3},{3,2},{4,5},{5,4},{6,7},{7,6},{8,9},{9,8},{10,11... | collective-permute-start | bytes 32 | tf_op jit(solution)/shard_map/ppermute | solution.py:155
  227.6 1.9 collective-permute-start.1
  229.5 28.5 %collective-permute-start.2 = (bf16[640,240]{1,0:T(8,128)(2,1)S(1)}, bf16[640,240]{1,0:T(8,128)(2,1)S(1)}, u32[]{:S(2)}, u32[]{:S(2)}) collective-permute-start(bf16[640,240]{1,0:T(8,128)(2,1)S(1)} %maximum_select_fusion.1), channel_id=1, source_target_pairs={{0,704},{64,0},{128,64},{192,128},{256,192},{320,256},{384,320},{4... | collective-permute-start | bytes 921608 | tf_op jit(solution)/shard_map/ppermute | solution.py:195
  258.8 2.3 broadcast_in_dim.57
  261.9 2.1 collective-permute-done.1
  265.2 1.9 collective-permute-start.18
  267.1 18.3 %collective-permute-start.19 = (f32[2]{0:T(128)S(1)}, f32[2]{0:T(128)S(1)}, u32[]{:S(2)}, u32[]{:S(2)}) collective-permute-start(f32[2]{0:T(128)S(1)} %fusion.16), channel_id=1, source_target_pairs={{0,4},{2,6},{4,0},{6,2},{1,5},{3,7},{5,1},{7,3},{8,12},{10,14},{12... | collective-permute-start | bytes 32 | tf_op jit(solution)/shard_map/ppermute | solution.py:155
  285.5 2.4 collective-permute-start.20
  287.8 1.9 collective-permute-start.16
  289.8 5.6 %collective-permute-start.17 = (bf16[640,240]{1,0:T(8,128)(2,1)S(1)}, bf16[640,240]{1,0:T(8,128)(2,1)S(1)}, u32[]{:S(2)}, u32[]{:S(2)}) collective-permute-start(bf16[640,240]{1,0:T(8,128)(2,1)S(1)} %collective-permute-done.2), channel_id=1, source_target_pairs={{0,704},{64,0},{128,64},{192,128},{256,192},{320,256},{384,320},{4... | collective-permute-start | bytes 921608 | tf_op jit(solution)/shard_map/ppermute | solution.py:195
  296.9 3.1 collective-permute-done.16
  301.2 1.9 collective-permute-start.23
  303.1 1.9 collective-permute-start.24
  305.0 3.9 collective-permute-start.25
  309.0 2.0 collective-permute-start.21
  310.9 5.6 %collective-permute-start.22 = (bf16[640,240]{1,0:T(8,128)(2,1)S(1)}, bf16[640,240]{1,0:T(8,128)(2,1)S(1)}, u32[]{:S(2)}, u32[]{:S(2)}) collective-permute-start(bf16[640,240]{1,0:T(8,128)(2,1)S(1)} %collective-permute-done.17), channel_id=1, source_target_pairs={{0,704},{64,0},{128,64},{192,128},{256,192},{320,256},{384,320},{4... | collective-permute-start | bytes 921608 | tf_op jit(solution)/shard_map/ppermute | solution.py:195
  321.1 8.7 %collective-permute-start.28 = (f32[2]{0:T(128)S(1)}, f32[2]{0:T(128)S(1)}, u32[]{:S(2)}, u32[]{:S(2)}) collective-permute-start(f32[2]{0:T(128)S(1)} %fusion.22), channel_id=1, source_target_pairs={{0,32},{32,0},{1,33},{33,1},{2,34},{34,2},{3,35},{35,3},{4,36},{36... | collective-permute-start | bytes 32 | tf_op jit(solution)/shard_map/ppermute | solution.py:155
  329.8 3.6 collective-permute-start.26
  333.4 3.4 collective-permute-start.27
  340.0 2.4 collective-permute-done.27
  342.4 4.7 %collective-permute-start.31 = (f32[2]{0:T(128)S(1)}, f32[2]{0:T(128)S(1)}, u32[]{:S(2)}, u32[]{:S(2)}) collective-permute-start(f32[2]{0:T(128)S(1)} %fusion.23), channel_id=1, source_target_pairs={{0,192},{64,0},{128,64},{192,128},{256,448},{320,256},{384,320},{4... | collective-permute-start | bytes 32 | tf_op jit(solution)/shard_map/ppermute | solution.py:155
  347.1 2.1 collective-permute-start.32
  349.2 3.1 collective-permute-start.33
  352.3 4.0 %collective-permute-start.29 = (bf16[640,240]{1,0:T(8,128)(2,1)S(1)}, bf16[640,240]{1,0:T(8,128)(2,1)S(1)}, u32[]{:S(2)}, u32[]{:S(2)}) collective-permute-start(bf16[640,240]{1,0:T(8,128)(2,1)S(1)} %collective-permute-done.26), channel_id=1, source_target_pairs={{0,64},{64,128},{128,192},{192,256},{256,320},{320,384},{384,448},... | collective-permute-start | bytes 921608 | tf_op jit(solution)/shard_map/ppermute | solution.py:193
  356.4 3.0 collective-permute-start.30
  362.5 2.8 collective-permute-done.30
  365.3 5.0 %collective-permute-start.35 = (f32[2]{0:T(128)S(1)}, f32[2]{0:T(128)S(1)}, u32[]{:S(2)}, u32[]{:S(2)}) collective-permute-start(f32[2]{0:T(128)S(1)} %fusion.26), channel_id=1, source_target_pairs={{0,512},{64,576},{128,640},{192,704},{256,0},{320,64},{384,128},{4... | collective-permute-start | bytes 32 | tf_op jit(solution)/shard_map/ppermute | solution.py:155
  370.4 4.7 %collective-permute-start.36 = (f32[2]{0:T(128)S(1)}, f32[2]{0:T(128)S(1)}, u32[]{:S(2)}, u32[]{:S(2)}) collective-permute-start(f32[2]{0:T(128)S(1)} %fusion.26), channel_id=1, source_target_pairs={{0,256},{64,320},{128,384},{192,448},{256,512},{320,576},{384,640}... | collective-permute-start | bytes 32 | tf_op jit(solution)/shard_map/ppermute | solution.py:155
  375.1 1.9 collective-permute-start.34
  379.7 5.5 %collective-permute-done.34 = bf16[640,240]{1,0:T(8,128)(2,1)S(1)} collective-permute-done((bf16[640,240]{1,0:T(8,128)(2,1)S(1)}, bf16[640,240]{1,0:T(8,128)(2,1)S(1)}, u32[]{:S(2)}, u32[]{:S(2)}) %collective-permute-start.34) | collective-permute-done | bytes 307232 | tf_op jit(solution)/shard_map/ppermute | solution.py:193
  386.5 6.4 %shard_map.581 = bf16[320,240]{1,0:T(8,128)(2,1)} custom-call(bf16[32,320,240]{2,1,0:T(8,128)(2,1)} %bitcast.129, bf16[7680,240]{1,0:T(8,128)(2,1)} %bitcast.78.right_ref, s32[320,240]{1,0:T(8,128)} %fusion.29.keep_ref), custom_call_target="tpu_custom_call" | custom-call | flops 1179648000 | bytes 9062400 | tf_op jit(solution)/shard_map/pallas_call | solution.py:53
  (137 shorter events, 96.7 us)
Async XLA Ops:
  7.2 379.4 %all-gather.3.cloned.1.call-start = ((), (), s32[]{:S(2)}) async-start(), calls=%async_computation | async-start | bytes 5406720 | tf_op jit(solution)/shard_map/all_gather | solution.py:215
  28.3 232.8 %copy-start = (bf16[320,240]{1,0:T(8,128)(2,1)S(1)}, bf16[320,240]{1,0:T(8,128)(2,1)}, u32[]{:S(2)}) copy-start(bf16[320,240]{1,0:T(8,128)(2,1)} %get-tuple-element.49) | copy-start | bytes 460804
  39.1 135.5 %collective-permute-start.14 = (bf16[80,80]{0,1:T(8,128)(2,1)S(1)}, bf16[80,80]{0,1:T(8,128)(2,1)S(1)}, u32[]{:S(2)}, u32[]{:S(2)}) collective-permute-start(bf16[80,80]{0,1:T(8,128)(2,1)S(1)} %copy.104), channel_id=1, source_target_pairs={{1,32},{2,33},{3,64},{4,96},{5,128},{6,129},{7,160},{8,192},{9,224... | collective-permute-start | bytes 38408 | tf_op jit(solution)/shard_map/ppermute | solution.py:138
  86.6 100.0 %collective-permute-start.11 = (bf16[80,80]{0,1:T(8,128)(2,1)S(1)}, bf16[80,80]{0,1:T(8,128)(2,1)S(1)}, u32[]{:S(2)}, u32[]{:S(2)}) collective-permute-start(bf16[80,80]{0,1:T(8,128)(2,1)S(1)} %copy.101), channel_id=1, source_target_pairs={{1,33},{2,32},{3,64},{4,96},{5,129},{6,128},{7,160},{8,192},{9,225... | collective-permute-start | bytes 38408 | tf_op jit(solution)/shard_map/ppermute | solution.py:138
  89.1 58.4 %collective-permute-start.7 = (bf16[80,80]{0,1:T(8,128)(2,1)S(1)}, bf16[80,80]{0,1:T(8,128)(2,1)S(1)}, u32[]{:S(2)}, u32[]{:S(2)}) collective-permute-start(bf16[80,80]{0,1:T(8,128)(2,1)S(1)} %copy.97), channel_id=1, source_target_pairs={{1,32},{2,64},{3,65},{4,96},{5,128},{6,160},{7,161},{8,192},{9,224... | collective-permute-start | bytes 38408 | tf_op jit(solution)/shard_map/ppermute | solution.py:138
  97.3 54.4 %collective-permute-start.10 = (bf16[80,80]{0,1:T(8,128)(2,1)S(1)}, bf16[80,80]{0,1:T(8,128)(2,1)S(1)}, u32[]{:S(2)}, u32[]{:S(2)}) collective-permute-start(bf16[80,80]{0,1:T(8,128)(2,1)S(1)} %copy.100), channel_id=1, source_target_pairs={{1,33},{2,32},{3,64},{4,96},{5,129},{6,128},{7,160},{8,192},{9,225... | collective-permute-start | bytes 38408 | tf_op jit(solution)/shard_map/ppermute | solution.py:138
  102.4 55.4 %collective-permute-start.6 = (bf16[80,80]{0,1:T(8,128)(2,1)S(1)}, bf16[80,80]{0,1:T(8,128)(2,1)S(1)}, u32[]{:S(2)}, u32[]{:S(2)}) collective-permute-start(bf16[80,80]{0,1:T(8,128)(2,1)S(1)} %copy.96), channel_id=1, source_target_pairs={{1,32},{2,64},{3,65},{4,96},{5,128},{6,160},{7,161},{8,192},{9,224... | collective-permute-start | bytes 38408 | tf_op jit(solution)/shard_map/ppermute | solution.py:138
  147.5 41.0 %collective-permute-start.12 = (bf16[80,80]{0,1:T(8,128)(2,1)S(1)}, bf16[80,80]{0,1:T(8,128)(2,1)S(1)}, u32[]{:S(2)}, u32[]{:S(2)}) collective-permute-start(bf16[80,80]{0,1:T(8,128)(2,1)S(1)} %copy.102), channel_id=1, source_target_pairs={{1,32},{2,33},{3,64},{4,96},{5,128},{6,129},{7,160},{8,192},{9,224... | collective-permute-start | bytes 38408 | tf_op jit(solution)/shard_map/ppermute | solution.py:138
  151.7 47.4 %collective-permute-start.13 = (bf16[80,80]{0,1:T(8,128)(2,1)S(1)}, bf16[80,80]{0,1:T(8,128)(2,1)S(1)}, u32[]{:S(2)}, u32[]{:S(2)}) collective-permute-start(bf16[80,80]{0,1:T(8,128)(2,1)S(1)} %copy.103), channel_id=1, source_target_pairs={{1,32},{2,65},{3,64},{4,96},{5,128},{6,161},{7,160},{8,192},{9,224... | collective-permute-start | bytes 38408 | tf_op jit(solution)/shard_map/ppermute | solution.py:138
  157.8 14.8 %collective-permute-start.3 = (bf16[80,80]{0,1:T(8,128)(2,1)S(1)}, bf16[80,80]{0,1:T(8,128)(2,1)S(1)}, u32[]{:S(2)}, u32[]{:S(2)}) collective-permute-start(bf16[80,80]{0,1:T(8,128)(2,1)S(1)} %copy.93), channel_id=1, source_target_pairs={{0,1},{1,0},{2,32},{3,64},{4,97},{5,96},{6,128},{7,160},{8,193},{9... | collective-permute-start | bytes 38408 | tf_op jit(solution)/shard_map/ppermute | solution.py:138
  172.6 53.9 %collective-permute-start = (bf16[320,240]{1,0:T(8,128)(2,1)}, bf16[320,240]{1,0:T(8,128)(2,1)S(1)}, u32[]{:S(2)}, u32[]{:S(2)}) collective-permute-start(bf16[320,240]{1,0:T(8,128)(2,1)} %get-tuple-element.49), channel_id=1, source_target_pairs={{0,32},{32,0},{1,33},{33,1},{2,34},{34,2},{3,35},{35,3},{4,36},{36... | collective-permute-start | bytes 460808 | tf_op jit(solution)/shard_map/ppermute | solution.py:179
  174.6 37.5 %collective-permute-start.9 = (bf16[80,80]{1,0:T(8,128)(2,1)S(1)}, bf16[80,80]{1,0:T(8,128)(2,1)S(1)}, u32[]{:S(2)}, u32[]{:S(2)}) collective-permute-start(bf16[80,80]{1,0:T(8,128)(2,1)S(1)} %get-tuple-element.64), channel_id=1, source_target_pairs={{1,32},{2,64},{3,65},{4,96},{5,128},{6,160},{7,161},{8,192},{9,224... | collective-permute-start | bytes 38408 | tf_op jit(solution)/shard_map/ppermute | solution.py:138
  186.6 26.2 %collective-permute-start.8 = (bf16[80,80]{1,0:T(8,128)(2,1)S(1)}, bf16[80,80]{1,0:T(8,128)(2,1)S(1)}, u32[]{:S(2)}, u32[]{:S(2)}) collective-permute-start(bf16[80,80]{1,0:T(8,128)(2,1)S(1)} %get-tuple-element.56), channel_id=1, source_target_pairs={{2,32},{3,64},{4,96},{5,97},{6,128},{7,160},{8,192},{9,193},{10,22... | collective-permute-start | bytes 38408 | tf_op jit(solution)/shard_map/ppermute | solution.py:138
  188.5 14.7 %collective-permute-start.5 = (bf16[80,80]{1,0:T(8,128)(2,1)S(1)}, bf16[80,80]{1,0:T(8,128)(2,1)S(1)}, u32[]{:S(2)}, u32[]{:S(2)}) collective-permute-start(bf16[80,80]{1,0:T(8,128)(2,1)S(1)} %get-tuple-element.62), channel_id=1, source_target_pairs={{0,1},{1,0},{2,32},{3,64},{4,97},{5,96},{6,128},{7,160},{8,193},{9... | collective-permute-start | bytes 38408 | tf_op jit(solution)/shard_map/ppermute | solution.py:138
  199.1 12.4 %collective-permute-start.4 = (bf16[80,80]{1,0:T(8,128)(2,1)S(1)}, bf16[80,80]{1,0:T(8,128)(2,1)S(1)}, u32[]{:S(2)}, u32[]{:S(2)}) collective-permute-start(bf16[80,80]{1,0:T(8,128)(2,1)S(1)} %get-tuple-element.63), channel_id=1, source_target_pairs={{0,1},{1,0},{2,32},{3,64},{4,97},{5,96},{6,128},{7,160},{8,193},{9... | collective-permute-start | bytes 38408 | tf_op jit(solution)/shard_map/ppermute | solution.py:138
  221.8 36.3 %collective-permute-start.15 = (f32[2]{0:T(128)S(1)}, f32[2]{0:T(128)S(1)}, u32[]{:S(2)}, u32[]{:S(2)}) collective-permute-start(f32[2]{0:T(128)S(1)} %pad_maximum_fusion), channel_id=1, source_target_pairs={{0,1},{1,0},{2,3},{3,2},{4,5},{5,4},{6,7},{7,6},{8,9},{9,8},{10,11... | collective-permute-start | bytes 32 | tf_op jit(solution)/shard_map/ppermute | solution.py:155
  227.6 36.4 %collective-permute-start.1 = (bf16[640,240]{1,0:T(8,128)(2,1)S(1)}, bf16[640,240]{1,0:T(8,128)(2,1)S(1)}, u32[]{:S(2)}, u32[]{:S(2)}) collective-permute-start(bf16[640,240]{1,0:T(8,128)(2,1)S(1)} %maximum_select_fusion.1), channel_id=1, source_target_pairs={{0,64},{64,128},{128,192},{192,256},{256,320},{320,384},{384,448},... | collective-permute-start | bytes 921608 | tf_op jit(solution)/shard_map/ppermute | solution.py:193
  229.5 35.7 %collective-permute-start.2 = (bf16[640,240]{1,0:T(8,128)(2,1)S(1)}, bf16[640,240]{1,0:T(8,128)(2,1)S(1)}, u32[]{:S(2)}, u32[]{:S(2)}) collective-permute-start(bf16[640,240]{1,0:T(8,128)(2,1)S(1)} %maximum_select_fusion.1), channel_id=1, source_target_pairs={{0,704},{64,0},{128,64},{192,128},{256,192},{320,256},{384,320},{4... | collective-permute-start | bytes 921608 | tf_op jit(solution)/shard_map/ppermute | solution.py:195
  265.2 31.7 %collective-permute-start.18 = (f32[2]{0:T(128)S(1)}, f32[2]{0:T(128)S(1)}, u32[]{:S(2)}, u32[]{:S(2)}) collective-permute-start(f32[2]{0:T(128)S(1)} %fusion.16), channel_id=1, source_target_pairs={{0,6},{2,0},{4,2},{6,4},{1,7},{3,1},{5,3},{7,5},{8,14},{10,8},{12,... | collective-permute-start | bytes 32 | tf_op jit(solution)/shard_map/ppermute | solution.py:155
  267.1 29.8 %collective-permute-start.19 = (f32[2]{0:T(128)S(1)}, f32[2]{0:T(128)S(1)}, u32[]{:S(2)}, u32[]{:S(2)}) collective-permute-start(f32[2]{0:T(128)S(1)} %fusion.16), channel_id=1, source_target_pairs={{0,4},{2,6},{4,0},{6,2},{1,5},{3,7},{5,1},{7,3},{8,12},{10,14},{12... | collective-permute-start | bytes 32 | tf_op jit(solution)/shard_map/ppermute | solution.py:155
  285.5 11.5 %collective-permute-start.20 = (f32[2]{0:T(128)S(1)}, f32[2]{0:T(128)S(1)}, u32[]{:S(2)}, u32[]{:S(2)}) collective-permute-start(f32[2]{0:T(128)S(1)} %fusion.16), channel_id=1, source_target_pairs={{0,2},{2,4},{4,6},{6,0},{1,3},{3,5},{5,7},{7,1},{8,10},{10,12},{12... | collective-permute-start | bytes 32 | tf_op jit(solution)/shard_map/ppermute | solution.py:155
  287.8 12.2 %collective-permute-start.16 = (bf16[640,240]{1,0:T(8,128)(2,1)S(1)}, bf16[640,240]{1,0:T(8,128)(2,1)S(1)}, u32[]{:S(2)}, u32[]{:S(2)}) collective-permute-start(bf16[640,240]{1,0:T(8,128)(2,1)S(1)} %collective-permute-done.1), channel_id=1, source_target_pairs={{0,64},{64,128},{128,192},{192,256},{256,320},{320,384},{384,448},... | collective-permute-start | bytes 921608 | tf_op jit(solution)/shard_map/ppermute | solution.py:193
  289.8 11.4 %collective-permute-start.17 = (bf16[640,240]{1,0:T(8,128)(2,1)S(1)}, bf16[640,240]{1,0:T(8,128)(2,1)S(1)}, u32[]{:S(2)}, u32[]{:S(2)}) collective-permute-start(bf16[640,240]{1,0:T(8,128)(2,1)S(1)} %collective-permute-done.2), channel_id=1, source_target_pairs={{0,704},{64,0},{128,64},{192,128},{256,192},{320,256},{384,320},{4... | collective-permute-start | bytes 921608 | tf_op jit(solution)/shard_map/ppermute | solution.py:195
  301.2 16.9 %collective-permute-start.23 = (f32[2]{0:T(128)S(1)}, f32[2]{0:T(128)S(1)}, u32[]{:S(2)}, u32[]{:S(2)}) collective-permute-start(f32[2]{0:T(128)S(1)} %fusion.19), channel_id=1, source_target_pairs={{0,24},{8,0},{16,8},{24,16},{1,25},{9,1},{17,9},{25,17},{2,26},{10... | collective-permute-start | bytes 32 | tf_op jit(solution)/shard_map/ppermute | solution.py:155
  303.1 14.9 %collective-permute-start.24 = (f32[2]{0:T(128)S(1)}, f32[2]{0:T(128)S(1)}, u32[]{:S(2)}, u32[]{:S(2)}) collective-permute-start(f32[2]{0:T(128)S(1)} %fusion.19), channel_id=1, source_target_pairs={{0,16},{8,24},{16,0},{24,8},{1,17},{9,25},{17,1},{25,9},{2,18},{10... | collective-permute-start | bytes 32 | tf_op jit(solution)/shard_map/ppermute | solution.py:155
  305.0 13.0 %collective-permute-start.25 = (f32[2]{0:T(128)S(1)}, f32[2]{0:T(128)S(1)}, u32[]{:S(2)}, u32[]{:S(2)}) collective-permute-start(f32[2]{0:T(128)S(1)} %fusion.19), channel_id=1, source_target_pairs={{0,8},{8,16},{16,24},{24,0},{1,9},{9,17},{17,25},{25,1},{2,10},{10... | collective-permute-start | bytes 32 | tf_op jit(solution)/shard_map/ppermute | solution.py:155
  309.0 10.7 %collective-permute-start.21 = (bf16[640,240]{1,0:T(8,128)(2,1)S(1)}, bf16[640,240]{1,0:T(8,128)(2,1)S(1)}, u32[]{:S(2)}, u32[]{:S(2)}) collective-permute-start(bf16[640,240]{1,0:T(8,128)(2,1)S(1)} %collective-permute-done.16), channel_id=1, source_target_pairs={{0,64},{64,128},{128,192},{192,256},{256,320},{320,384},{384,448},... | collective-permute-start | bytes 921608 | tf_op jit(solution)/shard_map/ppermute | solution.py:193
  310.9 10.1 %collective-permute-start.22 = (bf16[640,240]{1,0:T(8,128)(2,1)S(1)}, bf16[640,240]{1,0:T(8,128)(2,1)S(1)}, u32[]{:S(2)}, u32[]{:S(2)}) collective-permute-start(bf16[640,240]{1,0:T(8,128)(2,1)S(1)} %collective-permute-done.17), channel_id=1, source_target_pairs={{0,704},{64,0},{128,64},{192,128},{256,192},{320,256},{384,320},{4... | collective-permute-start | bytes 921608 | tf_op jit(solution)/shard_map/ppermute | solution.py:195
  321.1 17.3 %collective-permute-start.28 = (f32[2]{0:T(128)S(1)}, f32[2]{0:T(128)S(1)}, u32[]{:S(2)}, u32[]{:S(2)}) collective-permute-start(f32[2]{0:T(128)S(1)} %fusion.22), channel_id=1, source_target_pairs={{0,32},{32,0},{1,33},{33,1},{2,34},{34,2},{3,35},{35,3},{4,36},{36... | collective-permute-start | bytes 32 | tf_op jit(solution)/shard_map/ppermute | solution.py:155
  329.8 10.2 %collective-permute-start.26 = (bf16[640,240]{1,0:T(8,128)(2,1)S(1)}, bf16[640,240]{1,0:T(8,128)(2,1)S(1)}, u32[]{:S(2)}, u32[]{:S(2)}) collective-permute-start(bf16[640,240]{1,0:T(8,128)(2,1)S(1)} %collective-permute-done.21), channel_id=1, source_target_pairs={{0,64},{64,128},{128,192},{192,256},{256,320},{320,384},{384,448},... | collective-permute-start | bytes 921608 | tf_op jit(solution)/shard_map/ppermute | solution.py:193
  333.4 9.0 %collective-permute-start.27 = (bf16[640,240]{1,0:T(8,128)(2,1)S(1)}, bf16[640,240]{1,0:T(8,128)(2,1)S(1)}, u32[]{:S(2)}, u32[]{:S(2)}) collective-permute-start(bf16[640,240]{1,0:T(8,128)(2,1)S(1)} %collective-permute-done.22), channel_id=1, source_target_pairs={{0,704},{64,0},{128,64},{192,128},{256,192},{320,256},{384,320},{4... | collective-permute-start | bytes 921608 | tf_op jit(solution)/shard_map/ppermute | solution.py:195
  342.4 18.5 %collective-permute-start.31 = (f32[2]{0:T(128)S(1)}, f32[2]{0:T(128)S(1)}, u32[]{:S(2)}, u32[]{:S(2)}) collective-permute-start(f32[2]{0:T(128)S(1)} %fusion.23), channel_id=1, source_target_pairs={{0,192},{64,0},{128,64},{192,128},{256,448},{320,256},{384,320},{4... | collective-permute-start | bytes 32 | tf_op jit(solution)/shard_map/ppermute | solution.py:155
  347.1 13.8 %collective-permute-start.32 = (f32[2]{0:T(128)S(1)}, f32[2]{0:T(128)S(1)}, u32[]{:S(2)}, u32[]{:S(2)}) collective-permute-start(f32[2]{0:T(128)S(1)} %fusion.23), channel_id=1, source_target_pairs={{0,128},{64,192},{128,0},{192,64},{256,384},{320,448},{384,256},{4... | collective-permute-start | bytes 32 | tf_op jit(solution)/shard_map/ppermute | solution.py:155
  349.2 11.7 %collective-permute-start.33 = (f32[2]{0:T(128)S(1)}, f32[2]{0:T(128)S(1)}, u32[]{:S(2)}, u32[]{:S(2)}) collective-permute-start(f32[2]{0:T(128)S(1)} %fusion.23), channel_id=1, source_target_pairs={{0,64},{64,128},{128,192},{192,0},{256,320},{320,384},{384,448},{4... | collective-permute-start | bytes 32 | tf_op jit(solution)/shard_map/ppermute | solution.py:155
  352.3 10.2 %collective-permute-start.29 = (bf16[640,240]{1,0:T(8,128)(2,1)S(1)}, bf16[640,240]{1,0:T(8,128)(2,1)S(1)}, u32[]{:S(2)}, u32[]{:S(2)}) collective-permute-start(bf16[640,240]{1,0:T(8,128)(2,1)S(1)} %collective-permute-done.26), channel_id=1, source_target_pairs={{0,64},{64,128},{128,192},{192,256},{256,320},{320,384},{384,448},... | collective-permute-start | bytes 921608 | tf_op jit(solution)/shard_map/ppermute | solution.py:193
  356.4 9.0 %collective-permute-start.30 = (bf16[640,240]{1,0:T(8,128)(2,1)S(1)}, bf16[640,240]{1,0:T(8,128)(2,1)S(1)}, u32[]{:S(2)}, u32[]{:S(2)}) collective-permute-start(bf16[640,240]{1,0:T(8,128)(2,1)S(1)} %collective-permute-done.27), channel_id=1, source_target_pairs={{0,704},{64,0},{128,64},{192,128},{256,192},{320,256},{384,320},{4... | collective-permute-start | bytes 921608 | tf_op jit(solution)/shard_map/ppermute | solution.py:195
  365.3 13.2 %collective-permute-start.35 = (f32[2]{0:T(128)S(1)}, f32[2]{0:T(128)S(1)}, u32[]{:S(2)}, u32[]{:S(2)}) collective-permute-start(f32[2]{0:T(128)S(1)} %fusion.26), channel_id=1, source_target_pairs={{0,512},{64,576},{128,640},{192,704},{256,0},{320,64},{384,128},{4... | collective-permute-start | bytes 32 | tf_op jit(solution)/shard_map/ppermute | solution.py:155
  370.4 9.3 %collective-permute-start.36 = (f32[2]{0:T(128)S(1)}, f32[2]{0:T(128)S(1)}, u32[]{:S(2)}, u32[]{:S(2)}) collective-permute-start(f32[2]{0:T(128)S(1)} %fusion.26), channel_id=1, source_target_pairs={{0,256},{64,320},{128,384},{192,448},{256,512},{320,576},{384,640}... | collective-permute-start | bytes 32 | tf_op jit(solution)/shard_map/ppermute | solution.py:155
  375.1 10.2 %collective-permute-start.34 = (bf16[640,240]{1,0:T(8,128)(2,1)S(1)}, bf16[640,240]{1,0:T(8,128)(2,1)S(1)}, u32[]{:S(2)}, u32[]{:S(2)}) collective-permute-start(bf16[640,240]{1,0:T(8,128)(2,1)S(1)} %collective-permute-done.29), channel_id=1, source_target_pairs={{0,64},{64,128},{128,192},{192,256},{256,320},{320,384},{384,448},... | collective-permute-start | bytes 921608 | tf_op jit(solution)/shard_map/ppermute | solution.py:193
Sparse Core Ops, SparseCore 0:
  11.0 77.0 all-gather.2

commit v6 on v4

--- a/solution.py
+++ b/solution.py
@@ -33,25 +33,33 @@
 def panel_kernel(
     place_ref, left_ref, right_ref, keep_ref, square_ref, trace_ref, total_ref
 ):
-    pieces, _, depth = left_ref.shape
-    total_ref[...] = jnp.dot(
-        left_ref[0], right_ref[0:depth, :], preferred_element_type=jnp.float32
-    )
-    for piece in range(1, pieces):
-        total_ref[...] += jnp.dot(
-            left_ref[piece],
-            right_ref[piece * depth:(piece + 1) * depth, :],
-            preferred_element_type=jnp.float32,
+    pieces, tile_rows, depth = left_ref.shape
+    chunk = tile_rows // 2
+    first = jnp.zeros((), jnp.float32)
+    second = jnp.zeros((), jnp.float32)
+    for start in range(0, tile_rows, chunk):
+        rows = slice(start, start + chunk)
+        total = jnp.dot(
+            left_ref[0, rows, :], right_ref[0:depth, :], preferred_element_type=jnp.float32
         )
-    total = total_ref[...]
-    square_ref[...] = jnp.where(keep_ref[...] != 0, total, 0.0).astype(square_ref.dtype)
-    rows = lax.broadcasted_iota(jnp.int32, total.shape, 0)
-    cols = lax.broadcasted_iota(jnp.int32, total.shape, 1)
-    on_diagonal = cols - rows == place_ref[0]
-    own = left_ref[place_ref[1]].astype(jnp.float32)
+        for piece in range(1, pieces):
+            total = total + jnp.dot(
+                left_ref[piece, rows, :],
+                right_ref[piece * depth:(piece + 1) * depth, :],
+                preferred_element_type=jnp.float32,
+            )
+        square_ref[rows, :] = jnp.where(keep_ref[rows, :] != 0, total, 0.0).astype(
+            square_ref.dtype
+        )
+        local_rows = lax.broadcasted_iota(jnp.int32, total.shape, 0) + start
+        cols = lax.broadcasted_iota(jnp.int32, total.shape, 1)
+        on_diagonal = cols - local_rows == place_ref[0]
+        own = left_ref[place_ref[1], rows, :].astype(jnp.float32)
+        first = first + jnp.sum(jnp.where(on_diagonal, own, 0.0))
+        second = second + jnp.sum(jnp.where(on_diagonal, total, 0.0))
     scale = 1.0 / place_ref[2].astype(jnp.float32)
-    trace_ref[0] = jnp.sum(jnp.where(on_diagonal, own, 0.0)) * scale
-    trace_ref[1] = jnp.sum(jnp.where(on_diagonal, total, 0.0)) * scale
+    trace_ref[0] = first * scale
+    trace_ref[1] = second * scale
 
 
 def panel_product(place, left, right, keep):

time: 172 us -> 172 us (level)
  no operation moved by 1% of the time
where the time goes in v6:
time: 172 us; the launch traced here: 171 us
  blocking collectives  57.5 us (33%)
  starting transfers between devices  49.5 us (29%)
  waiting for transfers between devices  25.5 us (15%)
  between operations  14.5 us (8%)
  local copies, waits for them, and re-layouts  10.9 us (6%)
  other arithmetic  7.54 us (4%)
  Pallas kernels  5.91 us (3%)
    psum x5, blocking collectives, on_device(): traces = lax.psum(traces, axis)  57.5 us
    ppermute x5, starting transfers between devices, column_slab(): behind = lax.ppermute(behind, 'row_0', backward)  32.8 us
    ppermute x6, waiting for transfers between devices, column_slab(): ahead = lax.ppermute(ahead, 'row_0', forward)  15.6 us
    ppermute x6, starting transfers between devices, column_slab(): ahead = lax.ppermute(ahead, 'row_0', forward)  13.8 us
    ppermute x1, waiting for transfers between devices, column_slab(): other = lax.ppermute(masked, 'row_1', [(0, 1), (1, 0)])  9.83 us
    pallas_call x1, Pallas kernels, panel_product(): pl.pallas_call(panel_kernel, out_shape=(jax.ShapeDtypeStruct((tile_rows,...  5.91 us
    dynamic_update_slice x6, local copies, waits for them, and re-layouts, column_slab(): lax.dynamic_update_index_in_dim(slab, ahead, (here - step) % depth, 0)  4.62 us
    dynamic_update_slice x5, local copies, waits for them, and re-layouts, column_slab(): lax.dynamic_update_index_in_dim(slab, behind, (here + step) % depth, 0)  3.74 us
  transfers between devices with their start and end apart: 13, of which 7 were waited for; matrix products, arithmetic and copies ran while one was open for 9% of the time, Pallas kernels for 0%

profile of v6, /device:TPU:40, one launch (start us, length us, event | category | flops | bytes accessed | tf_op | source)
XLA Modules:
  0.0 171.3 jit_solution(3234501395906670134)
XLA Ops:
  7.2 0.0 all-gather.3.cloned.1.call-start
  7.3 0.8 fusion.1
  8.1 0.1 copy.4
  8.2 0.1 broadcast_in_dim.52
  8.3 0.1 reshape.113
  8.4 1.9 %broadcast_select_fusion = bf16[320,240]{1,0:T(8,128)(2,1)} fusion(bf16[320,240]{1,0:T(8,128)(2,1)} %param.2, pred[320]{0:T(512)(128)(4,1)S(1)} %get-tuple-element.7, pred[240]{0:T(512)(128)(4,1)S(1)} %get-tuple-element.11, pred[320]{0:T(512)(128)(4,1)S(1)} %get-tuple-element.8, pred[240]{0:T(512)(128)(4,1)S(1)} %get-tuple-element.12, ...), kind=kLoop, calls=%fused_computation.15 | loop fusion | flops 768000 | bytes 310000 | tf_op jit(solution)/shard_map/jit(_where)/select_n | solution.py:119
  10.3 2.9 %collective-permute-start = (bf16[320,240]{1,0:T(8,128)(2,1)}, bf16[320,240]{1,0:T(8,128)(2,1)S(1)}, u32[]{:S(2)}, u32[]{:S(2)}) collective-permute-start(bf16[320,240]{1,0:T(8,128)(2,1)} %broadcast_select_fusion), channel_id=1, source_target_pairs={{0,32},{32,0},{1,33},{33,1},{2,34},{34,2},{3,35},{35,3},{4,36},{36... | collective-permute-start | bytes 460808 | tf_op jit(solution)/shard_map/ppermute | solution.py:90
  13.2 1.2 fusion.4
  14.7 0.6 pad_add_fusion.place_ref
  15.3 9.8 %collective-permute-done = bf16[320,240]{1,0:T(8,128)(2,1)S(1)} collective-permute-done((bf16[320,240]{1,0:T(8,128)(2,1)}, bf16[320,240]{1,0:T(8,128)(2,1)S(1)}, u32[]{:S(2)}, u32[]{:S(2)}) %collective-permute-start) | collective-permute-done | bytes 153632 | tf_op jit(solution)/shard_map/ppermute | solution.py:90
  25.1 1.1 maximum_select_fusion.1
  26.2 4.3 %collective-permute-start.1 = (bf16[640,240]{1,0:T(8,128)(2,1)S(1)}, bf16[640,240]{1,0:T(8,128)(2,1)S(1)}, u32[]{:S(2)}, u32[]{:S(2)}) collective-permute-start(bf16[640,240]{1,0:T(8,128)(2,1)S(1)} %maximum_select_fusion.1), channel_id=1, source_target_pairs={{0,64},{64,128},{128,192},{192,256},{256,320},{320,384},{384,448},... | collective-permute-start | bytes 921608 | tf_op jit(solution)/shard_map/ppermute | solution.py:104
  30.5 12.2 %collective-permute-start.2 = (bf16[640,240]{1,0:T(8,128)(2,1)S(1)}, bf16[640,240]{1,0:T(8,128)(2,1)S(1)}, u32[]{:S(2)}, u32[]{:S(2)}) collective-permute-start(bf16[640,240]{1,0:T(8,128)(2,1)S(1)} %maximum_select_fusion.1), channel_id=1, source_target_pairs={{0,704},{64,0},{128,64},{192,128},{256,192},{320,256},{384,320},{4... | collective-permute-start | bytes 921608 | tf_op jit(solution)/shard_map/ppermute | solution.py:107
  42.7 1.0 fusion.3.keep_ref
  43.8 2.3 %broadcast_in_dim.54 = bf16[12,640,240]{2,1,0:T(8,128)(2,1)} broadcast(bf16[]{:T(256)} %constant.136.clone.1), dimensions={} | broadcast | bytes 3686402 | tf_op jit(solution)/shard_map/broadcast_in_dim | solution.py:97
  46.1 0.8 fusion
  46.9 1.1 collective-permute-done.1
  48.0 1.9 %collective-permute-start.3 = (bf16[640,240]{1,0:T(8,128)(2,1)S(1)}, bf16[640,240]{1,0:T(8,128)(2,1)S(1)}, u32[]{:S(2)}, u32[]{:S(2)}) collective-permute-start(bf16[640,240]{1,0:T(8,128)(2,1)S(1)} %collective-permute-done.1), channel_id=1, source_target_pairs={{0,64},{64,128},{128,192},{192,256},{256,320},{320,384},{384,448},... | collective-permute-start | bytes 921608 | tf_op jit(solution)/shard_map/ppermute | solution.py:104
  49.9 5.1 %collective-permute-start.4 = (bf16[640,240]{1,0:T(8,128)(2,1)S(1)}, bf16[640,240]{1,0:T(8,128)(2,1)S(1)}, u32[]{:S(2)}, u32[]{:S(2)}) collective-permute-start(bf16[640,240]{1,0:T(8,128)(2,1)S(1)} %collective-permute-done.2), channel_id=1, source_target_pairs={{0,704},{64,0},{128,64},{192,128},{256,192},{320,256},{384,320},{4... | collective-permute-start | bytes 921608 | tf_op jit(solution)/shard_map/ppermute | solution.py:107
  55.0 0.8 bitcast_dynamic-update-slice_fusion.10
  55.8 0.7 bitcast_dynamic-update-slice_fusion.9
  56.6 2.8 %collective-permute-done.3 = bf16[640,240]{1,0:T(8,128)(2,1)S(1)} collective-permute-done((bf16[640,240]{1,0:T(8,128)(2,1)S(1)}, bf16[640,240]{1,0:T(8,128)(2,1)S(1)}, u32[]{:S(2)}, u32[]{:S(2)}) %collective-permute-start.3) | collective-permute-done | bytes 307232 | tf_op jit(solution)/shard_map/ppermute | solution.py:104
  59.3 1.9 %collective-permute-start.5 = (bf16[640,240]{1,0:T(8,128)(2,1)S(1)}, bf16[640,240]{1,0:T(8,128)(2,1)S(1)}, u32[]{:S(2)}, u32[]{:S(2)}) collective-permute-start(bf16[640,240]{1,0:T(8,128)(2,1)S(1)} %collective-permute-done.3), channel_id=1, source_target_pairs={{0,64},{64,128},{128,192},{192,256},{256,320},{320,384},{384,448},... | collective-permute-start | bytes 921608 | tf_op jit(solution)/shard_map/ppermute | solution.py:104
  61.3 5.1 %collective-permute-start.6 = (bf16[640,240]{1,0:T(8,128)(2,1)S(1)}, bf16[640,240]{1,0:T(8,128)(2,1)S(1)}, u32[]{:S(2)}, u32[]{:S(2)}) collective-permute-start(bf16[640,240]{1,0:T(8,128)(2,1)S(1)} %collective-permute-done.4), channel_id=1, source_target_pairs={{0,704},{64,0},{128,64},{192,128},{256,192},{320,256},{384,320},{4... | collective-permute-start | bytes 921608 | tf_op jit(solution)/shard_map/ppermute | solution.py:107
  66.4 0.8 bitcast_dynamic-update-slice_fusion.8
  67.2 0.8 bitcast_dynamic-update-slice_fusion.7
  67.9 1.8 %collective-permute-done.5 = bf16[640,240]{1,0:T(8,128)(2,1)S(1)} collective-permute-done((bf16[640,240]{1,0:T(8,128)(2,1)S(1)}, bf16[640,240]{1,0:T(8,128)(2,1)S(1)}, u32[]{:S(2)}, u32[]{:S(2)}) %collective-permute-start.5) | collective-permute-done | bytes 307232 | tf_op jit(solution)/shard_map/ppermute | solution.py:104
  69.8 1.9 %collective-permute-start.7 = (bf16[640,240]{1,0:T(8,128)(2,1)S(1)}, bf16[640,240]{1,0:T(8,128)(2,1)S(1)}, u32[]{:S(2)}, u32[]{:S(2)}) collective-permute-start(bf16[640,240]{1,0:T(8,128)(2,1)S(1)} %collective-permute-done.5), channel_id=1, source_target_pairs={{0,64},{64,128},{128,192},{192,256},{256,320},{320,384},{384,448},... | collective-permute-start | bytes 921608 | tf_op jit(solution)/shard_map/ppermute | solution.py:104
  71.7 5.1 %collective-permute-start.8 = (bf16[640,240]{1,0:T(8,128)(2,1)S(1)}, bf16[640,240]{1,0:T(8,128)(2,1)S(1)}, u32[]{:S(2)}, u32[]{:S(2)}) collective-permute-start(bf16[640,240]{1,0:T(8,128)(2,1)S(1)} %collective-permute-done.6), channel_id=1, source_target_pairs={{0,704},{64,0},{128,64},{192,128},{256,192},{320,256},{384,320},{4... | collective-permute-start | bytes 921608 | tf_op jit(solution)/shard_map/ppermute | solution.py:107
  76.9 0.8 bitcast_dynamic-update-slice_fusion.6
  77.6 0.7 bitcast_dynamic-update-slice_fusion.5
  78.4 1.6 collective-permute-done.7
  80.0 1.9 %collective-permute-start.9 = (bf16[640,240]{1,0:T(8,128)(2,1)S(1)}, bf16[640,240]{1,0:T(8,128)(2,1)S(1)}, u32[]{:S(2)}, u32[]{:S(2)}) collective-permute-start(bf16[640,240]{1,0:T(8,128)(2,1)S(1)} %collective-permute-done.7), channel_id=1, source_target_pairs={{0,64},{64,128},{128,192},{192,256},{256,320},{320,384},{384,448},... | collective-permute-start | bytes 921608 | tf_op jit(solution)/shard_map/ppermute | solution.py:104
  81.9 5.1 %collective-permute-start.10 = (bf16[640,240]{1,0:T(8,128)(2,1)S(1)}, bf16[640,240]{1,0:T(8,128)(2,1)S(1)}, u32[]{:S(2)}, u32[]{:S(2)}) collective-permute-start(bf16[640,240]{1,0:T(8,128)(2,1)S(1)} %collective-permute-done.8), channel_id=1, source_target_pairs={{0,704},{64,0},{128,64},{192,128},{256,192},{320,256},{384,320},{4... | collective-permute-start | bytes 921608 | tf_op jit(solution)/shard_map/ppermute | solution.py:107
  87.0 0.8 bitcast_dynamic-update-slice_fusion.4
  87.8 0.8 bitcast_dynamic-update-slice_fusion.3
  88.5 1.6 collective-permute-done.9
  90.1 1.9 %collective-permute-start.11 = (bf16[640,240]{1,0:T(8,128)(2,1)S(1)}, bf16[640,240]{1,0:T(8,128)(2,1)S(1)}, u32[]{:S(2)}, u32[]{:S(2)}) collective-permute-start(bf16[640,240]{1,0:T(8,128)(2,1)S(1)} %collective-permute-done.9), channel_id=1, source_target_pairs={{0,64},{64,128},{128,192},{192,256},{256,320},{320,384},{384,448},... | collective-permute-start | bytes 921608 | tf_op jit(solution)/shard_map/ppermute | solution.py:104
  92.0 0.7 bitcast_dynamic-update-slice_fusion.2
  92.8 0.7 bitcast_dynamic-update-slice_fusion.1
  93.5 6.8 %collective-permute-done.11 = bf16[640,240]{1,0:T(8,128)(2,1)S(1)} collective-permute-done((bf16[640,240]{1,0:T(8,128)(2,1)S(1)}, bf16[640,240]{1,0:T(8,128)(2,1)S(1)}, u32[]{:S(2)}, u32[]{:S(2)}) %collective-permute-start.11) | collective-permute-done | bytes 307232 | tf_op jit(solution)/shard_map/ppermute | solution.py:104
  100.3 0.8 bitcast_dynamic-update-slice_fusion
  101.0 5.9 %shard_map.41 = (bf16[320,240]{1,0:T(8,128)(2,1)}, f32[2]{0:T(128)}) custom-call(s32[3]{0:T(128)} %pad_add_fusion.place_ref, bf16[32,320,240]{2,1,0:T(8,128)(2,1)} %bitcast.31, bf16[7680,240]{1,0:T(8,128)(2,1)} %bitcast.16.right_ref, s32[320,240]{1,0:T(8,128)} %fusion.3.keep_ref), custom_call_target="tpu_custom_call" | custom-call | flops 1179648000 | bytes 9062400 | tf_op jit(solution)/shard_map/pallas_call | solution.py:70
  107.0 2.6 %psum.35 = f32[2]{0:T(128)S(1)} all-reduce(f32[2]{0:T(128)} %get-tuple-element.5), channel_id=1, replica_groups=mesh['row_0'=12,'row_1'=2,'col_0'=4,'col_1'=4,'col_2'=2] {'col_2'}, use_global_device_ids=true, to_apply=%region_0.1 | all-reduce | flops 2 | bytes 16 | tf_op jit(solution)/shard_map/psum | solution.py:128
  109.6 14.4 %psum.36 = f32[2]{0:T(128)S(1)} all-reduce(f32[2]{0:T(128)S(1)} %psum.35), channel_id=1, replica_groups=mesh['row_0'=12,'row_1'=2,'col_0'=4,'col_1'=4,'col_2'=2] {'col_1'}, use_global_device_ids=true, to_apply=%region_1.2 | all-reduce | flops 2 | bytes 16 | tf_op jit(solution)/shard_map/psum | solution.py:128
  124.0 10.5 %psum.37 = f32[2]{0:T(128)S(1)} all-reduce(f32[2]{0:T(128)S(1)} %psum.36), channel_id=1, replica_groups=mesh['row_0'=12,'row_1'=2,'col_0'=4,'col_1'=4,'col_2'=2] {'col_0'}, use_global_device_ids=true, to_apply=%region_2.3 | all-reduce | flops 2 | bytes 16 | tf_op jit(solution)/shard_map/psum | solution.py:128
  134.5 8.8 %psum.38 = f32[2]{0:T(128)S(1)} all-reduce(f32[2]{0:T(128)S(1)} %psum.37), channel_id=1, replica_groups=mesh['row_0'=12,'row_1'=2,'col_0'=4,'col_1'=4,'col_2'=2] {'row_1'}, use_global_device_ids=true, to_apply=%region_3.4 | all-reduce | flops 2 | bytes 16 | tf_op jit(solution)/shard_map/psum | solution.py:128
  143.3 21.1 %psum.39 = f32[2]{0:T(128)} all-reduce(f32[2]{0:T(128)S(1)} %psum.38), channel_id=1, replica_groups=mesh['row_0'=12,'row_1'=2,'col_0'=4,'col_1'=4,'col_2'=2] {'row_0'}, use_global_device_ids=true, to_apply=%region_4.5 | all-reduce | flops 2 | bytes 16 | tf_op jit(solution)/shard_map/psum | solution.py:128
  (12 shorter events, 0.1 us)
Async XLA Ops:
  7.2 93.9 %all-gather.3.cloned.1.call-start = ((), (), s32[]{:S(2)}) async-start(), calls=%async_computation | async-start | bytes 5406720 | tf_op jit(solution)/shard_map/all_gather | solution.py:120
  10.3 14.8 %collective-permute-start = (bf16[320,240]{1,0:T(8,128)(2,1)}, bf16[320,240]{1,0:T(8,128)(2,1)S(1)}, u32[]{:S(2)}, u32[]{:S(2)}) collective-permute-start(bf16[320,240]{1,0:T(8,128)(2,1)} %broadcast_select_fusion), channel_id=1, source_target_pairs={{0,32},{32,0},{1,33},{33,1},{2,34},{34,2},{3,35},{35,3},{4,36},{36... | collective-permute-start | bytes 460808 | tf_op jit(solution)/shard_map/ppermute | solution.py:90
  26.2 21.7 %collective-permute-start.1 = (bf16[640,240]{1,0:T(8,128)(2,1)S(1)}, bf16[640,240]{1,0:T(8,128)(2,1)S(1)}, u32[]{:S(2)}, u32[]{:S(2)}) collective-permute-start(bf16[640,240]{1,0:T(8,128)(2,1)S(1)} %maximum_select_fusion.1), channel_id=1, source_target_pairs={{0,64},{64,128},{128,192},{192,256},{256,320},{320,384},{384,448},... | collective-permute-start | bytes 921608 | tf_op jit(solution)/shard_map/ppermute | solution.py:104
  30.5 19.4 %collective-permute-start.2 = (bf16[640,240]{1,0:T(8,128)(2,1)S(1)}, bf16[640,240]{1,0:T(8,128)(2,1)S(1)}, u32[]{:S(2)}, u32[]{:S(2)}) collective-permute-start(bf16[640,240]{1,0:T(8,128)(2,1)S(1)} %maximum_select_fusion.1), channel_id=1, source_target_pairs={{0,704},{64,0},{128,64},{192,128},{256,192},{320,256},{384,320},{4... | collective-permute-start | bytes 921608 | tf_op jit(solution)/shard_map/ppermute | solution.py:107
  48.0 11.4 %collective-permute-start.3 = (bf16[640,240]{1,0:T(8,128)(2,1)S(1)}, bf16[640,240]{1,0:T(8,128)(2,1)S(1)}, u32[]{:S(2)}, u32[]{:S(2)}) collective-permute-start(bf16[640,240]{1,0:T(8,128)(2,1)S(1)} %collective-permute-done.1), channel_id=1, source_target_pairs={{0,64},{64,128},{128,192},{192,256},{256,320},{320,384},{384,448},... | collective-permute-start | bytes 921608 | tf_op jit(solution)/shard_map/ppermute | solution.py:104
  49.9 11.4 %collective-permute-start.4 = (bf16[640,240]{1,0:T(8,128)(2,1)S(1)}, bf16[640,240]{1,0:T(8,128)(2,1)S(1)}, u32[]{:S(2)}, u32[]{:S(2)}) collective-permute-start(bf16[640,240]{1,0:T(8,128)(2,1)S(1)} %collective-permute-done.2), channel_id=1, source_target_pairs={{0,704},{64,0},{128,64},{192,128},{256,192},{320,256},{384,320},{4... | collective-permute-start | bytes 921608 | tf_op jit(solution)/shard_map/ppermute | solution.py:107
  59.3 10.4 %collective-permute-start.5 = (bf16[640,240]{1,0:T(8,128)(2,1)S(1)}, bf16[640,240]{1,0:T(8,128)(2,1)S(1)}, u32[]{:S(2)}, u32[]{:S(2)}) collective-permute-start(bf16[640,240]{1,0:T(8,128)(2,1)S(1)} %collective-permute-done.3), channel_id=1, source_target_pairs={{0,64},{64,128},{128,192},{192,256},{256,320},{320,384},{384,448},... | collective-permute-start | bytes 921608 | tf_op jit(solution)/shard_map/ppermute | solution.py:104
  61.3 10.4 %collective-permute-start.6 = (bf16[640,240]{1,0:T(8,128)(2,1)S(1)}, bf16[640,240]{1,0:T(8,128)(2,1)S(1)}, u32[]{:S(2)}, u32[]{:S(2)}) collective-permute-start(bf16[640,240]{1,0:T(8,128)(2,1)S(1)} %collective-permute-done.4), channel_id=1, source_target_pairs={{0,704},{64,0},{128,64},{192,128},{256,192},{320,256},{384,320},{4... | collective-permute-start | bytes 921608 | tf_op jit(solution)/shard_map/ppermute | solution.py:107
  69.8 10.2 %collective-permute-start.7 = (bf16[640,240]{1,0:T(8,128)(2,1)S(1)}, bf16[640,240]{1,0:T(8,128)(2,1)S(1)}, u32[]{:S(2)}, u32[]{:S(2)}) collective-permute-start(bf16[640,240]{1,0:T(8,128)(2,1)S(1)} %collective-permute-done.5), channel_id=1, source_target_pairs={{0,64},{64,128},{128,192},{192,256},{256,320},{320,384},{384,448},... | collective-permute-start | bytes 921608 | tf_op jit(solution)/shard_map/ppermute | solution.py:104
  71.7 10.2 %collective-permute-start.8 = (bf16[640,240]{1,0:T(8,128)(2,1)S(1)}, bf16[640,240]{1,0:T(8,128)(2,1)S(1)}, u32[]{:S(2)}, u32[]{:S(2)}) collective-permute-start(bf16[640,240]{1,0:T(8,128)(2,1)S(1)} %collective-permute-done.6), channel_id=1, source_target_pairs={{0,704},{64,0},{128,64},{192,128},{256,192},{320,256},{384,320},{4... | collective-permute-start | bytes 921608 | tf_op jit(solution)/shard_map/ppermute | solution.py:107
  80.0 10.2 %collective-permute-start.9 = (bf16[640,240]{1,0:T(8,128)(2,1)S(1)}, bf16[640,240]{1,0:T(8,128)(2,1)S(1)}, u32[]{:S(2)}, u32[]{:S(2)}) collective-permute-start(bf16[640,240]{1,0:T(8,128)(2,1)S(1)} %collective-permute-done.7), channel_id=1, source_target_pairs={{0,64},{64,128},{128,192},{192,256},{256,320},{320,384},{384,448},... | collective-permute-start | bytes 921608 | tf_op jit(solution)/shard_map/ppermute | solution.py:104
  81.9 10.9 %collective-permute-start.10 = (bf16[640,240]{1,0:T(8,128)(2,1)S(1)}, bf16[640,240]{1,0:T(8,128)(2,1)S(1)}, u32[]{:S(2)}, u32[]{:S(2)}) collective-permute-start(bf16[640,240]{1,0:T(8,128)(2,1)S(1)} %collective-permute-done.8), channel_id=1, source_target_pairs={{0,704},{64,0},{128,64},{192,128},{256,192},{320,256},{384,320},{4... | collective-permute-start | bytes 921608 | tf_op jit(solution)/shard_map/ppermute | solution.py:107
  90.1 10.2 %collective-permute-start.11 = (bf16[640,240]{1,0:T(8,128)(2,1)S(1)}, bf16[640,240]{1,0:T(8,128)(2,1)S(1)}, u32[]{:S(2)}, u32[]{:S(2)}) collective-permute-start(bf16[640,240]{1,0:T(8,128)(2,1)S(1)} %collective-permute-done.9), channel_id=1, source_target_pairs={{0,64},{64,128},{128,192},{192,256},{256,320},{320,384},{384,448},... | collective-permute-start | bytes 921608 | tf_op jit(solution)/shard_map/ppermute | solution.py:104
Sparse Core Ops, SparseCore 0:
  11.0 75.1 all-gather.2

commit v7 on v6

--- a/solution.py
+++ b/solution.py
@@ -84,29 +84,45 @@
     )(place, left, right, keep)
 
 
+def ring_chain(own, partner, slab, here, depth, count, sign):
+    rows = own.shape[0]
+    half = lax.axis_index("row_1")
+    perm = [(i, (i + sign) % depth) for i in range(depth)]
+    received = None
+    for step in range(1, count + 2):
+        if step == 1:
+            message = own
+        elif step == 2:
+            message = jnp.concatenate([received, partner])
+        elif step <= count:
+            message = received
+        else:
+            message = received[rows:]
+        received = lax.ppermute(message, "row_0", perm)
+        own_at = (here - sign * step) % depth
+        partner_at = (here - sign * (step - 1)) % depth
+        if step <= count:
+            slab = lax.dynamic_update_slice(
+                slab, received[None, None, :rows], (own_at, half, 0, 0)
+            )
+        if step >= 2:
+            slab = lax.dynamic_update_slice(
+                slab, received[None, None, -rows:], (partner_at, 1 - half, 0, 0)
+            )
+    return slab
+
+
 def column_slab(masked):
     depth = lax.psum(1, "row_0")
     half = lax.axis_index("row_1")
-    other = lax.ppermute(masked, "row_1", [(0, 1), (1, 0)])
-    pair = jnp.where(
-        half == 0,
-        jnp.concatenate([masked, other]),
-        jnp.concatenate([other, masked]),
-    )
+    partner = lax.ppermute(masked, "row_1", [(0, 1), (1, 0)])
     here = lax.axis_index("row_0")
-    slab = jnp.zeros((depth,) + pair.shape, pair.dtype)
-    slab = lax.dynamic_update_index_in_dim(slab, pair, here, 0)
-    forward = [(i, (i + 1) % depth) for i in range(depth)]
-    backward = [(i, (i - 1) % depth) for i in range(depth)]
-    ahead = pair
-    behind = pair
-    for step in range(1, depth // 2 + 1):
-        ahead = lax.ppermute(ahead, "row_0", forward)
-        slab = lax.dynamic_update_index_in_dim(slab, ahead, (here - step) % depth, 0)
-        if step < depth - depth // 2:
-            behind = lax.ppermute(behind, "row_0", backward)
-            slab = lax.dynamic_update_index_in_dim(slab, behind, (here + step) % depth, 0)
-    return slab.reshape(depth * pair.shape[0], pair.shape[1])
+    slab = jnp.zeros((depth, 2) + masked.shape, masked.dtype)
+    slab = lax.dynamic_update_slice(slab, masked[None, None], (here, half, 0, 0))
+    slab = lax.dynamic_update_slice(slab, partner[None, None], (here, 1 - half, 0, 0))
+    slab = ring_chain(masked, partner, slab, here, depth, depth // 2, 1)
+    slab = ring_chain(masked, partner, slab, here, depth, depth - 1 - depth // 2, -1)
+    return slab.reshape(depth * 2 * masked.shape[0], masked.shape[1])
 
 
 def on_device(iterate, pattern):

time: 172 us -> 182 us (1.058)
  the two profiles are of different devices: /device:TPU:40 before, /device:TPU:64 now
where the time goes in v7:
time: 182 us
  starting transfers between devices  55.7 us (31%)
  blocking collectives  55.5 us (30%)
  waiting for transfers between devices  28.5 us (16%)
  local copies, waits for them, and re-layouts  18.2 us (10%)
  between operations  14.3 us (8%)
  Pallas kernels  5.9 us (3%)
  other arithmetic  3.64 us (2%)
    psum x5, blocking collectives, on_device(): traces = lax.psum(traces, axis)  55.5 us
    ppermute x13, starting transfers between devices, ring_chain(): received = lax.ppermute(message, 'row_0', perm)  47.9 us
    ppermute x13, waiting for transfers between devices, ring_chain(): received = lax.ppermute(message, 'row_0', perm)  28.5 us
    ppermute x1, starting transfers between devices, column_slab(): partner = lax.ppermute(masked, 'row_1', [(0, 1), (1, 0)])  7.73 us
    dynamic_update_slice x11, local copies, waits for them, and re-layouts, ring_chain(): lax.dynamic_update_slice(slab, received[None, None, :rows], (own_at, half...  7.46 us
    dynamic_update_slice x11, local copies, waits for them, and re-layouts, ring_chain(): lax.dynamic_update_slice(slab, received[None, None, -rows:], (partner_at,...  7.43 us
    pallas_call x1, Pallas kernels, panel_product(): pl.pallas_call(panel_kernel, out_shape=(jax.ShapeDtypeStruct((tile_rows,...  5.9 us
  transfers between devices with their start and end apart: 15, of which 7 were waited for; matrix products, arithmetic and copies ran while one was open for 10% of the time, Pallas kernels for 0%

profile of v7, /device:TPU:64, one launch (start us, length us, event | category | flops | bytes accessed | tf_op | source)
XLA Modules:
  0.0 181.7 jit_solution(64143261051128315)
XLA Ops:
  7.3 0.8 fusion.16
  8.4 2.4 %broadcast_in_dim.91 = bf16[12,2,320,240]{3,2,1,0:T(8,128)(2,1)} broadcast(bf16[]{:T(256)} %constant.143.clone.1), dimensions={} | broadcast | bytes 3686402 | tf_op jit(solution)/shard_map/broadcast_in_dim | solution.py:120
  10.8 1.0 bitcast_dynamic-update-slice_fusion.7
  11.8 7.7 %collective-permute-start = (bf16[320,240]{1,0:T(8,128)(2,1)}, bf16[320,240]{1,0:T(8,128)(2,1)S(1)}, u32[]{:S(2)}, u32[]{:S(2)}) collective-permute-start(bf16[320,240]{1,0:T(8,128)(2,1)} %get-tuple-element.12), channel_id=1, source_target_pairs={{0,32},{32,0},{1,33},{33,1},{2,34},{34,2},{3,35},{35,3},{4,36},{36... | collective-permute-start | bytes 460808 | tf_op jit(solution)/shard_map/ppermute | solution.py:118
  19.6 4.3 %collective-permute-start.1 = (bf16[320,240]{1,0:T(8,128)(2,1)}, bf16[320,240]{1,0:T(8,128)(2,1)S(1)}, u32[]{:S(2)}, u32[]{:S(2)}) collective-permute-start(bf16[320,240]{1,0:T(8,128)(2,1)} %get-tuple-element.12), channel_id=1, source_target_pairs={{0,64},{64,128},{128,192},{192,256},{256,320},{320,384},{384,448},... | collective-permute-start | bytes 460808 | tf_op jit(solution)/shard_map/ppermute | solution.py:101
  23.9 2.4 %collective-permute-start.8 = (bf16[320,240]{1,0:T(8,128)(2,1)}, bf16[320,240]{1,0:T(8,128)(2,1)S(1)}, u32[]{:S(2)}, u32[]{:S(2)}) collective-permute-start(bf16[320,240]{1,0:T(8,128)(2,1)} %get-tuple-element.12), channel_id=1, source_target_pairs={{0,704},{64,0},{128,64},{192,128},{256,192},{320,256},{384,320},{4... | collective-permute-start | bytes 460808 | tf_op jit(solution)/shard_map/ppermute | solution.py:101
  26.2 1.0 fusion.18.keep_ref
  27.9 4.1 %collective-permute-done.8 = bf16[320,240]{1,0:T(8,128)(2,1)S(1)} collective-permute-done((bf16[320,240]{1,0:T(8,128)(2,1)}, bf16[320,240]{1,0:T(8,128)(2,1)S(1)}, u32[]{:S(2)}, u32[]{:S(2)}) %collective-permute-start.8) | collective-permute-done | bytes 153632 | tf_op jit(solution)/shard_map/ppermute | solution.py:101
  32.1 5.5 %collective-permute-start.2 = (bf16[640,240]{1,0:T(8,128)(2,1)S(1)}, bf16[640,240]{1,0:T(8,128)(2,1)S(1)}, u32[]{:S(2)}, u32[]{:S(2)}) collective-permute-start(bf16[640,240]{1,0:T(8,128)(2,1)S(1)} %get-tuple-element.14), channel_id=1, source_target_pairs={{0,64},{64,128},{128,192},{192,256},{256,320},{320,384},{384,448},... | collective-permute-start | bytes 921608 | tf_op jit(solution)/shard_map/ppermute | solution.py:101
  37.5 5.6 %collective-permute-start.9 = (bf16[640,240]{1,0:T(8,128)(2,1)S(1)}, bf16[640,240]{1,0:T(8,128)(2,1)S(1)}, u32[]{:S(2)}, u32[]{:S(2)}) collective-permute-start(bf16[640,240]{1,0:T(8,128)(2,1)S(1)} %get-tuple-element.13), channel_id=1, source_target_pairs={{0,704},{64,0},{128,64},{192,128},{256,192},{320,256},{384,320},{4... | collective-permute-start | bytes 921608 | tf_op jit(solution)/shard_map/ppermute | solution.py:101
  43.1 0.7 bitcast_dynamic-update-slice_fusion.6
  44.5 3.2 %collective-permute-done.2 = bf16[640,240]{1,0:T(8,128)(2,1)S(1)} collective-permute-done((bf16[640,240]{1,0:T(8,128)(2,1)S(1)}, bf16[640,240]{1,0:T(8,128)(2,1)S(1)}, u32[]{:S(2)}, u32[]{:S(2)}) %collective-permute-start.2) | collective-permute-done | bytes 307232 | tf_op jit(solution)/shard_map/ppermute | solution.py:101
  47.7 1.9 %collective-permute-start.3 = (bf16[640,240]{1,0:T(8,128)(2,1)S(1)}, bf16[640,240]{1,0:T(8,128)(2,1)S(1)}, u32[]{:S(2)}, u32[]{:S(2)}) collective-permute-start(bf16[640,240]{1,0:T(8,128)(2,1)S(1)} %collective-permute-done.2), channel_id=1, source_target_pairs={{0,64},{64,128},{128,192},{192,256},{256,320},{320,384},{384,448},... | collective-permute-start | bytes 921608 | tf_op jit(solution)/shard_map/ppermute | solution.py:101
  49.6 5.5 %collective-permute-start.10 = (bf16[640,240]{1,0:T(8,128)(2,1)S(1)}, bf16[640,240]{1,0:T(8,128)(2,1)S(1)}, u32[]{:S(2)}, u32[]{:S(2)}) collective-permute-start(bf16[640,240]{1,0:T(8,128)(2,1)S(1)} %collective-permute-done.9), channel_id=1, source_target_pairs={{0,704},{64,0},{128,64},{192,128},{256,192},{320,256},{384,320},{4... | collective-permute-start | bytes 921608 | tf_op jit(solution)/shard_map/ppermute | solution.py:101
  55.1 0.7 fusion.15
  56.5 2.6 %collective-permute-done.3 = bf16[640,240]{1,0:T(8,128)(2,1)S(1)} collective-permute-done((bf16[640,240]{1,0:T(8,128)(2,1)S(1)}, bf16[640,240]{1,0:T(8,128)(2,1)S(1)}, u32[]{:S(2)}, u32[]{:S(2)}) %collective-permute-start.3) | collective-permute-done | bytes 307232 | tf_op jit(solution)/shard_map/ppermute | solution.py:101
  59.1 1.9 %collective-permute-start.4 = (bf16[640,240]{1,0:T(8,128)(2,1)S(1)}, bf16[640,240]{1,0:T(8,128)(2,1)S(1)}, u32[]{:S(2)}, u32[]{:S(2)}) collective-permute-start(bf16[640,240]{1,0:T(8,128)(2,1)S(1)} %collective-permute-done.3), channel_id=1, source_target_pairs={{0,64},{64,128},{128,192},{192,256},{256,320},{320,384},{384,448},... | collective-permute-start | bytes 921608 | tf_op jit(solution)/shard_map/ppermute | solution.py:101
  61.0 4.9 %collective-permute-start.11 = (bf16[640,240]{1,0:T(8,128)(2,1)S(1)}, bf16[640,240]{1,0:T(8,128)(2,1)S(1)}, u32[]{:S(2)}, u32[]{:S(2)}) collective-permute-start(bf16[640,240]{1,0:T(8,128)(2,1)S(1)} %collective-permute-done.10), channel_id=1, source_target_pairs={{0,704},{64,0},{128,64},{192,128},{256,192},{320,256},{384,320},{4... | collective-permute-start | bytes 921608 | tf_op jit(solution)/shard_map/ppermute | solution.py:101
  65.8 0.7 fusion.13
  66.5 0.7 fusion.12
  67.2 1.7 collective-permute-done.4
  68.9 1.9 %collective-permute-start.5 = (bf16[640,240]{1,0:T(8,128)(2,1)S(1)}, bf16[640,240]{1,0:T(8,128)(2,1)S(1)}, u32[]{:S(2)}, u32[]{:S(2)}) collective-permute-start(bf16[640,240]{1,0:T(8,128)(2,1)S(1)} %collective-permute-done.4), channel_id=1, source_target_pairs={{0,64},{64,128},{128,192},{192,256},{256,320},{320,384},{384,448},... | collective-permute-start | bytes 921608 | tf_op jit(solution)/shard_map/ppermute | solution.py:101
  70.9 5.1 %collective-permute-start.12 = (bf16[640,240]{1,0:T(8,128)(2,1)S(1)}, bf16[640,240]{1,0:T(8,128)(2,1)S(1)}, u32[]{:S(2)}, u32[]{:S(2)}) collective-permute-start(bf16[640,240]{1,0:T(8,128)(2,1)S(1)} %collective-permute-done.11), channel_id=1, source_target_pairs={{0,704},{64,0},{128,64},{192,128},{256,192},{320,256},{384,320},{4... | collective-permute-start | bytes 921608 | tf_op jit(solution)/shard_map/ppermute | solution.py:101
  76.0 0.7 fusion.11
  77.4 3.2 %collective-permute-done.12 = bf16[640,240]{1,0:T(8,128)(2,1)S(1)} collective-permute-done((bf16[640,240]{1,0:T(8,128)(2,1)S(1)}, bf16[640,240]{1,0:T(8,128)(2,1)S(1)}, u32[]{:S(2)}, u32[]{:S(2)}) %collective-permute-start.12) | collective-permute-done | bytes 307232 | tf_op jit(solution)/shard_map/ppermute | solution.py:101
  80.6 5.1 %collective-permute-start.13 = (bf16[320,240]{1,0:T(8,128)(2,1)S(1)}, bf16[320,240]{1,0:T(8,128)(2,1)S(1)}, u32[]{:S(2)}, u32[]{:S(2)}) collective-permute-start(bf16[320,240]{1,0:T(8,128)(2,1)S(1)} %slice.116), channel_id=1, source_target_pairs={{0,704},{64,0},{128,64},{192,128},{256,192},{320,256},{384,320},{4... | collective-permute-start | bytes 460808 | tf_op jit(solution)/shard_map/ppermute | solution.py:101
  85.8 1.9 %collective-permute-start.6 = (bf16[640,240]{1,0:T(8,128)(2,1)S(1)}, bf16[640,240]{1,0:T(8,128)(2,1)S(1)}, u32[]{:S(2)}, u32[]{:S(2)}) collective-permute-start(bf16[640,240]{1,0:T(8,128)(2,1)S(1)} %collective-permute-done.5), channel_id=1, source_target_pairs={{0,64},{64,128},{128,192},{192,256},{256,320},{320,384},{384,448},... | collective-permute-start | bytes 921608 | tf_op jit(solution)/shard_map/ppermute | solution.py:101
  87.7 0.7 fusion.9
  88.4 0.7 fusion.8
  89.0 8.2 %collective-permute-done.6 = bf16[640,240]{1,0:T(8,128)(2,1)S(1)} collective-permute-done((bf16[640,240]{1,0:T(8,128)(2,1)S(1)}, bf16[640,240]{1,0:T(8,128)(2,1)S(1)}, u32[]{:S(2)}, u32[]{:S(2)}) %collective-permute-start.6) | collective-permute-done | bytes 307232 | tf_op jit(solution)/shard_map/ppermute | solution.py:101
  97.3 1.9 %collective-permute-start.7 = (bf16[320,240]{1,0:T(8,128)(2,1)S(1)}, bf16[320,240]{1,0:T(8,128)(2,1)S(1)}, u32[]{:S(2)}, u32[]{:S(2)}) collective-permute-start(bf16[320,240]{1,0:T(8,128)(2,1)S(1)} %slice.108), channel_id=1, source_target_pairs={{0,64},{64,128},{128,192},{192,256},{256,320},{320,384},{384,448},... | collective-permute-start | bytes 460808 | tf_op jit(solution)/shard_map/ppermute | solution.py:101
  99.2 0.7 fusion.7
  99.9 0.7 bitcast_dynamic-update-slice_fusion.4
  100.6 5.4 %collective-permute-done.7 = bf16[320,240]{1,0:T(8,128)(2,1)S(1)} collective-permute-done((bf16[320,240]{1,0:T(8,128)(2,1)S(1)}, bf16[320,240]{1,0:T(8,128)(2,1)S(1)}, u32[]{:S(2)}, u32[]{:S(2)}) %collective-permute-start.7) | collective-permute-done | bytes 153632 | tf_op jit(solution)/shard_map/ppermute | solution.py:101
  106.7 0.7 bitcast_dynamic-update-slice_fusion.2
  108.0 0.7 fusion.5
  108.7 0.7 fusion.4
  109.4 0.7 fusion.3
  110.0 0.7 fusion.2
  110.7 0.7 fusion.1
  111.4 0.7 fusion
  112.7 0.7 bitcast_dynamic-update-slice_fusion
  113.4 5.9 %shard_map.41 = (bf16[320,240]{1,0:T(8,128)(2,1)}, f32[2]{0:T(128)}) custom-call(s32[3]{0:T(128)} %pad_add_fusion.place_ref, bf16[32,320,240]{2,1,0:T(8,128)(2,1)} %bitcast.86, bf16[7680,240]{1,0:T(8,128)(2,1)} %bitcast.27.right_ref, s32[320,240]{1,0:T(8,128)} %fusion.18.keep_ref), custom_call_target="tpu_custom_call" | custom-call | flops 1179648000 | bytes 9062400 | tf_op jit(solution)/shard_map/pallas_call | solution.py:70
  119.3 2.6 %psum.35 = f32[2]{0:T(128)S(1)} all-reduce(f32[2]{0:T(128)} %get-tuple-element.5), channel_id=1, replica_groups=mesh['row_0'=12,'row_1'=2,'col_0'=4,'col_1'=4,'col_2'=2] {'col_2'}, use_global_device_ids=true, to_apply=%region_0.1 | all-reduce | flops 2 | bytes 16 | tf_op jit(solution)/shard_map/psum | solution.py:144
  122.0 9.3 %psum.36 = f32[2]{0:T(128)S(1)} all-reduce(f32[2]{0:T(128)S(1)} %psum.35), channel_id=1, replica_groups=mesh['row_0'=12,'row_1'=2,'col_0'=4,'col_1'=4,'col_2'=2] {'col_1'}, use_global_device_ids=true, to_apply=%region_1.2 | all-reduce | flops 2 | bytes 16 | tf_op jit(solution)/shard_map/psum | solution.py:144
  131.2 10.5 %psum.37 = f32[2]{0:T(128)S(1)} all-reduce(f32[2]{0:T(128)S(1)} %psum.36), channel_id=1, replica_groups=mesh['row_0'=12,'row_1'=2,'col_0'=4,'col_1'=4,'col_2'=2] {'col_0'}, use_global_device_ids=true, to_apply=%region_2.3 | all-reduce | flops 2 | bytes 16 | tf_op jit(solution)/shard_map/psum | solution.py:144
  141.7 8.8 %psum.38 = f32[2]{0:T(128)S(1)} all-reduce(f32[2]{0:T(128)S(1)} %psum.37), channel_id=1, replica_groups=mesh['row_0'=12,'row_1'=2,'col_0'=4,'col_1'=4,'col_2'=2] {'row_1'}, use_global_device_ids=true, to_apply=%region_3.4 | all-reduce | flops 2 | bytes 16 | tf_op jit(solution)/shard_map/psum | solution.py:144
  150.5 24.3 %psum.39 = f32[2]{0:T(128)} all-reduce(f32[2]{0:T(128)S(1)} %psum.38), channel_id=1, replica_groups=mesh['row_0'=12,'row_1'=2,'col_0'=4,'col_1'=4,'col_2'=2] {'row_0'}, use_global_device_ids=true, to_apply=%region_4.5 | all-reduce | flops 2 | bytes 16 | tf_op jit(solution)/shard_map/psum | solution.py:144
  (30 shorter events, 5.1 us)
Async XLA Ops:
  7.2 3.6 %copy-start = (bf16[320,240]{1,0:T(8,128)(2,1)S(1)}, bf16[320,240]{1,0:T(8,128)(2,1)}, u32[]{:S(2)}) copy-start(bf16[320,240]{1,0:T(8,128)(2,1)} %param.2) | copy-start | bytes 460804
  7.2 106.3 %all-gather.3.cloned.1.call-start = ((), (), s32[]{:S(2)}) async-start(), calls=%async_computation | async-start | bytes 5406720 | tf_op jit(solution)/shard_map/all_gather | solution.py:136
  11.8 16.1 %collective-permute-start = (bf16[320,240]{1,0:T(8,128)(2,1)}, bf16[320,240]{1,0:T(8,128)(2,1)S(1)}, u32[]{:S(2)}, u32[]{:S(2)}) collective-permute-start(bf16[320,240]{1,0:T(8,128)(2,1)} %get-tuple-element.12), channel_id=1, source_target_pairs={{0,32},{32,0},{1,33},{33,1},{2,34},{34,2},{3,35},{35,3},{4,36},{36... | collective-permute-start | bytes 460808 | tf_op jit(solution)/shard_map/ppermute | solution.py:118
  19.6 8.4 %collective-permute-start.1 = (bf16[320,240]{1,0:T(8,128)(2,1)}, bf16[320,240]{1,0:T(8,128)(2,1)S(1)}, u32[]{:S(2)}, u32[]{:S(2)}) collective-permute-start(bf16[320,240]{1,0:T(8,128)(2,1)} %get-tuple-element.12), channel_id=1, source_target_pairs={{0,64},{64,128},{128,192},{192,256},{256,320},{320,384},{384,448},... | collective-permute-start | bytes 460808 | tf_op jit(solution)/shard_map/ppermute | solution.py:101
  23.9 8.1 %collective-permute-start.8 = (bf16[320,240]{1,0:T(8,128)(2,1)}, bf16[320,240]{1,0:T(8,128)(2,1)S(1)}, u32[]{:S(2)}, u32[]{:S(2)}) collective-permute-start(bf16[320,240]{1,0:T(8,128)(2,1)} %get-tuple-element.12), channel_id=1, source_target_pairs={{0,704},{64,0},{128,64},{192,128},{256,192},{320,256},{384,320},{4... | collective-permute-start | bytes 460808 | tf_op jit(solution)/shard_map/ppermute | solution.py:101
  32.1 15.6 %collective-permute-start.2 = (bf16[640,240]{1,0:T(8,128)(2,1)S(1)}, bf16[640,240]{1,0:T(8,128)(2,1)S(1)}, u32[]{:S(2)}, u32[]{:S(2)}) collective-permute-start(bf16[640,240]{1,0:T(8,128)(2,1)S(1)} %get-tuple-element.14), channel_id=1, source_target_pairs={{0,64},{64,128},{128,192},{192,256},{256,320},{320,384},{384,448},... | collective-permute-start | bytes 921608 | tf_op jit(solution)/shard_map/ppermute | solution.py:101
  37.5 12.1 %collective-permute-start.9 = (bf16[640,240]{1,0:T(8,128)(2,1)S(1)}, bf16[640,240]{1,0:T(8,128)(2,1)S(1)}, u32[]{:S(2)}, u32[]{:S(2)}) collective-permute-start(bf16[640,240]{1,0:T(8,128)(2,1)S(1)} %get-tuple-element.13), channel_id=1, source_target_pairs={{0,704},{64,0},{128,64},{192,128},{256,192},{320,256},{384,320},{4... | collective-permute-start | bytes 921608 | tf_op jit(solution)/shard_map/ppermute | solution.py:101
  47.7 11.4 %collective-permute-start.3 = (bf16[640,240]{1,0:T(8,128)(2,1)S(1)}, bf16[640,240]{1,0:T(8,128)(2,1)S(1)}, u32[]{:S(2)}, u32[]{:S(2)}) collective-permute-start(bf16[640,240]{1,0:T(8,128)(2,1)S(1)} %collective-permute-done.2), channel_id=1, source_target_pairs={{0,64},{64,128},{128,192},{192,256},{256,320},{320,384},{384,448},... | collective-permute-start | bytes 921608 | tf_op jit(solution)/shard_map/ppermute | solution.py:101
  49.6 11.3 %collective-permute-start.10 = (bf16[640,240]{1,0:T(8,128)(2,1)S(1)}, bf16[640,240]{1,0:T(8,128)(2,1)S(1)}, u32[]{:S(2)}, u32[]{:S(2)}) collective-permute-start(bf16[640,240]{1,0:T(8,128)(2,1)S(1)} %collective-permute-done.9), channel_id=1, source_target_pairs={{0,704},{64,0},{128,64},{192,128},{256,192},{320,256},{384,320},{4... | collective-permute-start | bytes 921608 | tf_op jit(solution)/shard_map/ppermute | solution.py:101
  59.1 9.9 %collective-permute-start.4 = (bf16[640,240]{1,0:T(8,128)(2,1)S(1)}, bf16[640,240]{1,0:T(8,128)(2,1)S(1)}, u32[]{:S(2)}, u32[]{:S(2)}) collective-permute-start(bf16[640,240]{1,0:T(8,128)(2,1)S(1)} %collective-permute-done.3), channel_id=1, source_target_pairs={{0,64},{64,128},{128,192},{192,256},{256,320},{320,384},{384,448},... | collective-permute-start | bytes 921608 | tf_op jit(solution)/shard_map/ppermute | solution.py:101
  61.0 9.9 %collective-permute-start.11 = (bf16[640,240]{1,0:T(8,128)(2,1)S(1)}, bf16[640,240]{1,0:T(8,128)(2,1)S(1)}, u32[]{:S(2)}, u32[]{:S(2)}) collective-permute-start(bf16[640,240]{1,0:T(8,128)(2,1)S(1)} %collective-permute-done.10), channel_id=1, source_target_pairs={{0,704},{64,0},{128,64},{192,128},{256,192},{320,256},{384,320},{4... | collective-permute-start | bytes 921608 | tf_op jit(solution)/shard_map/ppermute | solution.py:101
  68.9 16.8 %collective-permute-start.5 = (bf16[640,240]{1,0:T(8,128)(2,1)S(1)}, bf16[640,240]{1,0:T(8,128)(2,1)S(1)}, u32[]{:S(2)}, u32[]{:S(2)}) collective-permute-start(bf16[640,240]{1,0:T(8,128)(2,1)S(1)} %collective-permute-done.4), channel_id=1, source_target_pairs={{0,64},{64,128},{128,192},{192,256},{256,320},{320,384},{384,448},... | collective-permute-start | bytes 921608 | tf_op jit(solution)/shard_map/ppermute | solution.py:101
  70.9 9.7 %collective-permute-start.12 = (bf16[640,240]{1,0:T(8,128)(2,1)S(1)}, bf16[640,240]{1,0:T(8,128)(2,1)S(1)}, u32[]{:S(2)}, u32[]{:S(2)}) collective-permute-start(bf16[640,240]{1,0:T(8,128)(2,1)S(1)} %collective-permute-done.11), channel_id=1, source_target_pairs={{0,704},{64,0},{128,64},{192,128},{256,192},{320,256},{384,320},{4... | collective-permute-start | bytes 921608 | tf_op jit(solution)/shard_map/ppermute | solution.py:101
  80.6 32.1 %collective-permute-start.13 = (bf16[320,240]{1,0:T(8,128)(2,1)S(1)}, bf16[320,240]{1,0:T(8,128)(2,1)S(1)}, u32[]{:S(2)}, u32[]{:S(2)}) collective-permute-start(bf16[320,240]{1,0:T(8,128)(2,1)S(1)} %slice.116), channel_id=1, source_target_pairs={{0,704},{64,0},{128,64},{192,128},{256,192},{320,256},{384,320},{4... | collective-permute-start | bytes 460808 | tf_op jit(solution)/shard_map/ppermute | solution.py:101
  85.8 11.5 %collective-permute-start.6 = (bf16[640,240]{1,0:T(8,128)(2,1)S(1)}, bf16[640,240]{1,0:T(8,128)(2,1)S(1)}, u32[]{:S(2)}, u32[]{:S(2)}) collective-permute-start(bf16[640,240]{1,0:T(8,128)(2,1)S(1)} %collective-permute-done.5), channel_id=1, source_target_pairs={{0,64},{64,128},{128,192},{192,256},{256,320},{320,384},{384,448},... | collective-permute-start | bytes 921608 | tf_op jit(solution)/shard_map/ppermute | solution.py:101
  97.3 8.7 %collective-permute-start.7 = (bf16[320,240]{1,0:T(8,128)(2,1)S(1)}, bf16[320,240]{1,0:T(8,128)(2,1)S(1)}, u32[]{:S(2)}, u32[]{:S(2)}) collective-permute-start(bf16[320,240]{1,0:T(8,128)(2,1)S(1)} %slice.108), channel_id=1, source_target_pairs={{0,64},{64,128},{128,192},{192,256},{256,320},{320,384},{384,448},... | collective-permute-start | bytes 460808 | tf_op jit(solution)/shard_map/ppermute | solution.py:101
Sparse Core Ops, SparseCore 0:
  11.9 76.2 all-gather.2

commit v8 on v6

--- a/solution.py
+++ b/solution.py
@@ -22,12 +22,12 @@
     block_rows = row_index * row_blocks + jnp.arange(row_blocks, dtype=jnp.int32)[:, None]
     block_cols = first_block + jnp.arange(span, dtype=jnp.int32)[None, :]
     window = jnp.maximum(window, (block_rows == block_cols).astype(window.dtype))
-    per_row = jnp.repeat(window, BS, axis=0)
+    bits = jnp.sum(
+        (window > 0).astype(jnp.int32) << jnp.arange(span, dtype=jnp.int32)[None, :], axis=1
+    )
+    per_row = jnp.repeat(bits, BS)[:, None]
     local_block = (first_col + jnp.arange(tile_cols, dtype=jnp.int32)) // BS - first_block
-    keep = jnp.zeros((tile_rows, tile_cols), jnp.bool_)
-    for block in range(span):
-        keep = keep | ((local_block[None, :] == block) & (per_row[:, block:block + 1] > 0))
-    return keep
+    return ((per_row >> local_block[None, :]) & 1) > 0
 
 
 def panel_kernel(

time: 172 us -> 172 us (level)
  no operation moved by 1% of the time
where the time goes in v8:
time: 172 us; the launch traced here: 171 us
  blocking collectives  57.3 us (33%)
  starting transfers between devices  49.5 us (29%)
  waiting for transfers between devices  25.8 us (15%)
  between operations  14.5 us (8%)
  local copies, waits for them, and re-layouts  10.8 us (6%)
  other arithmetic  7.08 us (4%)
  Pallas kernels  5.9 us (3%)
    psum x5, blocking collectives, on_device(): traces = lax.psum(traces, axis)  57.3 us
    ppermute x5, starting transfers between devices, column_slab(): behind = lax.ppermute(behind, 'row_0', backward)  32.8 us
    ppermute x6, waiting for transfers between devices, column_slab(): ahead = lax.ppermute(ahead, 'row_0', forward)  15.8 us
    ppermute x6, starting transfers between devices, column_slab(): ahead = lax.ppermute(ahead, 'row_0', forward)  13.8 us
    ppermute x1, waiting for transfers between devices, column_slab(): other = lax.ppermute(masked, 'row_1', [(0, 1), (1, 0)])  9.99 us
    pallas_call x1, Pallas kernels, panel_product(): pl.pallas_call(panel_kernel, out_shape=(jax.ShapeDtypeStruct((tile_rows,...  5.9 us
    dynamic_update_slice x6, local copies, waits for them, and re-layouts, column_slab(): lax.dynamic_update_index_in_dim(slab, ahead, (here - step) % depth, 0)  4.62 us
    dynamic_update_slice x5, local copies, waits for them, and re-layouts, column_slab(): lax.dynamic_update_index_in_dim(slab, behind, (here + step) % depth, 0)  3.74 us
  transfers between devices with their start and end apart: 13, of which 7 were waited for; matrix products, arithmetic and copies ran while one was open for 9% of the time, Pallas kernels for 0%

profile of v8, /device:TPU:40, one launch (start us, length us, event | category | flops | bytes accessed | tf_op | source)
XLA Modules:
  0.0 170.9 jit_solution(13177011286030441503)
XLA Ops:
  7.2 0.0 all-gather.3.cloned.1.call-start
  7.3 0.9 shift-left_reduce_fusion
  8.2 0.1 broadcast_in_dim.49
  8.3 0.1 shift_right_arithmetic.15
  8.3 1.7 %fusion.2 = bf16[320,240]{1,0:T(8,128)(2,1)} fusion(bf16[320,240]{1,0:T(8,128)(2,1)} %param.2, s32[240]{0:T(256)S(1)} %fusion.5, s32[320]{0:T(512)S(1)} %shift_right_arithmetic.15), kind=kLoop, calls=%fused_computation.16 | loop fusion | flops 307200 | bytes 309440 | tf_op jit(solution)/shard_map/jit(_where)/select_n | solution.py:119
  10.0 0.0 all-gather.3.cloned.1.call-update
  10.1 2.9 %collective-permute-start = (bf16[320,240]{1,0:T(8,128)(2,1)}, bf16[320,240]{1,0:T(8,128)(2,1)S(1)}, u32[]{:S(2)}, u32[]{:S(2)}) collective-permute-start(bf16[320,240]{1,0:T(8,128)(2,1)} %fusion.2), channel_id=1, source_target_pairs={{0,32},{32,0},{1,33},{33,1},{2,34},{34,2},{3,35},{35,3},{4,36},{36... | collective-permute-start | bytes 460808 | tf_op jit(solution)/shard_map/ppermute | solution.py:90
  13.0 1.0 fusion.6
  14.3 0.6 pad_add_fusion.place_ref
  14.9 10.0 %collective-permute-done = bf16[320,240]{1,0:T(8,128)(2,1)S(1)} collective-permute-done((bf16[320,240]{1,0:T(8,128)(2,1)}, bf16[320,240]{1,0:T(8,128)(2,1)S(1)}, u32[]{:S(2)}, u32[]{:S(2)}) %collective-permute-start) | collective-permute-done | bytes 153632 | tf_op jit(solution)/shard_map/ppermute | solution.py:90
  24.9 1.1 maximum_select_fusion.1
  26.0 4.3 %collective-permute-start.1 = (bf16[640,240]{1,0:T(8,128)(2,1)S(1)}, bf16[640,240]{1,0:T(8,128)(2,1)S(1)}, u32[]{:S(2)}, u32[]{:S(2)}) collective-permute-start(bf16[640,240]{1,0:T(8,128)(2,1)S(1)} %maximum_select_fusion.1), channel_id=1, source_target_pairs={{0,64},{64,128},{128,192},{192,256},{256,320},{320,384},{384,448},... | collective-permute-start | bytes 921608 | tf_op jit(solution)/shard_map/ppermute | solution.py:104
  30.3 12.2 %collective-permute-start.2 = (bf16[640,240]{1,0:T(8,128)(2,1)S(1)}, bf16[640,240]{1,0:T(8,128)(2,1)S(1)}, u32[]{:S(2)}, u32[]{:S(2)}) collective-permute-start(bf16[640,240]{1,0:T(8,128)(2,1)S(1)} %maximum_select_fusion.1), channel_id=1, source_target_pairs={{0,704},{64,0},{128,64},{192,128},{256,192},{320,256},{384,320},{4... | collective-permute-start | bytes 921608 | tf_op jit(solution)/shard_map/ppermute | solution.py:107
  42.5 0.9 fusion.1.keep_ref
  43.4 2.3 %broadcast_in_dim.51 = bf16[12,640,240]{2,1,0:T(8,128)(2,1)} broadcast(bf16[]{:T(256)} %constant.131.clone.1), dimensions={} | broadcast | bytes 3686402 | tf_op jit(solution)/shard_map/broadcast_in_dim | solution.py:97
  45.7 0.8 fusion
  46.5 1.2 collective-permute-done.1
  47.7 1.9 %collective-permute-start.3 = (bf16[640,240]{1,0:T(8,128)(2,1)S(1)}, bf16[640,240]{1,0:T(8,128)(2,1)S(1)}, u32[]{:S(2)}, u32[]{:S(2)}) collective-permute-start(bf16[640,240]{1,0:T(8,128)(2,1)S(1)} %collective-permute-done.1), channel_id=1, source_target_pairs={{0,64},{64,128},{128,192},{192,256},{256,320},{320,384},{384,448},... | collective-permute-start | bytes 921608 | tf_op jit(solution)/shard_map/ppermute | solution.py:104
  49.7 5.1 %collective-permute-start.4 = (bf16[640,240]{1,0:T(8,128)(2,1)S(1)}, bf16[640,240]{1,0:T(8,128)(2,1)S(1)}, u32[]{:S(2)}, u32[]{:S(2)}) collective-permute-start(bf16[640,240]{1,0:T(8,128)(2,1)S(1)} %collective-permute-done.2), channel_id=1, source_target_pairs={{0,704},{64,0},{128,64},{192,128},{256,192},{320,256},{384,320},{4... | collective-permute-start | bytes 921608 | tf_op jit(solution)/shard_map/ppermute | solution.py:107
  54.8 0.8 bitcast_dynamic-update-slice_fusion.10
  55.6 0.7 bitcast_dynamic-update-slice_fusion.9
  56.3 2.8 %collective-permute-done.3 = bf16[640,240]{1,0:T(8,128)(2,1)S(1)} collective-permute-done((bf16[640,240]{1,0:T(8,128)(2,1)S(1)}, bf16[640,240]{1,0:T(8,128)(2,1)S(1)}, u32[]{:S(2)}, u32[]{:S(2)}) %collective-permute-start.3) | collective-permute-done | bytes 307232 | tf_op jit(solution)/shard_map/ppermute | solution.py:104
  59.1 1.9 %collective-permute-start.5 = (bf16[640,240]{1,0:T(8,128)(2,1)S(1)}, bf16[640,240]{1,0:T(8,128)(2,1)S(1)}, u32[]{:S(2)}, u32[]{:S(2)}) collective-permute-start(bf16[640,240]{1,0:T(8,128)(2,1)S(1)} %collective-permute-done.3), channel_id=1, source_target_pairs={{0,64},{64,128},{128,192},{192,256},{256,320},{320,384},{384,448},... | collective-permute-start | bytes 921608 | tf_op jit(solution)/shard_map/ppermute | solution.py:104
  61.0 5.1 %collective-permute-start.6 = (bf16[640,240]{1,0:T(8,128)(2,1)S(1)}, bf16[640,240]{1,0:T(8,128)(2,1)S(1)}, u32[]{:S(2)}, u32[]{:S(2)}) collective-permute-start(bf16[640,240]{1,0:T(8,128)(2,1)S(1)} %collective-permute-done.4), channel_id=1, source_target_pairs={{0,704},{64,0},{128,64},{192,128},{256,192},{320,256},{384,320},{4... | collective-permute-start | bytes 921608 | tf_op jit(solution)/shard_map/ppermute | solution.py:107
  66.2 0.8 bitcast_dynamic-update-slice_fusion.8
  67.0 0.8 bitcast_dynamic-update-slice_fusion.7
  67.7 1.8 %collective-permute-done.5 = bf16[640,240]{1,0:T(8,128)(2,1)S(1)} collective-permute-done((bf16[640,240]{1,0:T(8,128)(2,1)S(1)}, bf16[640,240]{1,0:T(8,128)(2,1)S(1)}, u32[]{:S(2)}, u32[]{:S(2)}) %collective-permute-start.5) | collective-permute-done | bytes 307232 | tf_op jit(solution)/shard_map/ppermute | solution.py:104
  69.6 1.9 %collective-permute-start.7 = (bf16[640,240]{1,0:T(8,128)(2,1)S(1)}, bf16[640,240]{1,0:T(8,128)(2,1)S(1)}, u32[]{:S(2)}, u32[]{:S(2)}) collective-permute-start(bf16[640,240]{1,0:T(8,128)(2,1)S(1)} %collective-permute-done.5), channel_id=1, source_target_pairs={{0,64},{64,128},{128,192},{192,256},{256,320},{320,384},{384,448},... | collective-permute-start | bytes 921608 | tf_op jit(solution)/shard_map/ppermute | solution.py:104
  71.5 5.1 %collective-permute-start.8 = (bf16[640,240]{1,0:T(8,128)(2,1)S(1)}, bf16[640,240]{1,0:T(8,128)(2,1)S(1)}, u32[]{:S(2)}, u32[]{:S(2)}) collective-permute-start(bf16[640,240]{1,0:T(8,128)(2,1)S(1)} %collective-permute-done.6), channel_id=1, source_target_pairs={{0,704},{64,0},{128,64},{192,128},{256,192},{320,256},{384,320},{4... | collective-permute-start | bytes 921608 | tf_op jit(solution)/shard_map/ppermute | solution.py:107
  76.6 0.8 bitcast_dynamic-update-slice_fusion.6
  77.4 0.7 bitcast_dynamic-update-slice_fusion.5
  78.2 1.6 collective-permute-done.7
  79.7 1.9 %collective-permute-start.9 = (bf16[640,240]{1,0:T(8,128)(2,1)S(1)}, bf16[640,240]{1,0:T(8,128)(2,1)S(1)}, u32[]{:S(2)}, u32[]{:S(2)}) collective-permute-start(bf16[640,240]{1,0:T(8,128)(2,1)S(1)} %collective-permute-done.7), channel_id=1, source_target_pairs={{0,64},{64,128},{128,192},{192,256},{256,320},{320,384},{384,448},... | collective-permute-start | bytes 921608 | tf_op jit(solution)/shard_map/ppermute | solution.py:104
  81.7 5.1 %collective-permute-start.10 = (bf16[640,240]{1,0:T(8,128)(2,1)S(1)}, bf16[640,240]{1,0:T(8,128)(2,1)S(1)}, u32[]{:S(2)}, u32[]{:S(2)}) collective-permute-start(bf16[640,240]{1,0:T(8,128)(2,1)S(1)} %collective-permute-done.8), channel_id=1, source_target_pairs={{0,704},{64,0},{128,64},{192,128},{256,192},{320,256},{384,320},{4... | collective-permute-start | bytes 921608 | tf_op jit(solution)/shard_map/ppermute | solution.py:107
  86.8 0.8 bitcast_dynamic-update-slice_fusion.4
  87.5 0.8 bitcast_dynamic-update-slice_fusion.3
  88.3 1.6 collective-permute-done.9
  89.9 1.9 %collective-permute-start.11 = (bf16[640,240]{1,0:T(8,128)(2,1)S(1)}, bf16[640,240]{1,0:T(8,128)(2,1)S(1)}, u32[]{:S(2)}, u32[]{:S(2)}) collective-permute-start(bf16[640,240]{1,0:T(8,128)(2,1)S(1)} %collective-permute-done.9), channel_id=1, source_target_pairs={{0,64},{64,128},{128,192},{192,256},{256,320},{320,384},{384,448},... | collective-permute-start | bytes 921608 | tf_op jit(solution)/shard_map/ppermute | solution.py:104
  91.8 0.7 bitcast_dynamic-update-slice_fusion.2
  92.6 0.7 bitcast_dynamic-update-slice_fusion.1
  93.3 6.8 %collective-permute-done.11 = bf16[640,240]{1,0:T(8,128)(2,1)S(1)} collective-permute-done((bf16[640,240]{1,0:T(8,128)(2,1)S(1)}, bf16[640,240]{1,0:T(8,128)(2,1)S(1)}, u32[]{:S(2)}, u32[]{:S(2)}) %collective-permute-start.11) | collective-permute-done | bytes 307232 | tf_op jit(solution)/shard_map/ppermute | solution.py:104
  100.1 0.8 bitcast_dynamic-update-slice_fusion
  100.8 5.9 %shard_map.41 = (bf16[320,240]{1,0:T(8,128)(2,1)}, f32[2]{0:T(128)}) custom-call(s32[3]{0:T(128)} %pad_add_fusion.place_ref, bf16[32,320,240]{2,1,0:T(8,128)(2,1)} %bitcast.29, bf16[7680,240]{1,0:T(8,128)(2,1)} %bitcast.16.right_ref, s32[320,240]{1,0:T(8,128)} %fusion.1.keep_ref), custom_call_target="tpu_custom_call" | custom-call | flops 1179648000 | bytes 9062400 | tf_op jit(solution)/shard_map/pallas_call | solution.py:70
  106.7 2.6 %psum.35 = f32[2]{0:T(128)S(1)} all-reduce(f32[2]{0:T(128)} %get-tuple-element.5), channel_id=1, replica_groups=mesh['row_0'=12,'row_1'=2,'col_0'=4,'col_1'=4,'col_2'=2] {'col_2'}, use_global_device_ids=true, to_apply=%region_1.2 | all-reduce | flops 2 | bytes 16 | tf_op jit(solution)/shard_map/psum | solution.py:128
  109.3 14.3 %psum.36 = f32[2]{0:T(128)S(1)} all-reduce(f32[2]{0:T(128)S(1)} %psum.35), channel_id=1, replica_groups=mesh['row_0'=12,'row_1'=2,'col_0'=4,'col_1'=4,'col_2'=2] {'col_1'}, use_global_device_ids=true, to_apply=%region_2.3 | all-reduce | flops 2 | bytes 16 | tf_op jit(solution)/shard_map/psum | solution.py:128
  123.6 10.5 %psum.37 = f32[2]{0:T(128)S(1)} all-reduce(f32[2]{0:T(128)S(1)} %psum.36), channel_id=1, replica_groups=mesh['row_0'=12,'row_1'=2,'col_0'=4,'col_1'=4,'col_2'=2] {'col_0'}, use_global_device_ids=true, to_apply=%region_3.4 | all-reduce | flops 2 | bytes 16 | tf_op jit(solution)/shard_map/psum | solution.py:128
  134.1 8.8 %psum.38 = f32[2]{0:T(128)S(1)} all-reduce(f32[2]{0:T(128)S(1)} %psum.37), channel_id=1, replica_groups=mesh['row_0'=12,'row_1'=2,'col_0'=4,'col_1'=4,'col_2'=2] {'row_1'}, use_global_device_ids=true, to_apply=%region_4.5 | all-reduce | flops 2 | bytes 16 | tf_op jit(solution)/shard_map/psum | solution.py:128
  143.0 21.1 %psum.39 = f32[2]{0:T(128)} all-reduce(f32[2]{0:T(128)S(1)} %psum.38), channel_id=1, replica_groups=mesh['row_0'=12,'row_1'=2,'col_0'=4,'col_1'=4,'col_2'=2] {'row_0'}, use_global_device_ids=true, to_apply=%region_5.6 | all-reduce | flops 2 | bytes 16 | tf_op jit(solution)/shard_map/psum | solution.py:128
  (8 shorter events, 0.0 us)
Async XLA Ops:
  7.2 93.7 %all-gather.3.cloned.1.call-start = ((), (), s32[]{:S(2)}) async-start(), calls=%async_computation | async-start | bytes 5406720 | tf_op jit(solution)/shard_map/all_gather | solution.py:120
  10.1 14.8 %collective-permute-start = (bf16[320,240]{1,0:T(8,128)(2,1)}, bf16[320,240]{1,0:T(8,128)(2,1)S(1)}, u32[]{:S(2)}, u32[]{:S(2)}) collective-permute-start(bf16[320,240]{1,0:T(8,128)(2,1)} %fusion.2), channel_id=1, source_target_pairs={{0,32},{32,0},{1,33},{33,1},{2,34},{34,2},{3,35},{35,3},{4,36},{36... | collective-permute-start | bytes 460808 | tf_op jit(solution)/shard_map/ppermute | solution.py:90
  26.0 21.7 %collective-permute-start.1 = (bf16[640,240]{1,0:T(8,128)(2,1)S(1)}, bf16[640,240]{1,0:T(8,128)(2,1)S(1)}, u32[]{:S(2)}, u32[]{:S(2)}) collective-permute-start(bf16[640,240]{1,0:T(8,128)(2,1)S(1)} %maximum_select_fusion.1), channel_id=1, source_target_pairs={{0,64},{64,128},{128,192},{192,256},{256,320},{320,384},{384,448},... | collective-permute-start | bytes 921608 | tf_op jit(solution)/shard_map/ppermute | solution.py:104
  30.3 19.4 %collective-permute-start.2 = (bf16[640,240]{1,0:T(8,128)(2,1)S(1)}, bf16[640,240]{1,0:T(8,128)(2,1)S(1)}, u32[]{:S(2)}, u32[]{:S(2)}) collective-permute-start(bf16[640,240]{1,0:T(8,128)(2,1)S(1)} %maximum_select_fusion.1), channel_id=1, source_target_pairs={{0,704},{64,0},{128,64},{192,128},{256,192},{320,256},{384,320},{4... | collective-permute-start | bytes 921608 | tf_op jit(solution)/shard_map/ppermute | solution.py:107
  47.7 11.4 %collective-permute-start.3 = (bf16[640,240]{1,0:T(8,128)(2,1)S(1)}, bf16[640,240]{1,0:T(8,128)(2,1)S(1)}, u32[]{:S(2)}, u32[]{:S(2)}) collective-permute-start(bf16[640,240]{1,0:T(8,128)(2,1)S(1)} %collective-permute-done.1), channel_id=1, source_target_pairs={{0,64},{64,128},{128,192},{192,256},{256,320},{320,384},{384,448},... | collective-permute-start | bytes 921608 | tf_op jit(solution)/shard_map/ppermute | solution.py:104
  49.7 11.4 %collective-permute-start.4 = (bf16[640,240]{1,0:T(8,128)(2,1)S(1)}, bf16[640,240]{1,0:T(8,128)(2,1)S(1)}, u32[]{:S(2)}, u32[]{:S(2)}) collective-permute-start(bf16[640,240]{1,0:T(8,128)(2,1)S(1)} %collective-permute-done.2), channel_id=1, source_target_pairs={{0,704},{64,0},{128,64},{192,128},{256,192},{320,256},{384,320},{4... | collective-permute-start | bytes 921608 | tf_op jit(solution)/shard_map/ppermute | solution.py:107
  59.1 10.4 %collective-permute-start.5 = (bf16[640,240]{1,0:T(8,128)(2,1)S(1)}, bf16[640,240]{1,0:T(8,128)(2,1)S(1)}, u32[]{:S(2)}, u32[]{:S(2)}) collective-permute-start(bf16[640,240]{1,0:T(8,128)(2,1)S(1)} %collective-permute-done.3), channel_id=1, source_target_pairs={{0,64},{64,128},{128,192},{192,256},{256,320},{320,384},{384,448},... | collective-permute-start | bytes 921608 | tf_op jit(solution)/shard_map/ppermute | solution.py:104
  61.0 10.4 %collective-permute-start.6 = (bf16[640,240]{1,0:T(8,128)(2,1)S(1)}, bf16[640,240]{1,0:T(8,128)(2,1)S(1)}, u32[]{:S(2)}, u32[]{:S(2)}) collective-permute-start(bf16[640,240]{1,0:T(8,128)(2,1)S(1)} %collective-permute-done.4), channel_id=1, source_target_pairs={{0,704},{64,0},{128,64},{192,128},{256,192},{320,256},{384,320},{4... | collective-permute-start | bytes 921608 | tf_op jit(solution)/shard_map/ppermute | solution.py:107
  69.6 10.2 %collective-permute-start.7 = (bf16[640,240]{1,0:T(8,128)(2,1)S(1)}, bf16[640,240]{1,0:T(8,128)(2,1)S(1)}, u32[]{:S(2)}, u32[]{:S(2)}) collective-permute-start(bf16[640,240]{1,0:T(8,128)(2,1)S(1)} %collective-permute-done.5), channel_id=1, source_target_pairs={{0,64},{64,128},{128,192},{192,256},{256,320},{320,384},{384,448},... | collective-permute-start | bytes 921608 | tf_op jit(solution)/shard_map/ppermute | solution.py:104
  71.5 10.2 %collective-permute-start.8 = (bf16[640,240]{1,0:T(8,128)(2,1)S(1)}, bf16[640,240]{1,0:T(8,128)(2,1)S(1)}, u32[]{:S(2)}, u32[]{:S(2)}) collective-permute-start(bf16[640,240]{1,0:T(8,128)(2,1)S(1)} %collective-permute-done.6), channel_id=1, source_target_pairs={{0,704},{64,0},{128,64},{192,128},{256,192},{320,256},{384,320},{4... | collective-permute-start | bytes 921608 | tf_op jit(solution)/shard_map/ppermute | solution.py:107
  79.7 10.2 %collective-permute-start.9 = (bf16[640,240]{1,0:T(8,128)(2,1)S(1)}, bf16[640,240]{1,0:T(8,128)(2,1)S(1)}, u32[]{:S(2)}, u32[]{:S(2)}) collective-permute-start(bf16[640,240]{1,0:T(8,128)(2,1)S(1)} %collective-permute-done.7), channel_id=1, source_target_pairs={{0,64},{64,128},{128,192},{192,256},{256,320},{320,384},{384,448},... | collective-permute-start | bytes 921608 | tf_op jit(solution)/shard_map/ppermute | solution.py:104
  81.7 10.9 %collective-permute-start.10 = (bf16[640,240]{1,0:T(8,128)(2,1)S(1)}, bf16[640,240]{1,0:T(8,128)(2,1)S(1)}, u32[]{:S(2)}, u32[]{:S(2)}) collective-permute-start(bf16[640,240]{1,0:T(8,128)(2,1)S(1)} %collective-permute-done.8), channel_id=1, source_target_pairs={{0,704},{64,0},{128,64},{192,128},{256,192},{320,256},{384,320},{4... | collective-permute-start | bytes 921608 | tf_op jit(solution)/shard_map/ppermute | solution.py:107
  89.9 10.2 %collective-permute-start.11 = (bf16[640,240]{1,0:T(8,128)(2,1)S(1)}, bf16[640,240]{1,0:T(8,128)(2,1)S(1)}, u32[]{:S(2)}, u32[]{:S(2)}) collective-permute-start(bf16[640,240]{1,0:T(8,128)(2,1)S(1)} %collective-permute-done.9), channel_id=1, source_target_pairs={{0,64},{64,128},{128,192},{192,256},{256,320},{320,384},{384,448},... | collective-permute-start | bytes 921608 | tf_op jit(solution)/shard_map/ppermute | solution.py:104
Sparse Core Ops, SparseCore 0:
  11.0 75.1 all-gather.2

commit v9 on v8

--- a/solution.py
+++ b/solution.py
@@ -100,7 +100,17 @@
     backward = [(i, (i - 1) % depth) for i in range(depth)]
     ahead = pair
     behind = pair
-    for step in range(1, depth // 2 + 1):
+    last = depth // 2
+    split = depth % 2 == 0
+    for step in range(1, last + 1):
+        if split and step == last:
+            rows = masked.shape[0]
+            top = lax.ppermute(ahead[:rows], "row_0", forward)
+            bottom = lax.ppermute(behind[rows:], "row_0", backward)
+            at = (here - step) % depth
+            slab = lax.dynamic_update_slice(slab, top[None], (at, 0, 0))
+            slab = lax.dynamic_update_slice(slab, bottom[None], (at, rows, 0))
+            continue
         ahead = lax.ppermute(ahead, "row_0", forward)
         slab = lax.dynamic_update_index_in_dim(slab, ahead, (here - step) % depth, 0)
         if step < depth - depth // 2:

time: 172 us -> 174 us (1.012)
  waiting for transfers between devices: 25.8 us -> 19.6 us
  starting transfers between devices: 49.5 us -> 54.7 us
  blocking collectives: 57.3 us -> 60 us
    ppermute x0 -> x2, starting transfers between devices: none -> 7.05 us  [the longest x1 5.13 us: column_slab(): bottom = lax.ppermute(behind[rows:], 'row_0', backward)]
    ppermute x6 -> x5, waiting for transfers between devices: 15.8 us -> 8.94 us  [column_slab(): ahead = lax.ppermute(ahead, 'row_0', forward)]
    psum x5, blocking collectives: 57.3 us -> 60 us  [on_device(): traces = lax.psum(traces, axis)]
    ppermute x6 -> x5, starting transfers between devices: 13.8 us -> 11.9 us  [column_slab(): ahead = lax.ppermute(ahead, 'row_0', forward)]
    dynamic_update_slice x6 -> x5, local copies, waits for them, and re-layouts: 4.62 us -> 3.9 us  [column_slab(): lax.dynamic_update_index_in_dim(slab, ahead, (here - step) % depth, 0)]
  transfers between devices with their start and end apart: 13 -> 14, of which waited for: 7 -> 7; matrix products, arithmetic and copies ran while one was open for 9% -> 9% of each run, Pallas kernels for 0% -> 0%
where the time goes in v9:
time: 174 us; the launch traced here: 173 us
  blocking collectives  60 us (34%)
  starting transfers between devices  54.7 us (31%)
  waiting for transfers between devices  19.6 us (11%)
  between operations  14.5 us (8%)
  local copies, waits for them, and re-layouts  11.5 us (7%)
  other arithmetic  7.04 us (4%)
  Pallas kernels  5.91 us (3%)
    psum x5, blocking collectives, on_device(): traces = lax.psum(traces, axis)  60 us
    ppermute x5, starting transfers between devices, column_slab(): behind = lax.ppermute(behind, 'row_0', backward)  32.8 us
    ppermute x5, starting transfers between devices, column_slab(): ahead = lax.ppermute(ahead, 'row_0', forward)  11.9 us
    ppermute x1, waiting for transfers between devices, column_slab(): other = lax.ppermute(masked, 'row_1', [(0, 1), (1, 0)])  10 us
    ppermute x5, waiting for transfers between devices, column_slab(): ahead = lax.ppermute(ahead, 'row_0', forward)  8.94 us
    pallas_call x1, Pallas kernels, panel_product(): pl.pallas_call(panel_kernel, out_shape=(jax.ShapeDtypeStruct((tile_rows,...  5.91 us
    ppermute x1, starting transfers between devices, column_slab(): bottom = lax.ppermute(behind[rows:], 'row_0', backward)  5.13 us
    dynamic_update_slice x5, local copies, waits for them, and re-layouts, column_slab(): lax.dynamic_update_index_in_dim(slab, ahead, (here - step) % depth, 0)  3.9 us
  transfers between devices with their start and end apart: 14, of which 7 were waited for; matrix products, arithmetic and copies ran while one was open for 9% of the time, Pallas kernels for 0%

profile of v9, /device:TPU:40, one launch (start us, length us, event | category | flops | bytes accessed | tf_op | source)
XLA Modules:
  0.0 173.3 jit_solution(3217923705663259837)
XLA Ops:
  7.3 0.9 shift-left_reduce_fusion
  8.2 0.1 broadcast_in_dim.52
  8.3 0.1 shift_right_arithmetic.15
  8.3 1.7 fusion.2
  10.1 2.9 %collective-permute-start = (bf16[320,240]{1,0:T(8,128)(2,1)}, bf16[320,240]{1,0:T(8,128)(2,1)S(1)}, u32[]{:S(2)}, u32[]{:S(2)}) collective-permute-start(bf16[320,240]{1,0:T(8,128)(2,1)} %fusion.2), channel_id=1, source_target_pairs={{0,32},{32,0},{1,33},{33,1},{2,34},{34,2},{3,35},{35,3},{4,36},{36... | collective-permute-start | bytes 460808 | tf_op jit(solution)/shard_map/ppermute | solution.py:90
  13.0 1.0 fusion.6
  14.3 0.6 pad_add_fusion.place_ref
  14.9 10.0 %collective-permute-done = bf16[320,240]{1,0:T(8,128)(2,1)S(1)} collective-permute-done((bf16[320,240]{1,0:T(8,128)(2,1)}, bf16[320,240]{1,0:T(8,128)(2,1)S(1)}, u32[]{:S(2)}, u32[]{:S(2)}) %collective-permute-start) | collective-permute-done | bytes 153632 | tf_op jit(solution)/shard_map/ppermute | solution.py:90
  24.9 1.1 maximum_select_fusion.1
  26.0 4.3 %collective-permute-start.1 = (bf16[640,240]{1,0:T(8,128)(2,1)S(1)}, bf16[640,240]{1,0:T(8,128)(2,1)S(1)}, u32[]{:S(2)}, u32[]{:S(2)}) collective-permute-start(bf16[640,240]{1,0:T(8,128)(2,1)S(1)} %maximum_select_fusion.1), channel_id=1, source_target_pairs={{0,64},{64,128},{128,192},{192,256},{256,320},{320,384},{384,448},... | collective-permute-start | bytes 921608 | tf_op jit(solution)/shard_map/ppermute | solution.py:114
  30.3 12.2 %collective-permute-start.2 = (bf16[640,240]{1,0:T(8,128)(2,1)S(1)}, bf16[640,240]{1,0:T(8,128)(2,1)S(1)}, u32[]{:S(2)}, u32[]{:S(2)}) collective-permute-start(bf16[640,240]{1,0:T(8,128)(2,1)S(1)} %maximum_select_fusion.1), channel_id=1, source_target_pairs={{0,704},{64,0},{128,64},{192,128},{256,192},{320,256},{384,320},{4... | collective-permute-start | bytes 921608 | tf_op jit(solution)/shard_map/ppermute | solution.py:117
  42.5 0.9 fusion.1.keep_ref
  43.4 2.3 %broadcast_in_dim.54 = bf16[12,640,240]{2,1,0:T(8,128)(2,1)} broadcast(bf16[]{:T(256)} %constant.129.clone.1), dimensions={} | broadcast | bytes 3686402 | tf_op jit(solution)/shard_map/broadcast_in_dim | solution.py:97
  45.7 0.8 fusion
  46.5 1.3 collective-permute-done.1
  47.7 1.9 %collective-permute-start.3 = (bf16[640,240]{1,0:T(8,128)(2,1)S(1)}, bf16[640,240]{1,0:T(8,128)(2,1)S(1)}, u32[]{:S(2)}, u32[]{:S(2)}) collective-permute-start(bf16[640,240]{1,0:T(8,128)(2,1)S(1)} %collective-permute-done.1), channel_id=1, source_target_pairs={{0,64},{64,128},{128,192},{192,256},{256,320},{320,384},{384,448},... | collective-permute-start | bytes 921608 | tf_op jit(solution)/shard_map/ppermute | solution.py:114
  49.7 5.1 %collective-permute-start.4 = (bf16[640,240]{1,0:T(8,128)(2,1)S(1)}, bf16[640,240]{1,0:T(8,128)(2,1)S(1)}, u32[]{:S(2)}, u32[]{:S(2)}) collective-permute-start(bf16[640,240]{1,0:T(8,128)(2,1)S(1)} %collective-permute-done.2), channel_id=1, source_target_pairs={{0,704},{64,0},{128,64},{192,128},{256,192},{320,256},{384,320},{4... | collective-permute-start | bytes 921608 | tf_op jit(solution)/shard_map/ppermute | solution.py:117
  54.8 0.8 bitcast_dynamic-update-slice_fusion.9
  55.6 0.8 bitcast_dynamic-update-slice_fusion.8
  56.4 2.8 %collective-permute-done.3 = bf16[640,240]{1,0:T(8,128)(2,1)S(1)} collective-permute-done((bf16[640,240]{1,0:T(8,128)(2,1)S(1)}, bf16[640,240]{1,0:T(8,128)(2,1)S(1)}, u32[]{:S(2)}, u32[]{:S(2)}) %collective-permute-start.3) | collective-permute-done | bytes 307232 | tf_op jit(solution)/shard_map/ppermute | solution.py:114
  59.1 1.9 %collective-permute-start.5 = (bf16[640,240]{1,0:T(8,128)(2,1)S(1)}, bf16[640,240]{1,0:T(8,128)(2,1)S(1)}, u32[]{:S(2)}, u32[]{:S(2)}) collective-permute-start(bf16[640,240]{1,0:T(8,128)(2,1)S(1)} %collective-permute-done.3), channel_id=1, source_target_pairs={{0,64},{64,128},{128,192},{192,256},{256,320},{320,384},{384,448},... | collective-permute-start | bytes 921608 | tf_op jit(solution)/shard_map/ppermute | solution.py:114
  61.0 5.1 %collective-permute-start.6 = (bf16[640,240]{1,0:T(8,128)(2,1)S(1)}, bf16[640,240]{1,0:T(8,128)(2,1)S(1)}, u32[]{:S(2)}, u32[]{:S(2)}) collective-permute-start(bf16[640,240]{1,0:T(8,128)(2,1)S(1)} %collective-permute-done.4), channel_id=1, source_target_pairs={{0,704},{64,0},{128,64},{192,128},{256,192},{320,256},{384,320},{4... | collective-permute-start | bytes 921608 | tf_op jit(solution)/shard_map/ppermute | solution.py:117
  66.2 0.8 bitcast_dynamic-update-slice_fusion.7
  67.0 0.8 bitcast_dynamic-update-slice_fusion.6
  67.7 1.8 %collective-permute-done.5 = bf16[640,240]{1,0:T(8,128)(2,1)S(1)} collective-permute-done((bf16[640,240]{1,0:T(8,128)(2,1)S(1)}, bf16[640,240]{1,0:T(8,128)(2,1)S(1)}, u32[]{:S(2)}, u32[]{:S(2)}) %collective-permute-start.5) | collective-permute-done | bytes 307232 | tf_op jit(solution)/shard_map/ppermute | solution.py:114
  69.6 1.9 %collective-permute-start.7 = (bf16[640,240]{1,0:T(8,128)(2,1)S(1)}, bf16[640,240]{1,0:T(8,128)(2,1)S(1)}, u32[]{:S(2)}, u32[]{:S(2)}) collective-permute-start(bf16[640,240]{1,0:T(8,128)(2,1)S(1)} %collective-permute-done.5), channel_id=1, source_target_pairs={{0,64},{64,128},{128,192},{192,256},{256,320},{320,384},{384,448},... | collective-permute-start | bytes 921608 | tf_op jit(solution)/shard_map/ppermute | solution.py:114
  71.5 5.1 %collective-permute-start.8 = (bf16[640,240]{1,0:T(8,128)(2,1)S(1)}, bf16[640,240]{1,0:T(8,128)(2,1)S(1)}, u32[]{:S(2)}, u32[]{:S(2)}) collective-permute-start(bf16[640,240]{1,0:T(8,128)(2,1)S(1)} %collective-permute-done.6), channel_id=1, source_target_pairs={{0,704},{64,0},{128,64},{192,128},{256,192},{320,256},{384,320},{4... | collective-permute-start | bytes 921608 | tf_op jit(solution)/shard_map/ppermute | solution.py:117
  76.6 0.8 bitcast_dynamic-update-slice_fusion.5
  77.4 0.8 bitcast_dynamic-update-slice_fusion.4
  78.2 1.5 collective-permute-done.7
  79.7 1.9 %collective-permute-start.9 = (bf16[640,240]{1,0:T(8,128)(2,1)S(1)}, bf16[640,240]{1,0:T(8,128)(2,1)S(1)}, u32[]{:S(2)}, u32[]{:S(2)}) collective-permute-start(bf16[640,240]{1,0:T(8,128)(2,1)S(1)} %collective-permute-done.7), channel_id=1, source_target_pairs={{0,64},{64,128},{128,192},{192,256},{256,320},{320,384},{384,448},... | collective-permute-start | bytes 921608 | tf_op jit(solution)/shard_map/ppermute | solution.py:114
  81.7 5.1 %collective-permute-start.10 = (bf16[640,240]{1,0:T(8,128)(2,1)S(1)}, bf16[640,240]{1,0:T(8,128)(2,1)S(1)}, u32[]{:S(2)}, u32[]{:S(2)}) collective-permute-start(bf16[640,240]{1,0:T(8,128)(2,1)S(1)} %collective-permute-done.8), channel_id=1, source_target_pairs={{0,704},{64,0},{128,64},{192,128},{256,192},{320,256},{384,320},{4... | collective-permute-start | bytes 921608 | tf_op jit(solution)/shard_map/ppermute | solution.py:117
  86.8 0.8 bitcast_dynamic-update-slice_fusion.3
  87.6 0.8 bitcast_dynamic-update-slice_fusion.2
  88.3 1.6 collective-permute-done.9
  89.9 1.9 %collective-permute-start.11 = (bf16[320,240]{1,0:T(8,128)(2,1)S(1)}, bf16[320,240]{1,0:T(8,128)(2,1)S(1)}, u32[]{:S(2)}, u32[]{:S(2)}) collective-permute-start(bf16[320,240]{1,0:T(8,128)(2,1)S(1)} %slice.8), channel_id=1, source_target_pairs={{0,64},{64,128},{128,192},{192,256},{256,320},{320,384},{384,448},... | collective-permute-start | bytes 460808 | tf_op jit(solution)/shard_map/ppermute | solution.py:108
  91.9 5.1 %collective-permute-start.12 = (bf16[320,240]{1,0:T(8,128)(2,1)S(1)}, bf16[320,240]{1,0:T(8,128)(2,1)S(1)}, u32[]{:S(2)}, u32[]{:S(2)}) collective-permute-start(bf16[320,240]{1,0:T(8,128)(2,1)S(1)} %slice.9), channel_id=1, source_target_pairs={{0,704},{64,0},{128,64},{192,128},{256,192},{320,256},{384,320},{4... | collective-permute-start | bytes 460808 | tf_op jit(solution)/shard_map/ppermute | solution.py:109
  97.0 0.7 bitcast_dynamic-update-slice_fusion.1
  97.7 0.8 bitcast_dynamic-update-slice_fusion
  98.5 0.7 bitcast_dynamic-update-slice_fusion.11
  99.2 0.6 collective-permute-done.12
  99.8 0.7 bitcast_dynamic-update-slice_fusion.10
  100.5 5.9 %shard_map.41 = (bf16[320,240]{1,0:T(8,128)(2,1)}, f32[2]{0:T(128)}) custom-call(s32[3]{0:T(128)} %pad_add_fusion.place_ref, bf16[32,320,240]{2,1,0:T(8,128)(2,1)} %bitcast.31, bf16[7680,240]{1,0:T(8,128)(2,1)} %bitcast.17.right_ref, s32[320,240]{1,0:T(8,128)} %fusion.1.keep_ref), custom_call_target="tpu_custom_call" | custom-call | flops 1179648000 | bytes 9062400 | tf_op jit(solution)/shard_map/pallas_call | solution.py:70
  106.4 2.6 %psum.35 = f32[2]{0:T(128)S(1)} all-reduce(f32[2]{0:T(128)} %get-tuple-element.5), channel_id=1, replica_groups=mesh['row_0'=12,'row_1'=2,'col_0'=4,'col_1'=4,'col_2'=2] {'col_2'}, use_global_device_ids=true, to_apply=%region_1.2 | all-reduce | flops 2 | bytes 16 | tf_op jit(solution)/shard_map/psum | solution.py:138
  109.0 13.3 %psum.36 = f32[2]{0:T(128)S(1)} all-reduce(f32[2]{0:T(128)S(1)} %psum.35), channel_id=1, replica_groups=mesh['row_0'=12,'row_1'=2,'col_0'=4,'col_1'=4,'col_2'=2] {'col_1'}, use_global_device_ids=true, to_apply=%region_2.3 | all-reduce | flops 2 | bytes 16 | tf_op jit(solution)/shard_map/psum | solution.py:138
  122.4 10.5 %psum.37 = f32[2]{0:T(128)S(1)} all-reduce(f32[2]{0:T(128)S(1)} %psum.36), channel_id=1, replica_groups=mesh['row_0'=12,'row_1'=2,'col_0'=4,'col_1'=4,'col_2'=2] {'col_0'}, use_global_device_ids=true, to_apply=%region_3.4 | all-reduce | flops 2 | bytes 16 | tf_op jit(solution)/shard_map/psum | solution.py:138
  132.9 8.8 %psum.38 = f32[2]{0:T(128)S(1)} all-reduce(f32[2]{0:T(128)S(1)} %psum.37), channel_id=1, replica_groups=mesh['row_0'=12,'row_1'=2,'col_0'=4,'col_1'=4,'col_2'=2] {'row_1'}, use_global_device_ids=true, to_apply=%region_4.5 | all-reduce | flops 2 | bytes 16 | tf_op jit(solution)/shard_map/psum | solution.py:138
  141.7 24.8 %psum.39 = f32[2]{0:T(128)} all-reduce(f32[2]{0:T(128)S(1)} %psum.38), channel_id=1, replica_groups=mesh['row_0'=12,'row_1'=2,'col_0'=4,'col_1'=4,'col_2'=2] {'row_0'}, use_global_device_ids=true, to_apply=%region_5.6 | all-reduce | flops 2 | bytes 16 | tf_op jit(solution)/shard_map/psum | solution.py:138
  (13 shorter events, 0.1 us)
Async XLA Ops:
  7.2 93.3 %all-gather.3.cloned.1.call-start = ((), (), s32[]{:S(2)}) async-start(), calls=%async_computation | async-start | bytes 5406720 | tf_op jit(solution)/shard_map/all_gather | solution.py:130
  10.1 14.8 %collective-permute-start = (bf16[320,240]{1,0:T(8,128)(2,1)}, bf16[320,240]{1,0:T(8,128)(2,1)S(1)}, u32[]{:S(2)}, u32[]{:S(2)}) collective-permute-start(bf16[320,240]{1,0:T(8,128)(2,1)} %fusion.2), channel_id=1, source_target_pairs={{0,32},{32,0},{1,33},{33,1},{2,34},{34,2},{3,35},{35,3},{4,36},{36... | collective-permute-start | bytes 460808 | tf_op jit(solution)/shard_map/ppermute | solution.py:90
  26.0 21.7 %collective-permute-start.1 = (bf16[640,240]{1,0:T(8,128)(2,1)S(1)}, bf16[640,240]{1,0:T(8,128)(2,1)S(1)}, u32[]{:S(2)}, u32[]{:S(2)}) collective-permute-start(bf16[640,240]{1,0:T(8,128)(2,1)S(1)} %maximum_select_fusion.1), channel_id=1, source_target_pairs={{0,64},{64,128},{128,192},{192,256},{256,320},{320,384},{384,448},... | collective-permute-start | bytes 921608 | tf_op jit(solution)/shard_map/ppermute | solution.py:114
  30.3 19.4 %collective-permute-start.2 = (bf16[640,240]{1,0:T(8,128)(2,1)S(1)}, bf16[640,240]{1,0:T(8,128)(2,1)S(1)}, u32[]{:S(2)}, u32[]{:S(2)}) collective-permute-start(bf16[640,240]{1,0:T(8,128)(2,1)S(1)} %maximum_select_fusion.1), channel_id=1, source_target_pairs={{0,704},{64,0},{128,64},{192,128},{256,192},{320,256},{384,320},{4... | collective-permute-start | bytes 921608 | tf_op jit(solution)/shard_map/ppermute | solution.py:117
  47.7 11.4 %collective-permute-start.3 = (bf16[640,240]{1,0:T(8,128)(2,1)S(1)}, bf16[640,240]{1,0:T(8,128)(2,1)S(1)}, u32[]{:S(2)}, u32[]{:S(2)}) collective-permute-start(bf16[640,240]{1,0:T(8,128)(2,1)S(1)} %collective-permute-done.1), channel_id=1, source_target_pairs={{0,64},{64,128},{128,192},{192,256},{256,320},{320,384},{384,448},... | collective-permute-start | bytes 921608 | tf_op jit(solution)/shard_map/ppermute | solution.py:114
  49.7 11.4 %collective-permute-start.4 = (bf16[640,240]{1,0:T(8,128)(2,1)S(1)}, bf16[640,240]{1,0:T(8,128)(2,1)S(1)}, u32[]{:S(2)}, u32[]{:S(2)}) collective-permute-start(bf16[640,240]{1,0:T(8,128)(2,1)S(1)} %collective-permute-done.2), channel_id=1, source_target_pairs={{0,704},{64,0},{128,64},{192,128},{256,192},{320,256},{384,320},{4... | collective-permute-start | bytes 921608 | tf_op jit(solution)/shard_map/ppermute | solution.py:117
  59.1 10.4 %collective-permute-start.5 = (bf16[640,240]{1,0:T(8,128)(2,1)S(1)}, bf16[640,240]{1,0:T(8,128)(2,1)S(1)}, u32[]{:S(2)}, u32[]{:S(2)}) collective-permute-start(bf16[640,240]{1,0:T(8,128)(2,1)S(1)} %collective-permute-done.3), channel_id=1, source_target_pairs={{0,64},{64,128},{128,192},{192,256},{256,320},{320,384},{384,448},... | collective-permute-start | bytes 921608 | tf_op jit(solution)/shard_map/ppermute | solution.py:114
  61.0 10.4 %collective-permute-start.6 = (bf16[640,240]{1,0:T(8,128)(2,1)S(1)}, bf16[640,240]{1,0:T(8,128)(2,1)S(1)}, u32[]{:S(2)}, u32[]{:S(2)}) collective-permute-start(bf16[640,240]{1,0:T(8,128)(2,1)S(1)} %collective-permute-done.4), channel_id=1, source_target_pairs={{0,704},{64,0},{128,64},{192,128},{256,192},{320,256},{384,320},{4... | collective-permute-start | bytes 921608 | tf_op jit(solution)/shard_map/ppermute | solution.py:117
  69.6 10.2 %collective-permute-start.7 = (bf16[640,240]{1,0:T(8,128)(2,1)S(1)}, bf16[640,240]{1,0:T(8,128)(2,1)S(1)}, u32[]{:S(2)}, u32[]{:S(2)}) collective-permute-start(bf16[640,240]{1,0:T(8,128)(2,1)S(1)} %collective-permute-done.5), channel_id=1, source_target_pairs={{0,64},{64,128},{128,192},{192,256},{256,320},{320,384},{384,448},... | collective-permute-start | bytes 921608 | tf_op jit(solution)/shard_map/ppermute | solution.py:114
  71.5 10.2 %collective-permute-start.8 = (bf16[640,240]{1,0:T(8,128)(2,1)S(1)}, bf16[640,240]{1,0:T(8,128)(2,1)S(1)}, u32[]{:S(2)}, u32[]{:S(2)}) collective-permute-start(bf16[640,240]{1,0:T(8,128)(2,1)S(1)} %collective-permute-done.6), channel_id=1, source_target_pairs={{0,704},{64,0},{128,64},{192,128},{256,192},{320,256},{384,320},{4... | collective-permute-start | bytes 921608 | tf_op jit(solution)/shard_map/ppermute | solution.py:117
  79.7 10.2 %collective-permute-start.9 = (bf16[640,240]{1,0:T(8,128)(2,1)S(1)}, bf16[640,240]{1,0:T(8,128)(2,1)S(1)}, u32[]{:S(2)}, u32[]{:S(2)}) collective-permute-start(bf16[640,240]{1,0:T(8,128)(2,1)S(1)} %collective-permute-done.7), channel_id=1, source_target_pairs={{0,64},{64,128},{128,192},{192,256},{256,320},{320,384},{384,448},... | collective-permute-start | bytes 921608 | tf_op jit(solution)/shard_map/ppermute | solution.py:114
  81.7 10.2 %collective-permute-start.10 = (bf16[640,240]{1,0:T(8,128)(2,1)S(1)}, bf16[640,240]{1,0:T(8,128)(2,1)S(1)}, u32[]{:S(2)}, u32[]{:S(2)}) collective-permute-start(bf16[640,240]{1,0:T(8,128)(2,1)S(1)} %collective-permute-done.8), channel_id=1, source_target_pairs={{0,704},{64,0},{128,64},{192,128},{256,192},{320,256},{384,320},{4... | collective-permute-start | bytes 921608 | tf_op jit(solution)/shard_map/ppermute | solution.py:117
  89.9 8.6 %collective-permute-start.11 = (bf16[320,240]{1,0:T(8,128)(2,1)S(1)}, bf16[320,240]{1,0:T(8,128)(2,1)S(1)}, u32[]{:S(2)}, u32[]{:S(2)}) collective-permute-start(bf16[320,240]{1,0:T(8,128)(2,1)S(1)} %slice.8), channel_id=1, source_target_pairs={{0,64},{64,128},{128,192},{192,256},{256,320},{320,384},{384,448},... | collective-permute-start | bytes 460808 | tf_op jit(solution)/shard_map/ppermute | solution.py:108
  91.9 8.0 %collective-permute-start.12 = (bf16[320,240]{1,0:T(8,128)(2,1)S(1)}, bf16[320,240]{1,0:T(8,128)(2,1)S(1)}, u32[]{:S(2)}, u32[]{:S(2)}) collective-permute-start(bf16[320,240]{1,0:T(8,128)(2,1)S(1)} %slice.9), channel_id=1, source_target_pairs={{0,704},{64,0},{128,64},{192,128},{256,192},{320,256},{384,320},{4... | collective-permute-start | bytes 460808 | tf_op jit(solution)/shard_map/ppermute | solution.py:109
Sparse Core Ops, SparseCore 0:
  11.0 75.2 all-gather.2

commit v10 on v8

--- a/solution.py
+++ b/solution.py
@@ -101,11 +101,11 @@
     ahead = pair
     behind = pair
     for step in range(1, depth // 2 + 1):
-        ahead = lax.ppermute(ahead, "row_0", forward)
-        slab = lax.dynamic_update_index_in_dim(slab, ahead, (here - step) % depth, 0)
         if step < depth - depth // 2:
             behind = lax.ppermute(behind, "row_0", backward)
             slab = lax.dynamic_update_index_in_dim(slab, behind, (here + step) % depth, 0)
+        ahead = lax.ppermute(ahead, "row_0", forward)
+        slab = lax.dynamic_update_index_in_dim(slab, ahead, (here - step) % depth, 0)
     return slab.reshape(depth * pair.shape[0], pair.shape[1])
 
 

time: 172 us -> 178 us (1.035)
  waiting for transfers between devices: 25.8 us -> 28.8 us
  starting transfers between devices: 49.5 us -> 51.4 us
  blocking collectives: 57.3 us -> 59.1 us
    ppermute x5, waiting for transfers between devices: 0.01 us -> 4.69 us  [column_slab(): behind = lax.ppermute(behind, 'row_0', backward)]
    ppermute x5, starting transfers between devices: 32.8 us -> 36.9 us  [column_slab(): behind = lax.ppermute(behind, 'row_0', backward)]
    ppermute x6, starting transfers between devices: 13.8 us -> 11.5 us  [column_slab(): ahead = lax.ppermute(ahead, 'row_0', forward)]
where the time goes in v10:
time: 178 us; the launch traced here: 177 us
  blocking collectives  59.1 us (33%)
  starting transfers between devices  51.4 us (29%)
  waiting for transfers between devices  28.8 us (16%)
  between operations  14.5 us (8%)
  local copies, waits for them, and re-layouts  10.8 us (6%)
  other arithmetic  7.08 us (4%)
  Pallas kernels  5.91 us (3%)
    psum x5, blocking collectives, on_device(): traces = lax.psum(traces, axis)  59.1 us
    ppermute x5, starting transfers between devices, column_slab(): behind = lax.ppermute(behind, 'row_0', backward)  36.9 us
    ppermute x6, waiting for transfers between devices, column_slab(): ahead = lax.ppermute(ahead, 'row_0', forward)  14.1 us
    ppermute x6, starting transfers between devices, column_slab(): ahead = lax.ppermute(ahead, 'row_0', forward)  11.5 us
    ppermute x1, waiting for transfers between devices, column_slab(): other = lax.ppermute(masked, 'row_1', [(0, 1), (1, 0)])  9.99 us
    pallas_call x1, Pallas kernels, panel_product(): pl.pallas_call(panel_kernel, out_shape=(jax.ShapeDtypeStruct((tile_rows,...  5.91 us
    ppermute x5, waiting for transfers between devices, column_slab(): behind = lax.ppermute(behind, 'row_0', backward)  4.69 us
    dynamic_update_slice x6, local copies, waits for them, and re-layouts, column_slab(): lax.dynamic_update_index_in_dim(slab, ahead, (here - step) % depth, 0)  4.59 us
  transfers between devices with their start and end apart: 13, of which 7 were waited for; matrix products, arithmetic and copies ran while one was open for 9% of the time, Pallas kernels for 0%

profile of v10, /device:TPU:40, one launch (start us, length us, event | category | flops | bytes accessed | tf_op | source)
XLA Modules:
  0.0 177.5 jit_solution(2899288466938717876)
XLA Ops:
  7.2 0.0 all-gather.3.cloned.1.call-start
  7.3 0.9 shift-left_reduce_fusion
  8.2 0.1 broadcast_in_dim.49
  8.3 0.1 shift_right_arithmetic.15
  8.3 1.7 fusion.2
  10.1 2.9 %collective-permute-start = (bf16[320,240]{1,0:T(8,128)(2,1)}, bf16[320,240]{1,0:T(8,128)(2,1)S(1)}, u32[]{:S(2)}, u32[]{:S(2)}) collective-permute-start(bf16[320,240]{1,0:T(8,128)(2,1)} %fusion.2), channel_id=1, source_target_pairs={{0,32},{32,0},{1,33},{33,1},{2,34},{34,2},{3,35},{35,3},{4,36},{36... | collective-permute-start | bytes 460808 | tf_op jit(solution)/shard_map/ppermute | solution.py:90
  13.0 1.0 fusion.6
  14.3 0.6 pad_add_fusion.place_ref
  14.9 10.0 %collective-permute-done = bf16[320,240]{1,0:T(8,128)(2,1)S(1)} collective-permute-done((bf16[320,240]{1,0:T(8,128)(2,1)}, bf16[320,240]{1,0:T(8,128)(2,1)S(1)}, u32[]{:S(2)}, u32[]{:S(2)}) %collective-permute-start) | collective-permute-done | bytes 153632 | tf_op jit(solution)/shard_map/ppermute | solution.py:90
  24.9 1.1 maximum_select_fusion.1
  26.0 14.6 %collective-permute-start.1 = (bf16[640,240]{1,0:T(8,128)(2,1)S(1)}, bf16[640,240]{1,0:T(8,128)(2,1)S(1)}, u32[]{:S(2)}, u32[]{:S(2)}) collective-permute-start(bf16[640,240]{1,0:T(8,128)(2,1)S(1)} %maximum_select_fusion.1), channel_id=1, source_target_pairs={{0,704},{64,0},{128,64},{192,128},{256,192},{320,256},{384,320},{4... | collective-permute-start | bytes 921608 | tf_op jit(solution)/shard_map/ppermute | solution.py:105
  40.6 1.9 %collective-permute-start.2 = (bf16[640,240]{1,0:T(8,128)(2,1)S(1)}, bf16[640,240]{1,0:T(8,128)(2,1)S(1)}, u32[]{:S(2)}, u32[]{:S(2)}) collective-permute-start(bf16[640,240]{1,0:T(8,128)(2,1)S(1)} %maximum_select_fusion.1), channel_id=1, source_target_pairs={{0,64},{64,128},{128,192},{192,256},{256,320},{320,384},{384,448},... | collective-permute-start | bytes 921608 | tf_op jit(solution)/shard_map/ppermute | solution.py:107
  42.5 0.9 fusion.1.keep_ref
  43.4 2.3 %broadcast_in_dim.51 = bf16[12,640,240]{2,1,0:T(8,128)(2,1)} broadcast(bf16[]{:T(256)} %constant.131.clone.1), dimensions={} | broadcast | bytes 3686402 | tf_op jit(solution)/shard_map/broadcast_in_dim | solution.py:97
  45.7 0.8 fusion
  46.5 0.5 collective-permute-done.1
  47.0 5.6 %collective-permute-start.3 = (bf16[640,240]{1,0:T(8,128)(2,1)S(1)}, bf16[640,240]{1,0:T(8,128)(2,1)S(1)}, u32[]{:S(2)}, u32[]{:S(2)}) collective-permute-start(bf16[640,240]{1,0:T(8,128)(2,1)S(1)} %collective-permute-done.1), channel_id=1, source_target_pairs={{0,704},{64,0},{128,64},{192,128},{256,192},{320,256},{384,320},{4... | collective-permute-start | bytes 921608 | tf_op jit(solution)/shard_map/ppermute | solution.py:105
  52.6 1.9 %collective-permute-start.4 = (bf16[640,240]{1,0:T(8,128)(2,1)S(1)}, bf16[640,240]{1,0:T(8,128)(2,1)S(1)}, u32[]{:S(2)}, u32[]{:S(2)}) collective-permute-start(bf16[640,240]{1,0:T(8,128)(2,1)S(1)} %collective-permute-done.2), channel_id=1, source_target_pairs={{0,64},{64,128},{128,192},{192,256},{256,320},{320,384},{384,448},... | collective-permute-start | bytes 921608 | tf_op jit(solution)/shard_map/ppermute | solution.py:107
  54.5 0.8 bitcast_dynamic-update-slice_fusion.10
  55.3 0.8 bitcast_dynamic-update-slice_fusion.9
  56.1 2.0 %collective-permute-done.3 = bf16[640,240]{1,0:T(8,128)(2,1)S(1)} collective-permute-done((bf16[640,240]{1,0:T(8,128)(2,1)S(1)}, bf16[640,240]{1,0:T(8,128)(2,1)S(1)}, u32[]{:S(2)}, u32[]{:S(2)}) %collective-permute-start.3) | collective-permute-done | bytes 307232 | tf_op jit(solution)/shard_map/ppermute | solution.py:105
  58.1 5.6 %collective-permute-start.5 = (bf16[640,240]{1,0:T(8,128)(2,1)S(1)}, bf16[640,240]{1,0:T(8,128)(2,1)S(1)}, u32[]{:S(2)}, u32[]{:S(2)}) collective-permute-start(bf16[640,240]{1,0:T(8,128)(2,1)S(1)} %collective-permute-done.3), channel_id=1, source_target_pairs={{0,704},{64,0},{128,64},{192,128},{256,192},{320,256},{384,320},{4... | collective-permute-start | bytes 921608 | tf_op jit(solution)/shard_map/ppermute | solution.py:105
  63.7 1.9 %collective-permute-start.6 = (bf16[640,240]{1,0:T(8,128)(2,1)S(1)}, bf16[640,240]{1,0:T(8,128)(2,1)S(1)}, u32[]{:S(2)}, u32[]{:S(2)}) collective-permute-start(bf16[640,240]{1,0:T(8,128)(2,1)S(1)} %collective-permute-done.4), channel_id=1, source_target_pairs={{0,64},{64,128},{128,192},{192,256},{256,320},{320,384},{384,448},... | collective-permute-start | bytes 921608 | tf_op jit(solution)/shard_map/ppermute | solution.py:107
  65.6 0.8 bitcast_dynamic-update-slice_fusion.8
  66.4 0.8 bitcast_dynamic-update-slice_fusion.7
  67.1 1.1 collective-permute-done.5
  68.2 5.6 %collective-permute-start.7 = (bf16[640,240]{1,0:T(8,128)(2,1)S(1)}, bf16[640,240]{1,0:T(8,128)(2,1)S(1)}, u32[]{:S(2)}, u32[]{:S(2)}) collective-permute-start(bf16[640,240]{1,0:T(8,128)(2,1)S(1)} %collective-permute-done.5), channel_id=1, source_target_pairs={{0,704},{64,0},{128,64},{192,128},{256,192},{320,256},{384,320},{4... | collective-permute-start | bytes 921608 | tf_op jit(solution)/shard_map/ppermute | solution.py:105
  73.8 0.0 collective-permute-done.6
  73.9 1.9 %collective-permute-start.8 = (bf16[640,240]{1,0:T(8,128)(2,1)S(1)}, bf16[640,240]{1,0:T(8,128)(2,1)S(1)}, u32[]{:S(2)}, u32[]{:S(2)}) collective-permute-start(bf16[640,240]{1,0:T(8,128)(2,1)S(1)} %collective-permute-done.6), channel_id=1, source_target_pairs={{0,64},{64,128},{128,192},{192,256},{256,320},{320,384},{384,448},... | collective-permute-start | bytes 921608 | tf_op jit(solution)/shard_map/ppermute | solution.py:107
  75.8 0.8 bitcast_dynamic-update-slice_fusion.6
  76.5 0.8 bitcast_dynamic-update-slice_fusion.5
  77.3 1.1 collective-permute-done.7
  78.4 5.6 %collective-permute-start.9 = (bf16[640,240]{1,0:T(8,128)(2,1)S(1)}, bf16[640,240]{1,0:T(8,128)(2,1)S(1)}, u32[]{:S(2)}, u32[]{:S(2)}) collective-permute-start(bf16[640,240]{1,0:T(8,128)(2,1)S(1)} %collective-permute-done.7), channel_id=1, source_target_pairs={{0,704},{64,0},{128,64},{192,128},{256,192},{320,256},{384,320},{4... | collective-permute-start | bytes 921608 | tf_op jit(solution)/shard_map/ppermute | solution.py:105
  84.0 1.9 %collective-permute-start.10 = (bf16[640,240]{1,0:T(8,128)(2,1)S(1)}, bf16[640,240]{1,0:T(8,128)(2,1)S(1)}, u32[]{:S(2)}, u32[]{:S(2)}) collective-permute-start(bf16[640,240]{1,0:T(8,128)(2,1)S(1)} %collective-permute-done.8), channel_id=1, source_target_pairs={{0,64},{64,128},{128,192},{192,256},{256,320},{320,384},{384,448},... | collective-permute-start | bytes 921608 | tf_op jit(solution)/shard_map/ppermute | solution.py:107
  85.9 0.8 bitcast_dynamic-update-slice_fusion.4
  86.7 0.7 bitcast_dynamic-update-slice_fusion.3
  87.5 7.3 %collective-permute-done.10 = bf16[640,240]{1,0:T(8,128)(2,1)S(1)} collective-permute-done((bf16[640,240]{1,0:T(8,128)(2,1)S(1)}, bf16[640,240]{1,0:T(8,128)(2,1)S(1)}, u32[]{:S(2)}, u32[]{:S(2)}) %collective-permute-start.10) | collective-permute-done | bytes 307232 | tf_op jit(solution)/shard_map/ppermute | solution.py:107
  94.7 1.9 %collective-permute-start.11 = (bf16[640,240]{1,0:T(8,128)(2,1)S(1)}, bf16[640,240]{1,0:T(8,128)(2,1)S(1)}, u32[]{:S(2)}, u32[]{:S(2)}) collective-permute-start(bf16[640,240]{1,0:T(8,128)(2,1)S(1)} %collective-permute-done.10), channel_id=1, source_target_pairs={{0,64},{64,128},{128,192},{192,256},{256,320},{320,384},{384,448},... | collective-permute-start | bytes 921608 | tf_op jit(solution)/shard_map/ppermute | solution.py:107
  96.6 0.7 bitcast_dynamic-update-slice_fusion.2
  97.4 0.7 bitcast_dynamic-update-slice_fusion.1
  98.1 6.8 %collective-permute-done.11 = bf16[640,240]{1,0:T(8,128)(2,1)S(1)} collective-permute-done((bf16[640,240]{1,0:T(8,128)(2,1)S(1)}, bf16[640,240]{1,0:T(8,128)(2,1)S(1)}, u32[]{:S(2)}, u32[]{:S(2)}) %collective-permute-start.11) | collective-permute-done | bytes 307232 | tf_op jit(solution)/shard_map/ppermute | solution.py:107
  104.9 0.8 bitcast_dynamic-update-slice_fusion
  105.6 5.9 %shard_map.41 = (bf16[320,240]{1,0:T(8,128)(2,1)}, f32[2]{0:T(128)}) custom-call(s32[3]{0:T(128)} %pad_add_fusion.place_ref, bf16[32,320,240]{2,1,0:T(8,128)(2,1)} %bitcast.29, bf16[7680,240]{1,0:T(8,128)(2,1)} %bitcast.16.right_ref, s32[320,240]{1,0:T(8,128)} %fusion.1.keep_ref), custom_call_target="tpu_custom_call" | custom-call | flops 1179648000 | bytes 9062400 | tf_op jit(solution)/shard_map/pallas_call | solution.py:70
  111.6 2.6 %psum.35 = f32[2]{0:T(128)S(1)} all-reduce(f32[2]{0:T(128)} %get-tuple-element.5), channel_id=1, replica_groups=mesh['row_0'=12,'row_1'=2,'col_0'=4,'col_1'=4,'col_2'=2] {'col_2'}, use_global_device_ids=true, to_apply=%region_1.2 | all-reduce | flops 2 | bytes 16 | tf_op jit(solution)/shard_map/psum | solution.py:128
  114.2 16.0 %psum.36 = f32[2]{0:T(128)S(1)} all-reduce(f32[2]{0:T(128)S(1)} %psum.35), channel_id=1, replica_groups=mesh['row_0'=12,'row_1'=2,'col_0'=4,'col_1'=4,'col_2'=2] {'col_1'}, use_global_device_ids=true, to_apply=%region_2.3 | all-reduce | flops 2 | bytes 16 | tf_op jit(solution)/shard_map/psum | solution.py:128
  130.2 10.5 %psum.37 = f32[2]{0:T(128)S(1)} all-reduce(f32[2]{0:T(128)S(1)} %psum.36), channel_id=1, replica_groups=mesh['row_0'=12,'row_1'=2,'col_0'=4,'col_1'=4,'col_2'=2] {'col_0'}, use_global_device_ids=true, to_apply=%region_3.4 | all-reduce | flops 2 | bytes 16 | tf_op jit(solution)/shard_map/psum | solution.py:128
  140.7 8.8 %psum.38 = f32[2]{0:T(128)S(1)} all-reduce(f32[2]{0:T(128)S(1)} %psum.37), channel_id=1, replica_groups=mesh['row_0'=12,'row_1'=2,'col_0'=4,'col_1'=4,'col_2'=2] {'row_1'}, use_global_device_ids=true, to_apply=%region_4.5 | all-reduce | flops 2 | bytes 16 | tf_op jit(solution)/shard_map/psum | solution.py:128
  149.5 21.1 %psum.39 = f32[2]{0:T(128)} all-reduce(f32[2]{0:T(128)S(1)} %psum.38), channel_id=1, replica_groups=mesh['row_0'=12,'row_1'=2,'col_0'=4,'col_1'=4,'col_2'=2] {'row_0'}, use_global_device_ids=true, to_apply=%region_5.6 | all-reduce | flops 2 | bytes 16 | tf_op jit(solution)/shard_map/psum | solution.py:128
  (8 shorter events, 0.1 us)
Async XLA Ops:
  7.2 98.5 %all-gather.3.cloned.1.call-start = ((), (), s32[]{:S(2)}) async-start(), calls=%async_computation | async-start | bytes 5406720 | tf_op jit(solution)/shard_map/all_gather | solution.py:120
  10.1 14.8 %collective-permute-start = (bf16[320,240]{1,0:T(8,128)(2,1)}, bf16[320,240]{1,0:T(8,128)(2,1)S(1)}, u32[]{:S(2)}, u32[]{:S(2)}) collective-permute-start(bf16[320,240]{1,0:T(8,128)(2,1)} %fusion.2), channel_id=1, source_target_pairs={{0,32},{32,0},{1,33},{33,1},{2,34},{34,2},{3,35},{35,3},{4,36},{36... | collective-permute-start | bytes 460808 | tf_op jit(solution)/shard_map/ppermute | solution.py:90
  26.0 21.0 %collective-permute-start.1 = (bf16[640,240]{1,0:T(8,128)(2,1)S(1)}, bf16[640,240]{1,0:T(8,128)(2,1)S(1)}, u32[]{:S(2)}, u32[]{:S(2)}) collective-permute-start(bf16[640,240]{1,0:T(8,128)(2,1)S(1)} %maximum_select_fusion.1), channel_id=1, source_target_pairs={{0,704},{64,0},{128,64},{192,128},{256,192},{320,256},{384,320},{4... | collective-permute-start | bytes 921608 | tf_op jit(solution)/shard_map/ppermute | solution.py:105
  40.6 12.0 %collective-permute-start.2 = (bf16[640,240]{1,0:T(8,128)(2,1)S(1)}, bf16[640,240]{1,0:T(8,128)(2,1)S(1)}, u32[]{:S(2)}, u32[]{:S(2)}) collective-permute-start(bf16[640,240]{1,0:T(8,128)(2,1)S(1)} %maximum_select_fusion.1), channel_id=1, source_target_pairs={{0,64},{64,128},{128,192},{192,256},{256,320},{320,384},{384,448},... | collective-permute-start | bytes 921608 | tf_op jit(solution)/shard_map/ppermute | solution.py:107
  47.0 11.1 %collective-permute-start.3 = (bf16[640,240]{1,0:T(8,128)(2,1)S(1)}, bf16[640,240]{1,0:T(8,128)(2,1)S(1)}, u32[]{:S(2)}, u32[]{:S(2)}) collective-permute-start(bf16[640,240]{1,0:T(8,128)(2,1)S(1)} %collective-permute-done.1), channel_id=1, source_target_pairs={{0,704},{64,0},{128,64},{192,128},{256,192},{320,256},{384,320},{4... | collective-permute-start | bytes 921608 | tf_op jit(solution)/shard_map/ppermute | solution.py:105
  52.6 11.1 %collective-permute-start.4 = (bf16[640,240]{1,0:T(8,128)(2,1)S(1)}, bf16[640,240]{1,0:T(8,128)(2,1)S(1)}, u32[]{:S(2)}, u32[]{:S(2)}) collective-permute-start(bf16[640,240]{1,0:T(8,128)(2,1)S(1)} %collective-permute-done.2), channel_id=1, source_target_pairs={{0,64},{64,128},{128,192},{192,256},{256,320},{320,384},{384,448},... | collective-permute-start | bytes 921608 | tf_op jit(solution)/shard_map/ppermute | solution.py:107
  58.1 10.2 %collective-permute-start.5 = (bf16[640,240]{1,0:T(8,128)(2,1)S(1)}, bf16[640,240]{1,0:T(8,128)(2,1)S(1)}, u32[]{:S(2)}, u32[]{:S(2)}) collective-permute-start(bf16[640,240]{1,0:T(8,128)(2,1)S(1)} %collective-permute-done.3), channel_id=1, source_target_pairs={{0,704},{64,0},{128,64},{192,128},{256,192},{320,256},{384,320},{4... | collective-permute-start | bytes 921608 | tf_op jit(solution)/shard_map/ppermute | solution.py:105
  63.7 10.2 %collective-permute-start.6 = (bf16[640,240]{1,0:T(8,128)(2,1)S(1)}, bf16[640,240]{1,0:T(8,128)(2,1)S(1)}, u32[]{:S(2)}, u32[]{:S(2)}) collective-permute-start(bf16[640,240]{1,0:T(8,128)(2,1)S(1)} %collective-permute-done.4), channel_id=1, source_target_pairs={{0,64},{64,128},{128,192},{192,256},{256,320},{320,384},{384,448},... | collective-permute-start | bytes 921608 | tf_op jit(solution)/shard_map/ppermute | solution.py:107
  68.2 10.2 %collective-permute-start.7 = (bf16[640,240]{1,0:T(8,128)(2,1)S(1)}, bf16[640,240]{1,0:T(8,128)(2,1)S(1)}, u32[]{:S(2)}, u32[]{:S(2)}) collective-permute-start(bf16[640,240]{1,0:T(8,128)(2,1)S(1)} %collective-permute-done.5), channel_id=1, source_target_pairs={{0,704},{64,0},{128,64},{192,128},{256,192},{320,256},{384,320},{4... | collective-permute-start | bytes 921608 | tf_op jit(solution)/shard_map/ppermute | solution.py:105
  73.9 10.2 %collective-permute-start.8 = (bf16[640,240]{1,0:T(8,128)(2,1)S(1)}, bf16[640,240]{1,0:T(8,128)(2,1)S(1)}, u32[]{:S(2)}, u32[]{:S(2)}) collective-permute-start(bf16[640,240]{1,0:T(8,128)(2,1)S(1)} %collective-permute-done.6), channel_id=1, source_target_pairs={{0,64},{64,128},{128,192},{192,256},{256,320},{320,384},{384,448},... | collective-permute-start | bytes 921608 | tf_op jit(solution)/shard_map/ppermute | solution.py:107
  78.4 18.2 %collective-permute-start.9 = (bf16[640,240]{1,0:T(8,128)(2,1)S(1)}, bf16[640,240]{1,0:T(8,128)(2,1)S(1)}, u32[]{:S(2)}, u32[]{:S(2)}) collective-permute-start(bf16[640,240]{1,0:T(8,128)(2,1)S(1)} %collective-permute-done.7), channel_id=1, source_target_pairs={{0,704},{64,0},{128,64},{192,128},{256,192},{320,256},{384,320},{4... | collective-permute-start | bytes 921608 | tf_op jit(solution)/shard_map/ppermute | solution.py:105
  84.0 10.7 %collective-permute-start.10 = (bf16[640,240]{1,0:T(8,128)(2,1)S(1)}, bf16[640,240]{1,0:T(8,128)(2,1)S(1)}, u32[]{:S(2)}, u32[]{:S(2)}) collective-permute-start(bf16[640,240]{1,0:T(8,128)(2,1)S(1)} %collective-permute-done.8), channel_id=1, source_target_pairs={{0,64},{64,128},{128,192},{192,256},{256,320},{320,384},{384,448},... | collective-permute-start | bytes 921608 | tf_op jit(solution)/shard_map/ppermute | solution.py:107
  94.7 10.2 %collective-permute-start.11 = (bf16[640,240]{1,0:T(8,128)(2,1)S(1)}, bf16[640,240]{1,0:T(8,128)(2,1)S(1)}, u32[]{:S(2)}, u32[]{:S(2)}) collective-permute-start(bf16[640,240]{1,0:T(8,128)(2,1)S(1)} %collective-permute-done.10), channel_id=1, source_target_pairs={{0,64},{64,128},{128,192},{192,256},{256,320},{320,384},{384,448},... | collective-permute-start | bytes 921608 | tf_op jit(solution)/shard_map/ppermute | solution.py:107
Sparse Core Ops, SparseCore 0:
  11.0 75.3 all-gather.2
